TPU v7x, 32 devices: a whole 2x2x4 slice. The times are simulated.
32 devices in a mesh: row: 4 (over x, core), col: 8 (over z, y).
Axes of the slice: x: 2, y: 2, z: 4, core: 2. Of those that a mesh axis runs over, the one named last changes fastest.
Arguments:
- tiles: bfloat16 [160, 1024, 1024], P(('row', 'col')), may hold values from 5 to 500
- tile_list: int32 [160], P(('row', 'col')), may hold values from 0 to 7, as said below
- tile_count: int32 [32], P(('row', 'col')), may hold values from 1 to 5, as said below
- w_rows: float32 [8192, 256], P(('row', 'col')), may hold values from 0.01 to 3, as said below
- h_cols: float32 [256, 32768], P(None, ('row', 'col')), may hold values from 0.05 to 1
Outputs:
- h_next: float32 [256, 32768], P(None, ('row', 'col'))
Inputs may be any that keep to these rules, and one draw needn't show every extreme that they name: `tile_list`: within the first tile_count[b] slots of column block b the row blocks are distinct; slots past the count hold row blocks that are ignored. `tile_count`: some column block has all 5 slots live in every draw. `w_rows`: entries are positive.
All inputs are finite; a program needn't handle non-finite values.
Results may differ from a plain program's by a relative error of at most 0.0003.
Values may be sent and summed in bfloat16 or wider, within the bound.
No kernel may reach another device: no remote copies, remote signals or barrier semaphores. Data moves between devices by JAX's collectives and lax.ppermute only.
A program may use at most 64 MiB of HBM per device.

v0:
```python
import jax
import jax.numpy as jnp
from jax import lax
from jax.sharding import PartitionSpec as P

TILE = 1024


contract_rows = (((0,), (0,)), ((), ()))


def tile_pass(numerator, w_source, row_base, row_span, squares, row_blocks, live_count):

    def one_slot(slot_index, running):
        row_start = row_blocks[slot_index] * TILE
        inside = (row_start >= row_base) & (row_start < row_base + row_span)

        def add_block(total_now):
            w_block = lax.dynamic_slice_in_dim(w_source, row_start - row_base, TILE, 0)
            square = lax.dynamic_index_in_dim(squares, slot_index, 0, keepdims=False)
            return total_now + lax.dot_general(
                w_block, square, contract_rows, preferred_element_type=jnp.float32
            )

        return lax.cond(inside, add_block, lambda total_now: total_now, running)

    return lax.fori_loop(0, live_count, one_slot, numerator)


def shards(tiles, tile_list, tile_count, w_rows, h_cols):
    rank_size = h_cols.shape[0]
    live_count = tile_count[0]
    w_half = w_rows.astype(jnp.bfloat16)
    numerator = jnp.zeros((rank_size, h_cols.shape[1]), jnp.float32)
    borrowed_init = jnp.zeros((rank_size, h_cols.shape[1]), jnp.float32)
    w_full = lax.all_gather(w_half, ("row", "col"), axis=0, tiled=True)
    partial_sum = numerator
    borrowed_sum = borrowed_init
    partial_sum = tile_pass(partial_sum, w_full, 0, w_full.shape[0], tiles, tile_list, live_count)
    gram_now = lax.dot_general(w_full, w_full, contract_rows, preferred_element_type=jnp.float32)
    numerator, borrowed_sum, gram_total = (partial_sum, borrowed_sum, gram_now)
    denominator = jnp.dot(
        gram_total, h_cols, precision=lax.Precision.HIGHEST, preferred_element_type=jnp.float32
    )
    return h_cols * numerator / denominator


def solution(mesh):
    placed = (
        P(("row", "col"), None, None),
        P(("row", "col")),
        P(("row", "col")),
        P(("row", "col"), None),
        P(None, ("row", "col")),
    )
    return jax.shard_map(
        shards, mesh=mesh, in_specs=placed, out_specs=P(None, ("row", "col")), check_vma=False
    )
```

profile of v0, /device:TPU:23, one launch (start us, length us, event | category | flops | bytes accessed | tf_op | source)
XLA Modules:
  0.0 112.5 jit_solution(9190705215986856970)
XLA Ops:
  6.5 0.0 all-gather.2.cloned.1.call-start
  6.5 1.6 %convert_element_type.6 = bf16[256,256]{1,0:T(8,128)(2,1)} convert(f32[256,256]{1,0:T(8,128)} %param.12) | non-fusion elementwise | flops 65536 | bytes 393216 | tf_op jit(solution)/shard_map/convert_element_type | solution.py:33
  8.2 0.0 all-gather.2.cloned.1.call-update
  8.2 64.1 %all-gather.2.cloned.1.call-done = bf16[8192,256]{1,0:T(8,128)(2,1)} async-done(((bf16[256,256]{1,0:T(8,128)(2,1)}), bf16[8192,256]{1,0:T(8,128)(2,1)}) %all-gather.2.cloned.1.call-update) | async-done | bytes 4194320 | tf_op jit(solution)/shard_map/all_gather | solution.py:36
  72.3 0.1 broadcast_in_dim.3
  72.4 26.3 %while.13 = (s32[]{:T(128)}, f32[256,1024]{1,0:T(8,128)S(1)}, s32[]{:T(128)}, s32[5]{0:T(128)}, bf16[8192,256]{1,0:T(8,128)(2,1)}, /*index=5*/bf16[5,1024,1024]{...) while((s32[]{:T(128)}, f32[256,1024]{1,0:T(8,128)S(1)}, s32[]{:T(128)}, ...), condition=%wide.region_3.4_spmd, body=%wide.region_0.3_spmd.sunk | while | flops 537133056 | bytes 4718909 | solution.py:27
  73.0 1.2 %dynamic_slice.19 = s32[1]{0:T(128)} dynamic-slice(s32[5]{0:T(128)} %get-tuple-element.133, s32[]{:T(128)S(6)} %select_n.11), dynamic_slice_sizes={1} | dynamic-slice | bytes 12 | tf_op jit(solution)/shard_map/while/body/dynamic_slice | solution.py:15
  74.9 2.6 %conditional.2 = (f32[256,1024]{1,0:T(8,128)S(1)}) conditional(s32[]{:T(128)} %convert_element_type.8, f32[256,1024]{1,0:T(8,128)S(1)} %get-tuple-element.120, (s32[]{:T(128)}, bf16[8192,256]{1,0:T(8,128)(2,1)}, s32[]{:T(128)}, bf16[5,1024,1024]{2,1,0:T(8,128)(2,1)}, f32[256,1024]{1,0:T(8,128)S(1)}) %tuple.25), branch_computations={%region_1.0_spmd, %region_2.2_spmd} | conditional | flops 537133056 | bytes 4718676 | solution.py:25
  75.0 2.5 %fusion.3 = f32[256,1024]{1,0:T(8,128)S(1)} fusion(f32[256,1024]{1,0:T(8,128)S(1)} %get-tuple-element.43, bf16[5,1024,1024]{2,1,0:T(8,128)(2,1)} %get-tuple-element.46, s32[]{:T(128)S(6)} %select_n.8, bf16[8192,256]{1,0:T(8,128)(2,1)} %get-tuple-element.44, s32[]{:T(128)S(6)} %select_n.7), kind=kOutput, calls=%fused_computation.3 | convolution fusion | flops 537133056 | bytes 4718600 | tf_op jit(solution)/shard_map/while/body/cond/branch_1_fun/dot_general | solution.py:21
  78.2 1.2 %dynamic_slice.19 = s32[1]{0:T(128)} dynamic-slice(s32[5]{0:T(128)} %get-tuple-element.133, s32[]{:T(128)S(6)} %select_n.11), dynamic_slice_sizes={1} | dynamic-slice | bytes 12 | tf_op jit(solution)/shard_map/while/body/dynamic_slice | solution.py:15
  80.1 2.6 %conditional.2 = (f32[256,1024]{1,0:T(8,128)S(1)}) conditional(s32[]{:T(128)} %convert_element_type.8, f32[256,1024]{1,0:T(8,128)S(1)} %get-tuple-element.120, (s32[]{:T(128)}, bf16[8192,256]{1,0:T(8,128)(2,1)}, s32[]{:T(128)}, bf16[5,1024,1024]{2,1,0:T(8,128)(2,1)}, f32[256,1024]{1,0:T(8,128)S(1)}) %tuple.25), branch_computations={%region_1.0_spmd, %region_2.2_spmd} | conditional | flops 537133056 | bytes 4718676 | solution.py:25
  80.1 2.5 %fusion.3 = f32[256,1024]{1,0:T(8,128)S(1)} fusion(f32[256,1024]{1,0:T(8,128)S(1)} %get-tuple-element.43, bf16[5,1024,1024]{2,1,0:T(8,128)(2,1)} %get-tuple-element.46, s32[]{:T(128)S(6)} %select_n.8, bf16[8192,256]{1,0:T(8,128)(2,1)} %get-tuple-element.44, s32[]{:T(128)S(6)} %select_n.7), kind=kOutput, calls=%fused_computation.3 | convolution fusion | flops 537133056 | bytes 4718600 | tf_op jit(solution)/shard_map/while/body/cond/branch_1_fun/dot_general | solution.py:21
  83.3 1.2 %dynamic_slice.19 = s32[1]{0:T(128)} dynamic-slice(s32[5]{0:T(128)} %get-tuple-element.133, s32[]{:T(128)S(6)} %select_n.11), dynamic_slice_sizes={1} | dynamic-slice | bytes 12 | tf_op jit(solution)/shard_map/while/body/dynamic_slice | solution.py:15
  85.2 2.6 %conditional.2 = (f32[256,1024]{1,0:T(8,128)S(1)}) conditional(s32[]{:T(128)} %convert_element_type.8, f32[256,1024]{1,0:T(8,128)S(1)} %get-tuple-element.120, (s32[]{:T(128)}, bf16[8192,256]{1,0:T(8,128)(2,1)}, s32[]{:T(128)}, bf16[5,1024,1024]{2,1,0:T(8,128)(2,1)}, f32[256,1024]{1,0:T(8,128)S(1)}) %tuple.25), branch_computations={%region_1.0_spmd, %region_2.2_spmd} | conditional | flops 537133056 | bytes 4718676 | solution.py:25
  85.2 2.5 %fusion.3 = f32[256,1024]{1,0:T(8,128)S(1)} fusion(f32[256,1024]{1,0:T(8,128)S(1)} %get-tuple-element.43, bf16[5,1024,1024]{2,1,0:T(8,128)(2,1)} %get-tuple-element.46, s32[]{:T(128)S(6)} %select_n.8, bf16[8192,256]{1,0:T(8,128)(2,1)} %get-tuple-element.44, s32[]{:T(128)S(6)} %select_n.7), kind=kOutput, calls=%fused_computation.3 | convolution fusion | flops 537133056 | bytes 4718600 | tf_op jit(solution)/shard_map/while/body/cond/branch_1_fun/dot_general | solution.py:21
  88.4 1.2 %dynamic_slice.19 = s32[1]{0:T(128)} dynamic-slice(s32[5]{0:T(128)} %get-tuple-element.133, s32[]{:T(128)S(6)} %select_n.11), dynamic_slice_sizes={1} | dynamic-slice | bytes 12 | tf_op jit(solution)/shard_map/while/body/dynamic_slice | solution.py:15
  90.3 2.6 %conditional.2 = (f32[256,1024]{1,0:T(8,128)S(1)}) conditional(s32[]{:T(128)} %convert_element_type.8, f32[256,1024]{1,0:T(8,128)S(1)} %get-tuple-element.120, (s32[]{:T(128)}, bf16[8192,256]{1,0:T(8,128)(2,1)}, s32[]{:T(128)}, bf16[5,1024,1024]{2,1,0:T(8,128)(2,1)}, f32[256,1024]{1,0:T(8,128)S(1)}) %tuple.25), branch_computations={%region_1.0_spmd, %region_2.2_spmd} | conditional | flops 537133056 | bytes 4718676 | solution.py:25
  90.4 2.5 %fusion.3 = f32[256,1024]{1,0:T(8,128)S(1)} fusion(f32[256,1024]{1,0:T(8,128)S(1)} %get-tuple-element.43, bf16[5,1024,1024]{2,1,0:T(8,128)(2,1)} %get-tuple-element.46, s32[]{:T(128)S(6)} %select_n.8, bf16[8192,256]{1,0:T(8,128)(2,1)} %get-tuple-element.44, s32[]{:T(128)S(6)} %select_n.7), kind=kOutput, calls=%fused_computation.3 | convolution fusion | flops 537133056 | bytes 4718600 | tf_op jit(solution)/shard_map/while/body/cond/branch_1_fun/dot_general | solution.py:21
  93.6 1.2 %dynamic_slice.19 = s32[1]{0:T(128)} dynamic-slice(s32[5]{0:T(128)} %get-tuple-element.133, s32[]{:T(128)S(6)} %select_n.11), dynamic_slice_sizes={1} | dynamic-slice | bytes 12 | tf_op jit(solution)/shard_map/while/body/dynamic_slice | solution.py:15
  95.5 2.6 %conditional.2 = (f32[256,1024]{1,0:T(8,128)S(1)}) conditional(s32[]{:T(128)} %convert_element_type.8, f32[256,1024]{1,0:T(8,128)S(1)} %get-tuple-element.120, (s32[]{:T(128)}, bf16[8192,256]{1,0:T(8,128)(2,1)}, s32[]{:T(128)}, bf16[5,1024,1024]{2,1,0:T(8,128)(2,1)}, f32[256,1024]{1,0:T(8,128)S(1)}) %tuple.25), branch_computations={%region_1.0_spmd, %region_2.2_spmd} | conditional | flops 537133056 | bytes 4718676 | solution.py:25
  95.5 2.5 %fusion.3 = f32[256,1024]{1,0:T(8,128)S(1)} fusion(f32[256,1024]{1,0:T(8,128)S(1)} %get-tuple-element.43, bf16[5,1024,1024]{2,1,0:T(8,128)(2,1)} %get-tuple-element.46, s32[]{:T(128)S(6)} %select_n.8, bf16[8192,256]{1,0:T(8,128)(2,1)} %get-tuple-element.44, s32[]{:T(128)S(6)} %select_n.7), kind=kOutput, calls=%fused_computation.3 | convolution fusion | flops 537133056 | bytes 4718600 | tf_op jit(solution)/shard_map/while/body/cond/branch_1_fun/dot_general | solution.py:21
  98.7 0.0 copy-start
  98.7 4.8 %fusion.8 = f32[256,256]{1,0:T(8,128)S(1)} fusion(bf16[8192,256]{1,0:T(8,128)(2,1)} %get-tuple-element.144), kind=kOutput, calls=%fused_computation.7 | convolution fusion | flops 1073741824 | bytes 4456448 | tf_op jit(solution)/shard_map/dot_general | solution.py:40
  103.5 0.0 copy-done
  103.6 2.1 %convolution_divide_fusion = f32[256,1024]{1,0:T(8,128)} fusion(f32[256,256]{1,0:T(8,128)S(1)} %fusion.8, f32[256,1024]{1,0:T(8,128)S(1)} %copy-done, f32[256,1024]{1,0:T(8,128)S(1)} %get-tuple-element.57), kind=kOutput, calls=%fused_computation.6 | convolution fusion | flops 805830656 | bytes 3407872 | tf_op jit(solution)/shard_map/dot_general | solution.py:42
Async XLA Ops:
  6.5 65.7 %all-gather.2.cloned.1.call-start = ((), (), s32[]{:S(2)}) async-start(), calls=%async_computation | async-start | bytes 4325376 | tf_op jit(solution)/shard_map/all_gather | solution.py:36
  98.7 4.8 %copy-start = (f32[256,1024]{1,0:T(8,128)S(1)}, f32[256,1024]{1,0:T(8,128)}, u32[]{:S(2)}) copy-start(f32[256,1024]{1,0:T(8,128)} %param.13) | copy-start | bytes 3145732
Sparse Core Ops, SparseCore 0:
  10.4 61.7 all-gather.1
where the time goes:
time: 115 us; the launch traced here: 113 us
  waiting for transfers between devices  64.1 us (56%)
  matrix products  19.6 us (17%)
  between operations  13.4 us (12%)
  loops' own time  7.46 us (6%)
  local copies, waits for them, and re-layouts  6.32 us (5%)
  other arithmetic  1.62 us (1%)
    all_gather x1, waiting for transfers between devices, shards(): w_full = lax.all_gather(w_half, ('row', 'col'), axis=0, tiled=True)  64.1 us
    dot_general x5, matrix products, add_block(): lax.dot_general(w_block, square, contract_rows, preferred_element_type=jn...  12.7 us
    another operation x1, loops' own time, tile_pass(): return lax.fori_loop(0, live_count, one_slot, numerator)  7.32 us
    dynamic_slice x5, local copies, waits for them, and re-layouts, one_slot(): row_start = row_blocks[slot_index] * TILE  6.21 us
    dot_general x1, matrix products, shards(): lax.dot_general(w_full, w_full, contract_rows, preferred_element_type=jnp...  4.82 us
  transfers between devices with their start and end apart: 1, of which 1 were waited for; matrix products, arithmetic and copies ran while one was open for 0% of the time, Pallas kernels for 0%

commit v1 on v0

v1 whole, which is shorter than its diff:
```python
import jax
import jax.numpy as jnp
from jax import lax
from jax.sharding import PartitionSpec as P

contract_rows = (((0,), (0,)), ((), ()))


def shards(tiles, tile_list, tile_count, w_rows, h_cols):
    slots, tile = tiles.shape[0], tiles.shape[1]
    rank_size = h_cols.shape[0]
    w_half = w_rows.astype(jnp.bfloat16)
    w_full = lax.all_gather(w_half, ("row", "col"), axis=0, tiled=True)
    gram = lax.dot_general(w_full, w_full, contract_rows, preferred_element_type=jnp.float32)
    blocks = w_full.reshape(-1, tile, rank_size)
    live = jnp.arange(slots, dtype=jnp.int32) < tile_count[0]
    picked = jnp.take(blocks, jnp.clip(tile_list, 0, blocks.shape[0] - 1), axis=0)
    picked = jnp.where(live[:, None, None], picked, jnp.zeros_like(picked))
    numerator = lax.dot_general(
        picked.reshape(slots * tile, rank_size),
        tiles.reshape(slots * tile, tiles.shape[2]),
        contract_rows,
        preferred_element_type=jnp.float32,
    )
    denominator = jnp.dot(
        gram, h_cols, precision=lax.Precision.HIGHEST, preferred_element_type=jnp.float32
    )
    return h_cols * numerator / denominator


def solution(mesh):
    placed = (
        P(("row", "col"), None, None),
        P(("row", "col")),
        P(("row", "col")),
        P(("row", "col"), None),
        P(None, ("row", "col")),
    )
    return jax.shard_map(
        shards, mesh=mesh, in_specs=placed, out_specs=P(None, ("row", "col")), check_vma=False
    )
```

time: 115 us -> 95.9 us (0.83)
  the two profiles are of different devices: /device:TPU:23 before, /device:TPU:0 now
where the time goes in v1:
time: 95.9 us; the launch traced here: 95.8 us
  waiting for transfers between devices  65.8 us (69%)
  between operations  14.1 us (15%)
  matrix products  10.7 us (11%)
  local copies, waits for them, and re-layouts  2.91 us (3%)
  other arithmetic  2.29 us (2%)
    all_gather x1, waiting for transfers between devices, shards(): w_full = lax.all_gather(w_half, ('row', 'col'), axis=0, tiled=True)  65.7 us
    dot_general x1, matrix products, shards(): lax.dot_general(picked.reshape(slots * tile, rank_size), tiles.reshape(sl...  7.38 us
    gather x1, local copies, waits for them, and re-layouts, shards(): jnp.take(blocks, jnp.clip(tile_list, 0, blocks.shape[0] - 1), axis=0)  2.9 us
    dot_general x1, matrix products, shards(): jnp.dot(gram, h_cols, precision=lax.Precision.HIGHEST, preferred_element_...  2.04 us
  transfers between devices with their start and end apart: 1, of which 1 were waited for; matrix products, arithmetic and copies ran while one was open for 1% of the time, Pallas kernels for 0%

profile of v1, /device:TPU:0, one launch (start us, length us, event | category | flops | bytes accessed | tf_op | source)
XLA Modules:
  0.0 95.8 jit_solution(9110875913328523421)
XLA Ops:
  6.5 0.0 all-gather.2.cloned.1.call-start
  6.5 1.6 %convert_element_type.3 = bf16[256,256]{1,0:T(8,128)(2,1)} convert(f32[256,256]{1,0:T(8,128)} %param.8) | non-fusion elementwise | flops 65536 | bytes 393216 | tf_op jit(solution)/shard_map/convert_element_type | solution.py:12
  8.2 0.0 all-gather.2.cloned.1.call-update
  8.8 0.7 compare_and_fusion
  9.5 65.7 %all-gather.2.cloned.1.call-done = bf16[8192,256]{1,0:T(8,128)(2,1)} async-done(((bf16[256,256]{1,0:T(8,128)(2,1)}), bf16[8192,256]{1,0:T(8,128)(2,1)}) %all-gather.2.cloned.1.call-update) | async-done | bytes 4194320 | tf_op jit(solution)/shard_map/all_gather | solution.py:13
  75.2 2.9 %gather_fusion = bf16[5,1024,256]{2,1,0:T(8,128)(2,1)S(1)} fusion(bf16[8,1024,256]{2,1,0:T(8,128)(2,1)} %bitcast.12, s32[1024]{0:T(1024)S(1)} %pad_clamp_fusion), kind=kCustom, calls=%fused_computation | custom fusion | bytes 5242900 | tf_op jit(solution)/shard_map/jit(_take)/gather | solution.py:17
  78.1 0.0 copy-start
  78.2 7.4 %fusion.8 = f32[256,1024]{1,0:T(8,128)S(1)} fusion(f32[256,1024]{1,0:T(8,128)} %param.9, bf16[5,1024,1024]{2,1,0:T(8,128)(2,1)} %param.5, bf16[5,1024,256]{2,1,0:T(8,128)(2,1)S(1)} %gather_fusion, pred[5]{0:T(512)(128)(4,1)S(1)} %get-tuple-element.5, pred[5]{0:T(512)(128)(4,1)S(1)} %get-tuple-element.7), kind=kOutput, calls=%fused_computation.7 | convolution fusion | flops 2687238144 | bytes 15204362 | tf_op jit(solution)/shard_map/dot_general | solution.py:19
  85.5 0.0 copy-done
  85.6 0.0 copy-start.1
  85.6 1.3 %fusion.15 = f32[256,256]{1,0:T(8,128)S(1)} fusion(bf16[8192,256]{1,0:T(8,128)(2,1)S(1)} %copy-done), kind=kOutput, calls=%fused_computation.17 | convolution fusion | flops 1073741824 | bytes 4456448 | tf_op jit(solution)/shard_map/dot_general | solution.py:14
  86.9 0.0 copy-done.1
  86.9 2.0 %convolution_divide_fusion = f32[256,1024]{1,0:T(8,128)} fusion(f32[256,1024]{1,0:T(8,128)S(1)} %fusion.8, f32[256,256]{1,0:T(8,128)S(1)} %fusion.15, f32[256,1024]{1,0:T(8,128)S(1)} %copy-done.1), kind=kOutput, calls=%fused_computation.8 | convolution fusion | flops 805568512 | bytes 3407872 | tf_op jit(solution)/shard_map/dot_general | solution.py:25
  (1 shorter events, 0.0 us)
Async XLA Ops:
  6.5 68.7 %all-gather.2.cloned.1.call-start = ((), (), s32[]{:S(2)}) async-start(), calls=%async_computation | async-start | bytes 4325376 | tf_op jit(solution)/shard_map/all_gather | solution.py:13
  78.1 7.4 %copy-start = (bf16[8192,256]{1,0:T(8,128)(2,1)S(1)}, bf16[8192,256]{1,0:T(8,128)(2,1)}, u32[]{:S(2)}) copy-start(bf16[8192,256]{1,0:T(8,128)(2,1)} %all-gather.2.cloned.1.call-done) | copy-start | bytes 12582916
  85.6 1.3 %copy-start.1 = (f32[256,1024]{1,0:T(8,128)S(1)}, f32[256,1024]{1,0:T(8,128)}, u32[]{:S(2)}) copy-start(f32[256,1024]{1,0:T(8,128)} %param.9) | copy-start | bytes 3145732
Sparse Core Ops, SparseCore 0:
  10.4 64.7 all-gather.1

commit v2 on v1

v2 whole, which is shorter than its diff:
```python
import jax
import jax.numpy as jnp
from jax import lax
from jax.sharding import PartitionSpec as P

contract_rows = (((0,), (0,)), ((), ()))
AXES = ("row", "col")


def doubling_order(n_row, n_col):
    col_bits = [1 << k for k in range(n_col.bit_length() - 1)][::-1]
    row_bits = [n_col << k for k in range(n_row.bit_length() - 1)][::-1]
    return col_bits + row_bits


def gather_rows(w_half, order, n):
    buf = w_half
    for mask in order:
        moved = lax.ppermute(buf, AXES, [(i, i ^ mask) for i in range(n)])
        buf = jnp.concatenate([buf, moved], axis=0)
    return buf


def slot_of(distance, order):
    pos = jnp.zeros_like(distance)
    for k, mask in enumerate(order):
        pos = pos + jnp.where((distance & mask) != 0, 1 << k, 0)
    return pos


def shards(tiles, tile_list, tile_count, w_rows, h_cols, n_row, n_col):
    slots, tile = tiles.shape[0], tiles.shape[1]
    rank_size = h_cols.shape[0]
    n = n_row * n_col
    share = w_rows.shape[0]
    w_half = w_rows.astype(jnp.bfloat16)
    order = doubling_order(n_row, n_col)
    buf = gather_rows(w_half, order, n)
    gram = lax.dot_general(buf, buf, contract_rows, preferred_element_type=jnp.float32)
    me = lax.axis_index("row") * n_col + lax.axis_index("col")
    per_block = tile // share
    blocks_total = n // per_block
    rows_of = jnp.clip(tile_list, 0, blocks_total - 1)
    owners = rows_of[:, None] * per_block + jnp.arange(per_block, dtype=jnp.int32)[None, :]
    where = slot_of(owners ^ me, order)
    pieces = buf.reshape(n, share, rank_size)
    picked = jnp.take(pieces, where.reshape(-1), axis=0).reshape(slots, tile, rank_size)
    live = jnp.arange(slots, dtype=jnp.int32) < tile_count[0]
    picked = jnp.where(live[:, None, None], picked, jnp.zeros_like(picked))
    numerator = lax.dot_general(
        picked.reshape(slots * tile, rank_size),
        tiles.reshape(slots * tile, tiles.shape[2]),
        contract_rows,
        preferred_element_type=jnp.float32,
    )
    denominator = jnp.dot(
        gram, h_cols, precision=lax.Precision.HIGHEST, preferred_element_type=jnp.float32
    )
    return h_cols * numerator / denominator


def solution(mesh):
    n_row, n_col = mesh.shape["row"], mesh.shape["col"]
    placed = (
        P(AXES, None, None),
        P(AXES),
        P(AXES),
        P(AXES, None),
        P(None, AXES),
    )

    def body(tiles, tile_list, tile_count, w_rows, h_cols):
        return shards(tiles, tile_list, tile_count, w_rows, h_cols, n_row, n_col)

    return jax.shard_map(
        body, mesh=mesh, in_specs=placed, out_specs=P(None, AXES), check_vma=False
    )
```

time: 95.9 us -> 82.7 us (0.86)
  the two profiles are of different devices: /device:TPU:0 before, /device:TPU:17 now
where the time goes in v2:
time: 82.7 us; the launch traced here: 82.4 us
  waiting for transfers between devices  44 us (53%)
  matrix products  14.9 us (18%)
  starting transfers between devices  10.5 us (13%)
  local copies, waits for them, and re-layouts  9.31 us (11%)
  other arithmetic  2.98 us (4%)
    ppermute x5, waiting for transfers between devices, gather_rows(): moved = lax.ppermute(buf, AXES, [(i, i ^ mask) for i in range(n)])  44 us
    ppermute x5, starting transfers between devices, gather_rows(): moved = lax.ppermute(buf, AXES, [(i, i ^ mask) for i in range(n)])  10.5 us
    dot_general x1, matrix products, shards(): lax.dot_general(picked.reshape(slots * tile, rank_size), tiles.reshape(sl...  7.86 us
    dot_general x1, matrix products, shards(): lax.dot_general(buf, buf, contract_rows, preferred_element_type=jnp.float32)  4.74 us
    unnamed x10, local copies, waits for them, and re-layouts  3.42 us
    concatenate x2, local copies, waits for them, and re-layouts, gather_rows(): buf = jnp.concatenate([buf, moved], axis=0)  2.9 us
    gather x1, local copies, waits for them, and re-layouts, shards(): jnp.take(pieces, where.reshape(-1), axis=0).reshape(slots, tile, rank_size)  2.9 us
    dot_general x1, matrix products, shards(): jnp.dot(gram, h_cols, precision=lax.Precision.HIGHEST, preferred_element_...  2.26 us
  transfers between devices with their start and end apart: 5, of which 5 were waited for; matrix products, arithmetic and copies ran while one was open for 4% of the time, Pallas kernels for 0%

profile of v2, /device:TPU:17, one launch (start us, length us, event | category | flops | bytes accessed | tf_op | source)
XLA Modules:
  0.0 82.4 jit_solution(9185693736549892885)
XLA Ops:
  0.0 1.6 %constant_dynamic-update-slice_fusion.4 = (bf16[4096,256]{1,0:T(8,128)(2,1)}, bf16[256,256]{1,0:T(8,128)(2,1)S(1)}) fusion(f32[256,256]{1,0:T(8,128)} %param.8), kind=kLoop, calls=%fused_computation.13 | loop fusion | flops 65535 | bytes 524288
  1.6 0.0 collective-permute-start
  1.6 5.3 %collective-permute-done = bf16[256,256]{1,0:T(8,128)(2,1)S(1)} collective-permute-done((bf16[256,256]{1,0:T(8,128)(2,1)S(1)}, bf16[256,256]{1,0:T(8,128)(2,1)S(1)}, u32[]{:S(2)}, u32[]{:S(2)}) %collective-permute-start) | collective-permute-done | bytes 131104 | tf_op jit(solution)/shard_map/ppermute | solution.py:19
  6.9 5.1 %collective-permute-start.1 = (bf16[512,256]{1,0:T(8,128)(2,1)S(1)}, bf16[512,256]{1,0:T(8,128)(2,1)S(1)}, u32[]{:S(2)}, u32[]{:S(2)}) collective-permute-start(bf16[512,256]{1,0:T(8,128)(2,1)S(1)} %pad_maximum_fusion.2), channel_id=1, source_target_pairs={{0,2},{1,3},{2,0},{3,1},{4,6},{5,7},{6,4},{7,5},{8,10},{9,11},{10,... | collective-permute-start | bytes 786440 | tf_op jit(solution)/shard_map/ppermute | solution.py:19
  12.0 6.2 %collective-permute-done.1 = bf16[512,256]{1,0:T(8,128)(2,1)S(1)} collective-permute-done((bf16[512,256]{1,0:T(8,128)(2,1)S(1)}, bf16[512,256]{1,0:T(8,128)(2,1)S(1)}, u32[]{:S(2)}, u32[]{:S(2)}) %collective-permute-start.1) | collective-permute-done | bytes 262176 | tf_op jit(solution)/shard_map/ppermute | solution.py:19
  18.3 1.3 %collective-permute-start.2 = (bf16[1024,256]{1,0:T(8,128)(2,1)S(1)}, bf16[1024,256]{1,0:T(8,128)(2,1)S(1)}, u32[]{:S(2)}, u32[]{:S(2)}) collective-permute-start(bf16[1024,256]{1,0:T(8,128)(2,1)S(1)} %pad_maximum_fusion.1), channel_id=1, source_target_pairs={{0,1},{1,0},{2,3},{3,2},{4,5},{5,4},{6,7},{7,6},{8,9},{9,8},{10,11... | collective-permute-start | bytes 1572872 | tf_op jit(solution)/shard_map/ppermute | solution.py:19
  19.6 11.2 %collective-permute-done.2 = bf16[1024,256]{1,0:T(8,128)(2,1)S(1)} collective-permute-done((bf16[1024,256]{1,0:T(8,128)(2,1)S(1)}, bf16[1024,256]{1,0:T(8,128)(2,1)S(1)}, u32[]{:S(2)}, u32[]{:S(2)}) %collective-permute-start.2) | collective-permute-done | bytes 524320 | tf_op jit(solution)/shard_map/ppermute | solution.py:19
  30.8 0.1 pad_maximum_fusion
  30.8 1.3 %collective-permute-start.3 = (bf16[2048,256]{1,0:T(8,128)(2,1)S(1)}, bf16[2048,256]{1,0:T(8,128)(2,1)S(1)}, u32[]{:S(2)}, u32[]{:S(2)}) collective-permute-start(bf16[2048,256]{1,0:T(8,128)(2,1)S(1)} %pad_maximum_fusion), channel_id=1, source_target_pairs={{0,16},{1,17},{2,18},{3,19},{4,20},{5,21},{6,22},{7,23},{8,24},{9,... | collective-permute-start | bytes 3145736 | tf_op jit(solution)/shard_map/ppermute | solution.py:19
  32.1 0.6 constant_dynamic-update-slice_fusion.10
  32.8 0.7 constant_dynamic-update-slice_fusion.3
  33.5 0.0 copy-start.1
  33.5 0.8 constant_dynamic-update-slice_fusion.2
  34.3 1.0 %constant_dynamic-update-slice_fusion.1 = (bf16[4096,256]{1,0:T(8,128)(2,1)}, bf16[8192,256]{1,0:T(8,128)(2,1)}) fusion(bf16[4096,256]{1,0:T(8,128)(2,1)} %get-tuple-element.11, bf16[1024,256]{1,0:T(8,128)(2,1)S(1)} %collective-permute-done.2, bf16[8192,256]{1,0:T(8,128)(2,1)} %get-tuple-element.12), kind=kLoop, calls=%fused_computation.10 | loop fusion | bytes 1572864
  35.3 18.3 %collective-permute-done.3 = bf16[2048,256]{1,0:T(8,128)(2,1)S(1)} collective-permute-done((bf16[2048,256]{1,0:T(8,128)(2,1)S(1)}, bf16[2048,256]{1,0:T(8,128)(2,1)S(1)}, u32[]{:S(2)}, u32[]{:S(2)}) %collective-permute-start.3) | collective-permute-done | bytes 1048608 | tf_op jit(solution)/shard_map/ppermute | solution.py:19
  53.6 1.5 %constant_dynamic-update-slice_fusion = (bf16[4096,256]{1,0:T(8,128)(2,1)}, bf16[8192,256]{1,0:T(8,128)(2,1)}) fusion(bf16[4096,256]{1,0:T(8,128)(2,1)} %get-tuple-element.9, bf16[2048,256]{1,0:T(8,128)(2,1)S(1)} %collective-permute-done.3, bf16[8192,256]{1,0:T(8,128)(2,1)} %get-tuple-element.10), kind=kLoop, calls=%fused_computation.9 | loop fusion | bytes 3145728 | tf_op jit(solution)/shard_map/concatenate | solution.py:20
  55.1 2.9 %collective-permute-start.4 = (bf16[4096,256]{1,0:T(8,128)(2,1)}, bf16[4096,256]{1,0:T(8,128)(2,1)S(1)}, u32[]{:S(2)}, u32[]{:S(2)}) collective-permute-start(bf16[4096,256]{1,0:T(8,128)(2,1)} %get-tuple-element.7), channel_id=1, source_target_pairs={{0,8},{1,9},{2,10},{3,11},{4,12},{5,13},{6,14},{7,15},{8,0},{9,1},... | collective-permute-start | bytes 6291464 | tf_op jit(solution)/shard_map/ppermute | solution.py:19
  57.9 0.0 copy-done.1
  57.9 0.1 select_add_fusion
  58.0 0.1 reshape.163
  58.1 0.1 compare_and_fusion
  58.2 0.1 broadcast_bitcast_fusion
  59.0 3.0 %collective-permute-done.4 = bf16[4096,256]{1,0:T(8,128)(2,1)S(1)} collective-permute-done((bf16[4096,256]{1,0:T(8,128)(2,1)}, bf16[4096,256]{1,0:T(8,128)(2,1)S(1)}, u32[]{:S(2)}, u32[]{:S(2)}) %collective-permute-start.4) | collective-permute-done | bytes 2097184 | tf_op jit(solution)/shard_map/ppermute | solution.py:19
  61.9 1.5 %constant_dynamic-update-slice_fusion.5 = bf16[8192,256]{1,0:T(8,128)(2,1)} fusion(bf16[8192,256]{1,0:T(8,128)(2,1)} %get-tuple-element.8, bf16[4096,256]{1,0:T(8,128)(2,1)S(1)} %collective-permute-done.4), kind=kLoop, calls=%fused_computation.14 | loop fusion | bytes 4194304 | tf_op jit(solution)/shard_map/concatenate | solution.py:20
  63.4 4.7 %fusion.4 = f32[256,256]{1,0:T(8,128)S(1)} fusion(bf16[8192,256]{1,0:T(8,128)(2,1)} %constant_dynamic-update-slice_fusion.5), kind=kOutput, calls=%fused_computation.35 | convolution fusion | flops 1073741824 | bytes 4456448 | tf_op jit(solution)/shard_map/dot_general | solution.py:39
  68.1 2.9 %gather_fusion = bf16[20,256,256]{2,1,0:T(8,128)(2,1)S(1)} fusion(bf16[32,256,256]{2,1,0:T(8,128)(2,1)} %bitcast.1, s32[1024]{0:T(1024)S(1)} %pad_clamp_fusion), kind=kCustom, calls=%fused_computation | custom fusion | bytes 5242960 | tf_op jit(solution)/shard_map/jit(_take)/gather | solution.py:47
  71.0 2.3 %fusion.5 = f32[256,1024]{1,0:T(8,128)S(1)} fusion(f32[256,256]{1,0:T(8,128)S(1)} %fusion.4, f32[256,1024]{1,0:T(8,128)} %param.9), kind=kOutput, calls=%fused_computation.36 | convolution fusion | flops 805306368 | bytes 2359296 | tf_op jit(solution)/shard_map/dot_general | solution.py:56
  73.3 0.0 copy-start
  73.3 1.1 %fusion = bf16[5,1024,256]{2,1,0:T(8,128)(2,1)S(1)} fusion(pred[5]{0:T(512)(128)(4,1)S(1)} %iota_compare_fusion, pred[5,1024]{1,0:T(8,128)(4,1)S(1)} %bitcast.26, bf16[5,1024,256]{2,1,0:T(8,128)(2,1)S(1)} %bitcast.25), kind=kLoop, calls=%fused_computation.2 | loop fusion | flops 2621440 | bytes 5248005 | tf_op jit(solution)/shard_map/jit(_where)/select_n | solution.py:49
  74.4 0.2 copy-done
  74.5 7.9 %fusion.2 = f32[256,1024]{1,0:T(8,128)} fusion(f32[256,1024]{1,0:T(8,128)S(1)} %fusion.5, f32[256,1024]{1,0:T(8,128)S(1)} %copy-done, bf16[5,1024,256]{2,1,0:T(8,128)(2,1)S(1)} %fusion, bf16[5,1024,1024]{2,1,0:T(8,128)(2,1)} %param.5), kind=kOutput, calls=%fused_computation.5 | convolution fusion | flops 2684878848 | bytes 16252928 | tf_op jit(solution)/shard_map/dot_general | solution.py:50
  (7 shorter events, 0.1 us)
Async XLA Ops:
  1.6 5.3 %collective-permute-start = (bf16[256,256]{1,0:T(8,128)(2,1)S(1)}, bf16[256,256]{1,0:T(8,128)(2,1)S(1)}, u32[]{:S(2)}, u32[]{:S(2)}) collective-permute-start(bf16[256,256]{1,0:T(8,128)(2,1)S(1)} %get-tuple-element.6), channel_id=1, source_target_pairs={{0,4},{1,5},{2,6},{3,7},{4,0},{5,1},{6,2},{7,3},{8,12},{9,13},{10,... | collective-permute-start | bytes 393224 | tf_op jit(solution)/shard_map/ppermute | solution.py:19
  6.9 11.3 %collective-permute-start.1 = (bf16[512,256]{1,0:T(8,128)(2,1)S(1)}, bf16[512,256]{1,0:T(8,128)(2,1)S(1)}, u32[]{:S(2)}, u32[]{:S(2)}) collective-permute-start(bf16[512,256]{1,0:T(8,128)(2,1)S(1)} %pad_maximum_fusion.2), channel_id=1, source_target_pairs={{0,2},{1,3},{2,0},{3,1},{4,6},{5,7},{6,4},{7,5},{8,10},{9,11},{10,... | collective-permute-start | bytes 786440 | tf_op jit(solution)/shard_map/ppermute | solution.py:19
  18.3 12.5 %collective-permute-start.2 = (bf16[1024,256]{1,0:T(8,128)(2,1)S(1)}, bf16[1024,256]{1,0:T(8,128)(2,1)S(1)}, u32[]{:S(2)}, u32[]{:S(2)}) collective-permute-start(bf16[1024,256]{1,0:T(8,128)(2,1)S(1)} %pad_maximum_fusion.1), channel_id=1, source_target_pairs={{0,1},{1,0},{2,3},{3,2},{4,5},{5,4},{6,7},{7,6},{8,9},{9,8},{10,11... | collective-permute-start | bytes 1572872 | tf_op jit(solution)/shard_map/ppermute | solution.py:19
  30.8 22.8 %collective-permute-start.3 = (bf16[2048,256]{1,0:T(8,128)(2,1)S(1)}, bf16[2048,256]{1,0:T(8,128)(2,1)S(1)}, u32[]{:S(2)}, u32[]{:S(2)}) collective-permute-start(bf16[2048,256]{1,0:T(8,128)(2,1)S(1)} %pad_maximum_fusion), channel_id=1, source_target_pairs={{0,16},{1,17},{2,18},{3,19},{4,20},{5,21},{6,22},{7,23},{8,24},{9,... | collective-permute-start | bytes 3145736 | tf_op jit(solution)/shard_map/ppermute | solution.py:19
  33.5 24.5 %copy-start.1 = (s32[5]{0:T(128)S(1)}, s32[5]{0:T(128)}, u32[]{:S(2)}) copy-start(s32[5]{0:T(128)} %param.6) | copy-start | bytes 64
  55.1 6.9 %collective-permute-start.4 = (bf16[4096,256]{1,0:T(8,128)(2,1)}, bf16[4096,256]{1,0:T(8,128)(2,1)S(1)}, u32[]{:S(2)}, u32[]{:S(2)}) collective-permute-start(bf16[4096,256]{1,0:T(8,128)(2,1)} %get-tuple-element.7), channel_id=1, source_target_pairs={{0,8},{1,9},{2,10},{3,11},{4,12},{5,13},{6,14},{7,15},{8,0},{9,1},... | collective-permute-start | bytes 6291464 | tf_op jit(solution)/shard_map/ppermute | solution.py:19
  73.3 1.2 %copy-start = (f32[256,1024]{1,0:T(8,128)S(1)}, f32[256,1024]{1,0:T(8,128)}, u32[]{:S(2)}) copy-start(f32[256,1024]{1,0:T(8,128)} %param.9) | copy-start | bytes 3145732

commit v3 on v2

v3 whole, which is shorter than its diff:
```python
import functools

import jax
import jax.numpy as jnp
from jax import lax
from jax.experimental import pallas as pl
from jax.experimental.pallas import tpu as pltpu
from jax.sharding import PartitionSpec as P

contract_rows = (((0,), (0,)), ((), ()))
AXES = ("row", "col")
COLUMN_CHUNK = 256


def doubling_order(n_row, n_col):
    col_bits = [1 << k for k in range(n_col.bit_length() - 1)][::-1]
    row_bits = [n_col << k for k in range(n_row.bit_length() - 1)][::-1]
    return col_bits + row_bits


def swap(value, mask, n):
    return lax.ppermute(value, AXES, [(i, i ^ mask) for i in range(n)])


def slot_of(distance, order):
    pos = jnp.zeros_like(distance)
    for k, mask in enumerate(order):
        pos = pos + jnp.where((distance & mask) != 0, 1 << k, 0)
    return pos


def slot_kernel(per_block, pos_ref, act_ref, acc_in, pieces_hbm, tiles_hbm, acc_out, w_vmem, t_vmem, sems):
    s = pl.program_id(0)
    tile = t_vmem.shape[0]

    @pl.when(s == 0)
    def _():
        acc_out[...] = acc_in[...]

    @pl.when(act_ref[s] != 0)
    def _():
        tile_copy = pltpu.make_async_copy(tiles_hbm.at[s], t_vmem, sems.at[per_block])
        tile_copy.start()
        for q in range(per_block):
            pltpu.make_async_copy(
                pieces_hbm.at[pos_ref[s * per_block + q]], w_vmem.at[q], sems.at[q]
            ).start()
        for q in range(per_block):
            pltpu.make_async_copy(pieces_hbm.at[0], w_vmem.at[q], sems.at[q]).wait()
        tile_copy.wait()
        w = w_vmem[...].reshape(tile, w_vmem.shape[2])
        for c in range(tile // COLUMN_CHUNK):
            cols = slice(c * COLUMN_CHUNK, (c + 1) * COLUMN_CHUNK)
            acc_out[:, cols] += lax.dot_general(
                w, t_vmem[:, cols], contract_rows, preferred_element_type=jnp.float32
            )


def slot_products(acc, pieces, tiles, pos, active):
    slots, tile, width = tiles.shape
    per_block, share, rank_size = pos.shape[1], pieces.shape[1], pieces.shape[2]
    kernel = functools.partial(slot_kernel, per_block)
    return pl.pallas_call(
        kernel,
        out_shape=jax.ShapeDtypeStruct(acc.shape, acc.dtype),
        grid_spec=pltpu.PrefetchScalarGridSpec(
            num_scalar_prefetch=2,
            grid=(slots,),
            in_specs=[
                pl.BlockSpec(acc.shape, lambda s, p, a: (0, 0)),
                pl.BlockSpec(memory_space=pl.ANY),
                pl.BlockSpec(memory_space=pl.ANY),
            ],
            out_specs=pl.BlockSpec(acc.shape, lambda s, p, a: (0, 0)),
            scratch_shapes=[
                pltpu.VMEM((per_block, share, rank_size), pieces.dtype),
                pltpu.VMEM((tile, width), tiles.dtype),
                pltpu.SemaphoreType.DMA((per_block + 1,)),
            ],
        ),
        input_output_aliases={2: 0},
        cost_estimate=pl.CostEstimate(
            flops=2 * slots * tile * width * rank_size,
            transcendentals=0,
            bytes_accessed=slots * (tile * width * 2 + tile * rank_size * 2) + 2 * acc.size * 4,
        ),
    )(pos.reshape(-1), active.astype(jnp.int32), acc, pieces, tiles)


def shards(tiles, tile_list, tile_count, w_rows, h_cols, n_row, n_col):
    slots, tile = tiles.shape[0], tiles.shape[1]
    rank_size = h_cols.shape[0]
    n = n_row * n_col
    share = w_rows.shape[0]
    order = doubling_order(n_row, n_col)
    steps = len(order)

    me = lax.axis_index("row") * n_col + lax.axis_index("col")
    per_block = tile // share
    blocks_total = n // per_block
    rows_of = jnp.clip(tile_list, 0, blocks_total - 1)
    owners = rows_of[:, None] * per_block + jnp.arange(per_block, dtype=jnp.int32)[None, :]
    where = slot_of(owners ^ me, order)
    need = functools.reduce(jnp.bitwise_or, [owners[:, q] ^ me for q in range(per_block)])
    done_at = jnp.full((slots,), -1, jnp.int32)
    for k, mask in enumerate(order):
        done_at = jnp.where((need & mask) != 0, k, done_at)
    live = jnp.arange(slots, dtype=jnp.int32) < tile_count[0]

    def phase(acc, source, base, first_step, last_step):
        active = live & (done_at >= first_step) & (done_at <= last_step)
        size = source.shape[0] // share
        pos = jnp.clip(where - base, 0, size - 1)
        return slot_products(acc, source.reshape(size, share, rank_size), tiles, pos, active)

    buf = w_rows.astype(jnp.bfloat16)
    gram = lax.dot_general(buf, buf, contract_rows, preferred_element_type=jnp.float32)
    for k in range(steps - 2):
        moved = swap(buf, order[k], n)
        gram = gram + lax.dot_general(moved, moved, contract_rows, preferred_element_type=jnp.float32)
        buf = jnp.concatenate([buf, moved], axis=0)

    zeros = jnp.zeros((rank_size, tiles.shape[2]), jnp.float32)
    moved = swap(buf, order[steps - 2], n)
    early = phase(zeros, buf, 0, -1, steps - 3)
    gram = gram + lax.dot_general(moved, moved, contract_rows, preferred_element_type=jnp.float32)
    moved, early = lax.optimization_barrier((moved, early))
    numerator = phase(zeros, moved, buf.shape[0] // share, steps - 2, steps - 2)
    buf = jnp.concatenate([buf, moved], axis=0)

    moved, partner_gram = swap((buf, gram), order[steps - 1], n)
    numerator = phase(numerator, moved, buf.shape[0] // share, steps - 1, steps - 1)
    gram = gram + partner_gram
    numerator = numerator + early

    denominator = jnp.dot(
        gram, h_cols, precision=lax.Precision.HIGHEST, preferred_element_type=jnp.float32
    )
    return h_cols * numerator / denominator


def solution(mesh):
    n_row, n_col = mesh.shape["row"], mesh.shape["col"]
    placed = (
        P(AXES, None, None),
        P(AXES),
        P(AXES),
        P(AXES, None),
        P(None, AXES),
    )

    def body(tiles, tile_list, tile_count, w_rows, h_cols):
        return shards(tiles, tile_list, tile_count, w_rows, h_cols, n_row, n_col)

    return jax.shard_map(
        body, mesh=mesh, in_specs=placed, out_specs=P(None, AXES), check_vma=False
    )
```

time: 82.7 us -> 82.4 us (level)
  the two profiles are of different devices: /device:TPU:17 before, /device:TPU:20 now
where the time goes in v3:
time: 82.4 us; the launch traced here: 83.8 us
  waiting for transfers between devices  38.9 us (47%)
  Pallas kernels  21.4 us (26%)
  local copies, waits for them, and re-layouts  7.67 us (9%)
  starting transfers between devices  7.28 us (9%)
  matrix products  4.86 us (6%)
  other arithmetic  2.85 us (3%)
    ppermute x6, waiting for transfers between devices, swap(): return lax.ppermute(value, AXES, [(i, i ^ mask) for i in range(n)])  38.9 us
    pallas_call x3, Pallas kernels, slot_products(): pl.pallas_call(kernel, out_shape=jax.ShapeDtypeStruct(acc.shape, acc.dtyp...  21.4 us
    ppermute x6, starting transfers between devices, swap(): return lax.ppermute(value, AXES, [(i, i ^ mask) for i in range(n)])  7.28 us
    dot_general x1, matrix products, shards(): jnp.dot(gram, h_cols, precision=lax.Precision.HIGHEST, preferred_element_...  3.34 us
    unnamed x13, local copies, waits for them, and re-layouts  2.25 us
    broadcast_in_dim x2, local copies, waits for them, and re-layouts, shards(): zeros = jnp.zeros((rank_size, tiles.shape[2]), jnp.float32)  2.23 us
    min x6, local copies, waits for them, and re-layouts, phase(): pos = jnp.clip(where - base, 0, size - 1)  2.09 us
  transfers between devices with their start and end apart: 6, of which 4 were waited for; matrix products, arithmetic and copies ran while one was open for 11% of the time, Pallas kernels for 26%

profile of v3, /device:TPU:20, one launch (start us, length us, event | category | flops | bytes accessed | tf_op | source)
XLA Modules:
  0.0 83.8 jit_solution(11820763681543917223)
XLA Ops:
  0.0 0.0 copy-start.4
  0.0 1.6 %constant_dynamic-update-slice_fusion.4 = (bf16[4096,256]{1,0:T(8,128)(2,1)}, bf16[256,256]{1,0:T(8,128)(2,1)S(1)}) fusion(f32[256,256]{1,0:T(8,128)} %param.8), kind=kLoop, calls=%fused_computation.14 | loop fusion | flops 65535 | bytes 524288
  1.6 0.3 collective-permute-start
  2.0 5.9 %collective-permute-done = bf16[256,256]{1,0:T(8,128)(2,1)S(1)} collective-permute-done((bf16[256,256]{1,0:T(8,128)(2,1)S(1)}, bf16[256,256]{1,0:T(8,128)(2,1)S(1)}, u32[]{:S(2)}, u32[]{:S(2)}) %collective-permute-start) | collective-permute-done | bytes 131104 | tf_op jit(solution)/shard_map/ppermute | solution.py:22
  7.9 4.2 %collective-permute-start.1 = (bf16[512,256]{1,0:T(8,128)(2,1)S(1)}, bf16[512,256]{1,0:T(8,128)(2,1)S(1)}, u32[]{:S(2)}, u32[]{:S(2)}) collective-permute-start(bf16[512,256]{1,0:T(8,128)(2,1)S(1)} %pad_maximum_fusion.2), channel_id=1, source_target_pairs={{0,2},{1,3},{2,0},{3,1},{4,6},{5,7},{6,4},{7,5},{8,10},{9,11},{10,... | collective-permute-start | bytes 786440 | tf_op jit(solution)/shard_map/ppermute | solution.py:22
  12.1 6.5 %collective-permute-done.1 = bf16[512,256]{1,0:T(8,128)(2,1)S(1)} collective-permute-done((bf16[512,256]{1,0:T(8,128)(2,1)S(1)}, bf16[512,256]{1,0:T(8,128)(2,1)S(1)}, u32[]{:S(2)}, u32[]{:S(2)}) %collective-permute-start.1) | collective-permute-done | bytes 262176 | tf_op jit(solution)/shard_map/ppermute | solution.py:22
  18.7 0.6 collective-permute-start.2
  19.9 0.0 copy-done.4
  19.9 12.1 %collective-permute-done.2 = bf16[1024,256]{1,0:T(8,128)(2,1)S(1)} collective-permute-done((bf16[1024,256]{1,0:T(8,128)(2,1)S(1)}, bf16[1024,256]{1,0:T(8,128)(2,1)S(1)}, u32[]{:S(2)}, u32[]{:S(2)}) %collective-permute-start.2) | collective-permute-done | bytes 524320 | tf_op jit(solution)/shard_map/ppermute | solution.py:22
  32.0 0.1 pad_maximum_fusion
  32.1 0.0 copy-start.2
  32.1 1.6 %collective-permute-start.3 = (bf16[2048,256]{1,0:T(8,128)(2,1)S(1)}, bf16[2048,256]{1,0:T(8,128)(2,1)S(1)}, u32[]{:S(2)}, u32[]{:S(2)}) collective-permute-start(bf16[2048,256]{1,0:T(8,128)(2,1)S(1)} %pad_maximum_fusion), channel_id=1, source_target_pairs={{0,16},{1,17},{2,18},{3,19},{4,20},{5,21},{6,22},{7,23},{8,24},{9,... | collective-permute-start | bytes 3145736 | tf_op jit(solution)/shard_map/ppermute | solution.py:22
  33.7 0.1 copy.14
  33.8 0.6 reshape.111.pos_ref
  34.4 0.5 fusion.6
  34.9 0.7 constant_dynamic-update-slice_fusion.3
  35.5 0.7 constant_dynamic-update-slice_fusion.2
  36.3 0.8 constant_dynamic-update-slice_fusion.1
  37.1 1.1 %broadcast_in_dim.41.clone.acc_in = f32[256,1024]{1,0:T(8,128)} broadcast(f32[]{:T(128)} %constant.6.clone.1), dimensions={} | broadcast | bytes 1048580 | tf_op jit(solution)/shard_map/broadcast_in_dim | solution.py:123
  38.2 0.0 copy-done.2
  38.2 3.1 %shard_map.55 = f32[256,1024]{1,0:T(8,128)} custom-call(s32[20]{0:T(128)} %reshape.111.pos_ref, s32[5]{0:T(128)} %get-tuple-element.11.act_ref, f32[256,1024]{1,0:T(8,128)} %broadcast_in_dim.41.clone.acc_in, bf16[8,256,256]{2,1,0:T(8,128)(2,1)} %bitcast.42, bf16[5,1024,1024]{2,1,0:T(8,128)(2,1)} %tiles_hbm.5), custom_call_target="tpu_custom_call", output_to_operand_aliasing={{}: (2, {})} | custom-call | flops 2684354560 | bytes 15204352 | tf_op jit(solution)/shard_map/pallas_call | solution.py:63
  41.4 14.4 %collective-permute-done.3 = bf16[2048,256]{1,0:T(8,128)(2,1)S(1)} collective-permute-done((bf16[2048,256]{1,0:T(8,128)(2,1)S(1)}, bf16[2048,256]{1,0:T(8,128)(2,1)S(1)}, u32[]{:S(2)}, u32[]{:S(2)}) %collective-permute-start.3) | collective-permute-done | bytes 1048608 | tf_op jit(solution)/shard_map/ppermute | solution.py:22
  55.8 0.0 copy-start
  55.8 1.1 %constant_dynamic-update-slice_fusion = bf16[4096,256]{1,0:T(8,128)(2,1)} fusion(bf16[4096,256]{1,0:T(8,128)(2,1)} %constant_dynamic-update-slice_fusion.1, bf16[2048,256]{1,0:T(8,128)(2,1)S(1)} %collective-permute-done.3), kind=kLoop, calls=%fused_computation.10 | loop fusion | bytes 2097152 | tf_op jit(solution)/shard_map/concatenate | solution.py:129
  56.9 0.0 collective-permute-start.4
  56.9 0.1 copy.13
  57.0 0.6 reshape.119.pos_ref
  57.6 0.1 copy.12
  57.7 0.6 reshape.114.pos_ref
  58.3 0.6 fusion.7
  58.9 0.2 fusion.9
  59.1 0.2 convolution_add_fusion.1
  59.4 0.3 fusion.10
  59.7 0.0 copy-done
  59.7 0.5 fusion.11
  60.2 0.3 fusion.1
  60.5 0.6 collective-permute-start.5
  61.1 1.1 %broadcast_in_dim.41.acc_in = f32[256,1024]{1,0:T(8,128)} broadcast(f32[]{:T(128)} %constant.6.clone.1), dimensions={} | broadcast | bytes 1048580 | tf_op jit(solution)/shard_map/broadcast_in_dim | solution.py:123
  62.1 5.5 %shard_map.56.acc_in = f32[256,1024]{1,0:T(8,128)} custom-call(s32[20]{0:T(128)} %reshape.119.pos_ref, s32[5]{0:T(128)} %get-tuple-element.17.act_ref, f32[256,1024]{1,0:T(8,128)} %broadcast_in_dim.41.acc_in, bf16[8,256,256]{2,1,0:T(8,128)(2,1)} %bitcast.41, bf16[5,1024,1024]{2,1,0:T(8,128)(2,1)} %tiles_hbm.5), custom_call_target="tpu_custom_call", output_to_operand_aliasing={{}: (2, {})} | custom-call | flops 2684354560 | bytes 15204352 | tf_op jit(solution)/shard_map/pallas_call | solution.py:63
  67.6 0.0 collective-permute-done.4
  67.6 0.0 copy-start.1
  67.7 0.0 copy-start.3
  67.7 12.8 %shard_map.57 = f32[256,1024]{1,0:T(8,128)} custom-call(s32[20]{0:T(128)} %reshape.114.pos_ref, s32[5]{0:T(128)} %get-tuple-element.18.act_ref, f32[256,1024]{1,0:T(8,128)} %shard_map.56.acc_in, bf16[16,256,256]{2,1,0:T(8,128)(2,1)} %bitcast.9.pieces_hbm, bf16[5,1024,1024]{2,1,0:T(8,128)(2,1)} %tiles_hbm.5), custom_call_target="tpu_custom_call", output_to_operand_aliasing={{}: (2, {})} | custom-call | flops 2684354560 | bytes 15204352 | tf_op jit(solution)/shard_map/pallas_call | solution.py:63
  80.4 0.0 collective-permute-done.5
  80.5 0.0 copy-done.1
  80.5 0.0 copy-done.3
  80.5 3.3 %multiply_divide_fusion = f32[256,1024]{1,0:T(8,128)} fusion(f32[256,1024]{1,0:T(8,128)S(1)} %copy-done.3, f32[256,1024]{1,0:T(8,128)} %shard_map.57, f32[256,1024]{1,0:T(8,128)S(1)} %copy-done.1, f32[256,256]{1,0:T(8,128)S(1)} %fusion.1, f32[256,256]{1,0:T(8,128)S(1)} %collective-permute-done.5), kind=kOutput, calls=%fused_computation.5 | convolution fusion | flops 806158336 | bytes 4718592 | tf_op jit(solution)/shard_map/dot_general | solution.py:136
  (4 shorter events, 0.1 us)
Async XLA Ops:
  0.0 19.9 %copy-start.4 = (s32[5]{0:T(128)S(1)}, s32[5]{0:T(128)}, u32[]{:S(2)}) copy-start(s32[5]{0:T(128)} %param.6) | copy-start | bytes 64
  1.6 6.2 %collective-permute-start = (bf16[256,256]{1,0:T(8,128)(2,1)S(1)}, bf16[256,256]{1,0:T(8,128)(2,1)S(1)}, u32[]{:S(2)}, u32[]{:S(2)}) collective-permute-start(bf16[256,256]{1,0:T(8,128)(2,1)S(1)} %get-tuple-element.10), channel_id=1, source_target_pairs={{0,4},{1,5},{2,6},{3,7},{4,0},{5,1},{6,2},{7,3},{8,12},{9,13},{10,... | collective-permute-start | bytes 393224 | tf_op jit(solution)/shard_map/ppermute | solution.py:22
  7.9 10.7 %collective-permute-start.1 = (bf16[512,256]{1,0:T(8,128)(2,1)S(1)}, bf16[512,256]{1,0:T(8,128)(2,1)S(1)}, u32[]{:S(2)}, u32[]{:S(2)}) collective-permute-start(bf16[512,256]{1,0:T(8,128)(2,1)S(1)} %pad_maximum_fusion.2), channel_id=1, source_target_pairs={{0,2},{1,3},{2,0},{3,1},{4,6},{5,7},{6,4},{7,5},{8,10},{9,11},{10,... | collective-permute-start | bytes 786440 | tf_op jit(solution)/shard_map/ppermute | solution.py:22
  18.7 13.4 %collective-permute-start.2 = (bf16[1024,256]{1,0:T(8,128)(2,1)S(1)}, bf16[1024,256]{1,0:T(8,128)(2,1)S(1)}, u32[]{:S(2)}, u32[]{:S(2)}) collective-permute-start(bf16[1024,256]{1,0:T(8,128)(2,1)S(1)} %pad_maximum_fusion.1), channel_id=1, source_target_pairs={{0,1},{1,0},{2,3},{3,2},{4,5},{5,4},{6,7},{7,6},{8,9},{9,8},{10,11... | collective-permute-start | bytes 1572872 | tf_op jit(solution)/shard_map/ppermute | solution.py:22
  32.1 6.1 %copy-start.2 = (bf16[2048,256]{1,0:T(8,128)(2,1)}, bf16[2048,256]{1,0:T(8,128)(2,1)S(1)}, u32[]{:S(2)}) copy-start(bf16[2048,256]{1,0:T(8,128)(2,1)S(1)} %pad_maximum_fusion) | copy-start | bytes 3145732
  32.1 23.7 %collective-permute-start.3 = (bf16[2048,256]{1,0:T(8,128)(2,1)S(1)}, bf16[2048,256]{1,0:T(8,128)(2,1)S(1)}, u32[]{:S(2)}, u32[]{:S(2)}) collective-permute-start(bf16[2048,256]{1,0:T(8,128)(2,1)S(1)} %pad_maximum_fusion), channel_id=1, source_target_pairs={{0,16},{1,17},{2,18},{3,19},{4,20},{5,21},{6,22},{7,23},{8,24},{9,... | collective-permute-start | bytes 3145736 | tf_op jit(solution)/shard_map/ppermute | solution.py:22
  55.8 3.9 %copy-start = (bf16[2048,256]{1,0:T(8,128)(2,1)}, bf16[2048,256]{1,0:T(8,128)(2,1)S(1)}, u32[]{:S(2)}) copy-start(bf16[2048,256]{1,0:T(8,128)(2,1)S(1)} %collective-permute-done.3) | copy-start | bytes 3145732
  56.9 10.7 %collective-permute-start.4 = (bf16[4096,256]{1,0:T(8,128)(2,1)}, bf16[4096,256]{1,0:T(8,128)(2,1)}, u32[]{:S(2)}, u32[]{:S(2)}) collective-permute-start(bf16[4096,256]{1,0:T(8,128)(2,1)} %constant_dynamic-update-slice_fusion), channel_id=1, source_target_pairs={{0,8},{1,9},{2,10},{3,11},{4,12},{5,13},{6,14},{7,15},{8,0},{9,1},... | collective-permute-start | bytes 6291464 | tf_op jit(solution)/shard_map/ppermute | solution.py:22
  60.5 20.0 %collective-permute-start.5 = (f32[256,256]{1,0:T(8,128)S(1)}, f32[256,256]{1,0:T(8,128)S(1)}, u32[]{:S(2)}, u32[]{:S(2)}) collective-permute-start(f32[256,256]{1,0:T(8,128)S(1)} %fusion.1), channel_id=1, source_target_pairs={{0,8},{1,9},{2,10},{3,11},{4,12},{5,13},{6,14},{7,15},{8,0},{9,1},... | collective-permute-start | bytes 786440 | tf_op jit(solution)/shard_map/ppermute | solution.py:22
  67.6 12.8 %copy-start.1 = (f32[256,1024]{1,0:T(8,128)S(1)}, f32[256,1024]{1,0:T(8,128)}, u32[]{:S(2)}) copy-start(f32[256,1024]{1,0:T(8,128)} %shard_map.55) | copy-start | bytes 3145732
  67.7 12.8 %copy-start.3 = (f32[256,1024]{1,0:T(8,128)S(1)}, f32[256,1024]{1,0:T(8,128)}, u32[]{:S(2)}) copy-start(f32[256,1024]{1,0:T(8,128)} %param.9) | copy-start | bytes 3145732

commit v4 on v2

v4 whole, which is shorter than its diff:
```python
import jax
import jax.numpy as jnp
from jax import lax
from jax.sharding import Mesh
from jax.sharding import PartitionSpec as P

contract_rows = (((0,), (0,)), ((), ()))
SUB = ("rh", "core", "ch", "cl")


def swap(value, mask, n):
    return lax.ppermute(value, SUB, [(i, i ^ mask) for i in range(n)])


def gather_rows(w_half, n, n_col, col_masks):
    buf = w_half
    for mask in col_masks:
        buf = jnp.concatenate([buf, swap(buf, mask, n)], axis=0)
    group = lax.psum(1, ("rh", "cl"))
    spread = jnp.broadcast_to(buf[None], (group,) + buf.shape)
    buf = lax.all_to_all(spread, ("rh", "cl"), 0, 0, tiled=False).reshape(-1, buf.shape[1])
    return jnp.concatenate([buf, swap(buf, n_col, n)], axis=0)


def position_of(j, me, n_col, col_masks, group):
    near = jnp.zeros_like(j)
    for k, mask in enumerate(col_masks):
        near = near + jnp.where(((j ^ me) & mask) != 0, 1 << k, 0)
    first = 1 << len(col_masks)
    row_idx, col_idx = j // n_col, j % n_col
    member = (row_idx // 2) * 2 + (col_idx % 2)
    other_core = (row_idx % 2) != ((me // n_col) % 2)
    return jnp.where(other_core, group * first, 0) + member * first + near


def shards(tiles, tile_list, tile_count, w_rows, h_cols, n_row, n_col):
    slots, tile = tiles.shape[0], tiles.shape[1]
    rank_size = h_cols.shape[0]
    n = n_row * n_col
    share = w_rows.shape[0]
    col_masks = [2 << b for b in range(n_col.bit_length() - 2)][::-1]
    w_half = w_rows.astype(jnp.bfloat16)
    buf = gather_rows(w_half, n, n_col, col_masks)
    gram = lax.dot_general(buf, buf, contract_rows, preferred_element_type=jnp.float32)
    me = lax.axis_index(SUB)
    per_block = tile // share
    blocks_total = n // per_block
    rows_of = jnp.clip(tile_list, 0, blocks_total - 1)
    owners = rows_of[:, None] * per_block + jnp.arange(per_block, dtype=jnp.int32)[None, :]
    where = position_of(owners, me, n_col, col_masks, 2 * (n_row // 2))
    pieces = buf.reshape(n, share, rank_size)
    picked = jnp.take(pieces, where.reshape(-1), axis=0).reshape(slots, tile, rank_size)
    live = jnp.arange(slots, dtype=jnp.int32) < tile_count[0]
    picked = jnp.where(live[:, None, None], picked, jnp.zeros_like(picked))
    numerator = lax.dot_general(
        picked.reshape(slots * tile, rank_size),
        tiles.reshape(slots * tile, tiles.shape[2]),
        contract_rows,
        preferred_element_type=jnp.float32,
    )
    denominator = jnp.dot(
        gram, h_cols, precision=lax.Precision.HIGHEST, preferred_element_type=jnp.float32
    )
    return h_cols * numerator / denominator


def solution(mesh):
    n_row, n_col = mesh.shape["row"], mesh.shape["col"]
    sub = Mesh(mesh.devices.reshape(n_row // 2, 2, n_col // 2, 2), SUB)
    placed = (
        P(SUB, None, None),
        P(SUB),
        P(SUB),
        P(SUB, None),
        P(None, SUB),
    )

    def body(tiles, tile_list, tile_count, w_rows, h_cols):
        return shards(tiles, tile_list, tile_count, w_rows, h_cols, n_row, n_col)

    return jax.shard_map(
        body, mesh=sub, in_specs=placed, out_specs=P(None, SUB), check_vma=False
    )
```

time: 82.7 us -> 69.3 us (0.84)
  the two profiles are of different devices: /device:TPU:17 before, /device:TPU:0 now
where the time goes in v4:
time: 69.3 us; the launch traced here: 68.3 us
  blocking collectives  27.2 us (39%)
  waiting for transfers between devices  16.3 us (24%)
  matrix products  9.79 us (14%)
  other arithmetic  6.1 us (9%)
  starting transfers between devices  4.89 us (7%)
  local copies, waits for them, and re-layouts  3.24 us (5%)
  between operations  0.82 us (1%)
    all_to_all x1, blocking collectives, gather_rows(): lax.all_to_all(spread, ('rh', 'cl'), 0, 0, tiled=False)  27.2 us
    ppermute x3, waiting for transfers between devices, swap(): return lax.ppermute(value, SUB, [(i, i ^ mask) for i in range(n)])  16.3 us
    ppermute x3, starting transfers between devices, swap(): return lax.ppermute(value, SUB, [(i, i ^ mask) for i in range(n)])  4.89 us
    dot_general x1, matrix products, shards(): lax.dot_general(buf, buf, contract_rows, preferred_element_type=jnp.float32)  4.89 us
    dot_general x1, matrix products, shards(): lax.dot_general(picked.reshape(slots * tile, rank_size), tiles.reshape(sl...  3.87 us
    concatenate x1, other arithmetic, gather_rows(): return jnp.concatenate([buf, swap(buf, n_col, n)], axis=0)  3.82 us
    gather x1, local copies, waits for them, and re-layouts, shards(): jnp.take(pieces, where.reshape(-1), axis=0).reshape(slots, tile, rank_size)  2.9 us
  transfers between devices with their start and end apart: 3, of which 3 were waited for; matrix products, arithmetic and copies ran while one was open for 1% of the time, Pallas kernels for 0%

profile of v4, /device:TPU:0, one launch (start us, length us, event | category | flops | bytes accessed | tf_op | source)
XLA Modules:
  0.0 68.3 jit_solution(361934108131542663)
XLA Ops:
  0.0 1.0 %convert_element_type.3 = bf16[256,256]{1,0:T(8,128)(2,1)S(1)} convert(f32[256,256]{1,0:T(8,128)} %param.8) | non-fusion elementwise | flops 65536 | bytes 393216 | tf_op jit(solution)/shard_map/convert_element_type | solution.py:42
  1.0 4.1 %collective-permute-start = (bf16[256,256]{1,0:T(8,128)(2,1)S(1)}, bf16[256,256]{1,0:T(8,128)(2,1)S(1)}, u32[]{:S(2)}, u32[]{:S(2)}) collective-permute-start(bf16[256,256]{1,0:T(8,128)(2,1)S(1)} %convert_element_type.3), channel_id=1, source_target_pairs={{0,4},{1,5},{2,6},{3,7},{4,0},{5,1},{6,2},{7,3},{8,12},{9,13},{10,... | collective-permute-start | bytes 393224 | tf_op jit(solution)/shard_map/ppermute | solution.py:12
  5.1 6.3 %collective-permute-done = bf16[256,256]{1,0:T(8,128)(2,1)S(1)} collective-permute-done((bf16[256,256]{1,0:T(8,128)(2,1)S(1)}, bf16[256,256]{1,0:T(8,128)(2,1)S(1)}, u32[]{:S(2)}, u32[]{:S(2)}) %collective-permute-start) | collective-permute-done | bytes 131104 | tf_op jit(solution)/shard_map/ppermute | solution.py:12
  11.4 0.8 %collective-permute-start.1 = (bf16[512,256]{1,0:T(8,128)(2,1)S(1)}, bf16[512,256]{1,0:T(8,128)(2,1)S(1)}, u32[]{:S(2)}, u32[]{:S(2)}) collective-permute-start(bf16[512,256]{1,0:T(8,128)(2,1)S(1)} %pad_maximum_fusion.2), channel_id=1, source_target_pairs={{0,2},{1,3},{2,0},{3,1},{4,6},{5,7},{6,4},{7,5},{8,10},{9,11},{10,... | collective-permute-start | bytes 786440 | tf_op jit(solution)/shard_map/ppermute | solution.py:12
  12.2 6.8 %collective-permute-done.1 = bf16[512,256]{1,0:T(8,128)(2,1)S(1)} collective-permute-done((bf16[512,256]{1,0:T(8,128)(2,1)S(1)}, bf16[512,256]{1,0:T(8,128)(2,1)S(1)}, u32[]{:S(2)}, u32[]{:S(2)}) %collective-permute-start.1) | collective-permute-done | bytes 262176 | tf_op jit(solution)/shard_map/ppermute | solution.py:12
  19.0 0.1 broadcast_in_dim.51
  19.1 0.0 copy-start.2
  19.2 27.2 %all_to_all.5 = bf16[4,1024,256]{2,1,0:T(8,128)(2,1)S(1)} all-to-all(bf16[4,1024,256]{2,1,0:T(8,128)(2,1)S(1)} %broadcast_in_dim.51), channel_id=1, replica_groups=mesh['rh'=2,'core'=2,'ch'=4,'cl'=2] {'rh','cl'}, dimensions={0} | all-to-all | bytes 4194304 | tf_op jit(solution)/shard_map/all_to_all | solution.py:21
  46.4 0.0 copy-start
  46.4 0.0 collective-permute-start.2
  47.0 0.0 copy-done.2
  47.0 0.1 iota_add_fusion
  47.1 0.1 add.213
  47.2 0.1 compare_and_fusion
  47.3 0.1 broadcast_bitcast_fusion
  47.4 3.2 %collective-permute-done.2 = bf16[4096,256]{1,0:T(8,128)(2,1)} collective-permute-done((bf16[4096,256]{1,0:T(8,128)(2,1)S(1)}, bf16[4096,256]{1,0:T(8,128)(2,1)}, u32[]{:S(2)}, u32[]{:S(2)}) %collective-permute-start.2) | collective-permute-done | bytes 2097184 | tf_op jit(solution)/shard_map/ppermute | solution.py:12
  50.6 3.8 %pad_maximum_fusion = bf16[8192,256]{1,0:T(8,128)(2,1)} fusion(bf16[4096,256]{1,0:T(8,128)(2,1)} %collective-permute-done.2, bf16[4096,256]{1,0:T(8,128)(2,1)S(1)} %bitcast.29), kind=kLoop, calls=%fused_computation.1 | loop fusion | flops 8388608 | bytes 8388608 | tf_op jit(solution)/shard_map/concatenate | solution.py:22
  54.5 0.0 copy-done
  54.5 2.9 %gather_fusion = bf16[20,256,256]{2,1,0:T(8,128)(2,1)S(1)} fusion(bf16[32,256,256]{2,1,0:T(8,128)(2,1)} %bitcast.24, s32[1024]{0:T(1024)S(1)} %pad_clamp_fusion), kind=kCustom, calls=%fused_computation | custom fusion | bytes 5242960 | tf_op jit(solution)/shard_map/jit(_take)/gather | solution.py:52
  57.4 0.0 copy-start.1
  57.4 0.0 slice-start
  57.4 0.0 slice-start.1
  57.4 4.9 %fusion.24 = f32[256,256]{1,0:T(8,128)S(1)} fusion(bf16[4096,256]{1,0:T(8,128)(2,1)} %collective-permute-done.2, bf16[4096,256]{1,0:T(8,128)(2,1)} %bitcast.30), kind=kOutput, calls=%fused_computation.71 | convolution fusion | flops 1082130432 | bytes 4456448 | tf_op jit(solution)/shard_map/dot_general | solution.py:44
  62.3 0.0 copy-done.1
  62.3 0.0 slice-start.2
  62.3 1.0 %fusion.25 = f32[256,1024]{1,0:T(8,128)S(1)} fusion(f32[256,256]{1,0:T(8,128)S(1)} %fusion.24, f32[256,1024]{1,0:T(8,128)S(1)} %copy-done.1), kind=kOutput, calls=%fused_computation.72 | convolution fusion | flops 805306368 | bytes 2359296 | tf_op jit(solution)/shard_map/dot_general | solution.py:61
  63.4 1.1 %fusion = bf16[5,1024,256]{2,1,0:T(8,128)(2,1)S(1)} fusion(pred[5]{0:T(512)(128)(4,1)S(1)} %iota_compare_fusion, pred[5,1024]{1,0:T(8,128)(4,1)S(1)} %bitcast.31, bf16[5,1024,256]{2,1,0:T(8,128)(2,1)S(1)} %bitcast.27), kind=kLoop, calls=%fused_computation.3 | loop fusion | flops 2621440 | bytes 5248005 | tf_op jit(solution)/shard_map/jit(_where)/select_n | solution.py:54
  64.4 0.0 slice-done
  64.4 0.0 slice-done.1
  64.5 0.0 slice-done.2
  64.5 3.9 %fusion.2 = f32[256,1024]{1,0:T(8,128)} fusion(f32[256,1024]{1,0:T(8,128)S(1)} %fusion.25, f32[256,1024]{1,0:T(8,128)S(1)} %copy-done.1, bf16[5,1024,256]{2,1,0:T(8,128)(2,1)S(1)} %fusion, bf16[5,1024,1024]{2,1,0:T(8,128)(2,1)S(1)} %bitcast.26), kind=kOutput, calls=%fused_computation.6 | convolution fusion | flops 2684878848 | bytes 16252928 | tf_op jit(solution)/shard_map/dot_general | solution.py:55
  (8 shorter events, 0.1 us)
Async XLA Ops:
  1.0 10.4 %collective-permute-start = (bf16[256,256]{1,0:T(8,128)(2,1)S(1)}, bf16[256,256]{1,0:T(8,128)(2,1)S(1)}, u32[]{:S(2)}, u32[]{:S(2)}) collective-permute-start(bf16[256,256]{1,0:T(8,128)(2,1)S(1)} %convert_element_type.3), channel_id=1, source_target_pairs={{0,4},{1,5},{2,6},{3,7},{4,0},{5,1},{6,2},{7,3},{8,12},{9,13},{10,... | collective-permute-start | bytes 393224 | tf_op jit(solution)/shard_map/ppermute | solution.py:12
  11.4 7.6 %collective-permute-start.1 = (bf16[512,256]{1,0:T(8,128)(2,1)S(1)}, bf16[512,256]{1,0:T(8,128)(2,1)S(1)}, u32[]{:S(2)}, u32[]{:S(2)}) collective-permute-start(bf16[512,256]{1,0:T(8,128)(2,1)S(1)} %pad_maximum_fusion.2), channel_id=1, source_target_pairs={{0,2},{1,3},{2,0},{3,1},{4,6},{5,7},{6,4},{7,5},{8,10},{9,11},{10,... | collective-permute-start | bytes 786440 | tf_op jit(solution)/shard_map/ppermute | solution.py:12
  19.1 27.9 %copy-start.2 = (s32[5]{0:T(128)S(1)}, s32[5]{0:T(128)}, u32[]{:S(2)}) copy-start(s32[5]{0:T(128)} %param.6) | copy-start | bytes 64
  46.4 8.1 %copy-start = (bf16[4,1024,256]{2,1,0:T(8,128)(2,1)}, bf16[4,1024,256]{2,1,0:T(8,128)(2,1)S(1)}, u32[]{:S(2)}) copy-start(bf16[4,1024,256]{2,1,0:T(8,128)(2,1)S(1)} %all_to_all.5) | copy-start | bytes 6291460
  46.4 4.3 %collective-permute-start.2 = (bf16[4096,256]{1,0:T(8,128)(2,1)S(1)}, bf16[4096,256]{1,0:T(8,128)(2,1)}, u32[]{:S(2)}, u32[]{:S(2)}) collective-permute-start(bf16[4096,256]{1,0:T(8,128)(2,1)S(1)} %bitcast.28), channel_id=1, source_target_pairs={{0,8},{1,9},{2,10},{3,11},{4,12},{5,13},{6,14},{7,15},{8,0},{9,1},... | collective-permute-start | bytes 6291464 | tf_op jit(solution)/shard_map/ppermute | solution.py:12
  57.4 4.9 %copy-start.1 = (f32[256,1024]{1,0:T(8,128)S(1)}, f32[256,1024]{1,0:T(8,128)}, u32[]{:S(2)}) copy-start(f32[256,1024]{1,0:T(8,128)} %param.9) | copy-start | bytes 3145732
  57.4 7.0 %slice-start = ((s8[10485760]{0:T(1024)(128)(4,1)}), s8[4194304]{0:T(1024)(128)(4,1)S(1)}, s32[]{:S(2)}) async-start(s8[10485760]{0:T(1024)(128)(4,1)} %bitcast.25), calls=%async_computation.1 | async-start | bytes 8388608
  57.4 7.0 %slice-start.1 = ((s8[10485760]{0:T(1024)(128)(4,1)}), s8[4194304]{0:T(1024)(128)(4,1)S(1)}, s32[]{:S(2)}) async-start(s8[10485760]{0:T(1024)(128)(4,1)} %bitcast.25), calls=%async_computation.2 | async-start | bytes 8388608
  62.3 2.1 %slice-start.2 = ((s8[10485760]{0:T(1024)(128)(4,1)}), s8[2097152]{0:T(1024)(128)(4,1)S(1)}, s32[]{:S(2)}) async-start(s8[10485760]{0:T(1024)(128)(4,1)} %bitcast.25), calls=%async_computation.3 | async-start | bytes 4194304

commit v5 on v4

--- a/solution.py
+++ b/solution.py
@@ -19,7 +19,8 @@
     group = lax.psum(1, ("rh", "cl"))
     spread = jnp.broadcast_to(buf[None], (group,) + buf.shape)
     buf = lax.all_to_all(spread, ("rh", "cl"), 0, 0, tiled=False).reshape(-1, buf.shape[1])
-    return jnp.concatenate([buf, swap(buf, n_col, n)], axis=0)
+    pair = jnp.broadcast_to(buf[None], (2,) + buf.shape)
+    return lax.all_to_all(pair, "core", 0, 0, tiled=False).reshape(-1, buf.shape[1])
 
 
 def position_of(j, me, n_col, col_masks, group):
@@ -29,8 +30,7 @@
     first = 1 << len(col_masks)
     row_idx, col_idx = j // n_col, j % n_col
     member = (row_idx // 2) * 2 + (col_idx % 2)
-    other_core = (row_idx % 2) != ((me // n_col) % 2)
-    return jnp.where(other_core, group * first, 0) + member * first + near
+    return (row_idx % 2) * (group * first) + member * first + near
 
 
 def shards(tiles, tile_list, tile_count, w_rows, h_cols, n_row, n_col):

time: 69.3 us -> 70.4 us (1.016)
  waiting for transfers between devices: 16.3 us -> 35.6 us
  blocking collectives: 27.2 us -> 8.18 us
  other arithmetic: 6.1 us -> 2.28 us
  starting transfers between devices: 4.89 us -> 8.63 us
  local copies, waits for them, and re-layouts: 3.24 us -> 5 us
  matrix products: 9.79 us -> 9.04 us
    all_to_all x0 -> x1, waiting for transfers between devices: none -> 22.6 us  [gather_rows(): lax.all_to_all(spread, ('rh', 'cl'), 0, 0, tiled=False)]
    all_to_all x1, blocking collectives: 27.2 us -> 8.18 us  [gather_rows(): lax.all_to_all(pair, 'core', 0, 0, tiled=False).reshape(-1, buf.shape[1])]
    concatenate x1 -> x0, other arithmetic: 3.82 us -> none  [gather_rows(): return jnp.concatenate([buf, swap(buf, n_col, n)], axis=0)]
    all_to_all x0 -> x1, starting transfers between devices: none -> 3.74 us  [gather_rows(): lax.all_to_all(spread, ('rh', 'cl'), 0, 0, tiled=False)]
    dot_general x1, matrix products: 4.89 us -> 1.28 us  [shards(): lax.dot_general(buf, buf, contract_rows, preferred_element_type=jnp.float32)]
    ppermute x3 -> x2, waiting for transfers between devices: 16.3 us -> 13.1 us  [swap(): return lax.ppermute(value, SUB, [(i, i ^ mask) for i in range(n)])]
    dot_general x1, matrix products: 3.87 us -> 5.75 us  [shards(): lax.dot_general(picked.reshape(slots * tile, rank_size), tiles.reshape(sl...]
    broadcast_in_dim x1, local copies, waits for them, and re-layouts: 0.14 us -> 1.49 us  [gather_rows(): spread = jnp.broadcast_to(buf[None], (group,) + buf.shape)]
where the time goes in v5:
time: 70.4 us; the launch traced here: 69.5 us
  waiting for transfers between devices  35.6 us (51%)
  matrix products  9.04 us (13%)
  starting transfers between devices  8.63 us (12%)
  blocking collectives  8.18 us (12%)
  local copies, waits for them, and re-layouts  5 us (7%)
  other arithmetic  2.28 us (3%)
  between operations  0.76 us (1%)
    all_to_all x1, waiting for transfers between devices, gather_rows(): lax.all_to_all(spread, ('rh', 'cl'), 0, 0, tiled=False)  22.6 us
    ppermute x2, waiting for transfers between devices, swap(): return lax.ppermute(value, SUB, [(i, i ^ mask) for i in range(n)])  13.1 us
    all_to_all x1, blocking collectives, gather_rows(): lax.all_to_all(pair, 'core', 0, 0, tiled=False).reshape(-1, buf.shape[1])  8.18 us
    dot_general x1, matrix products, shards(): lax.dot_general(picked.reshape(slots * tile, rank_size), tiles.reshape(sl...  5.75 us
    ppermute x2, starting transfers between devices, swap(): return lax.ppermute(value, SUB, [(i, i ^ mask) for i in range(n)])  4.89 us
    all_to_all x1, starting transfers between devices, gather_rows(): lax.all_to_all(spread, ('rh', 'cl'), 0, 0, tiled=False)  3.74 us
    gather x1, local copies, waits for them, and re-layouts, shards(): jnp.take(pieces, where.reshape(-1), axis=0).reshape(slots, tile, rank_size)  2.9 us
    dot_general x1, matrix products, shards(): jnp.dot(gram, h_cols, precision=lax.Precision.HIGHEST, preferred_element_...  2.02 us
  transfers between devices with their start and end apart: 3, of which 3 were waited for; matrix products, arithmetic and copies ran while one was open for 1% of the time, Pallas kernels for 0%

profile of v5, /device:TPU:0, one launch (start us, length us, event | category | flops | bytes accessed | tf_op | source)
XLA Modules:
  0.0 69.5 jit_solution(15312111281103018034)
XLA Ops:
  0.0 1.0 %convert_element_type.3 = bf16[256,256]{1,0:T(8,128)(2,1)S(1)} convert(f32[256,256]{1,0:T(8,128)} %param.8) | non-fusion elementwise | flops 65536 | bytes 393216 | tf_op jit(solution)/shard_map/convert_element_type | solution.py:42
  1.0 4.1 %collective-permute-start = (bf16[256,256]{1,0:T(8,128)(2,1)S(1)}, bf16[256,256]{1,0:T(8,128)(2,1)S(1)}, u32[]{:S(2)}, u32[]{:S(2)}) collective-permute-start(bf16[256,256]{1,0:T(8,128)(2,1)S(1)} %convert_element_type.3), channel_id=1, source_target_pairs={{0,4},{1,5},{2,6},{3,7},{4,0},{5,1},{6,2},{7,3},{8,12},{9,13},{10,... | collective-permute-start | bytes 393224 | tf_op jit(solution)/shard_map/ppermute | solution.py:12
  5.1 6.3 %collective-permute-done = bf16[256,256]{1,0:T(8,128)(2,1)S(1)} collective-permute-done((bf16[256,256]{1,0:T(8,128)(2,1)S(1)}, bf16[256,256]{1,0:T(8,128)(2,1)S(1)}, u32[]{:S(2)}, u32[]{:S(2)}) %collective-permute-start) | collective-permute-done | bytes 131104 | tf_op jit(solution)/shard_map/ppermute | solution.py:12
  11.4 0.8 %collective-permute-start.1 = (bf16[512,256]{1,0:T(8,128)(2,1)S(1)}, bf16[512,256]{1,0:T(8,128)(2,1)S(1)}, u32[]{:S(2)}, u32[]{:S(2)}) collective-permute-start(bf16[512,256]{1,0:T(8,128)(2,1)S(1)} %pad_maximum_fusion.1), channel_id=1, source_target_pairs={{0,2},{1,3},{2,0},{3,1},{4,6},{5,7},{6,4},{7,5},{8,10},{9,11},{10,... | collective-permute-start | bytes 786440 | tf_op jit(solution)/shard_map/ppermute | solution.py:12
  12.2 6.8 %collective-permute-done.1 = bf16[512,256]{1,0:T(8,128)(2,1)S(1)} collective-permute-done((bf16[512,256]{1,0:T(8,128)(2,1)S(1)}, bf16[512,256]{1,0:T(8,128)(2,1)S(1)}, u32[]{:S(2)}, u32[]{:S(2)}) %collective-permute-start.1) | collective-permute-done | bytes 262176 | tf_op jit(solution)/shard_map/ppermute | solution.py:12
  19.0 1.5 %broadcast_in_dim.51 = bf16[4,1024,256]{2,1,0:T(8,128)(2,1)} broadcast(bf16[1024,256]{1,0:T(8,128)(2,1)S(1)} %pad_maximum_fusion), dimensions={1,2} | broadcast | bytes 2621440 | tf_op jit(solution)/shard_map/broadcast_in_dim | solution.py:20
  20.5 0.0 copy-start.2
  20.5 3.7 %all-to-all-start = ((bf16[4,1024,256]{2,1,0:T(8,128)(2,1)}), bf16[4,1024,256]{2,1,0:T(8,128)(2,1)S(1)}, u32[]{:S(2)}, u32[]{:S(2)}) async-start(bf16[4,1024,256]{2,1,0:T(8,128)(2,1)} %broadcast_in_dim.51), calls=%async_computation | async-start | bytes 4194304 | tf_op jit(solution)/shard_map/all_to_all | solution.py:21
  24.9 0.0 copy-done.2
  24.9 0.1 iota_add_fusion
  25.0 0.1 add.207
  25.1 0.1 compare_and_fusion
  25.2 0.1 broadcast_bitcast_fusion
  25.3 22.6 %all-to-all-done = bf16[4,1024,256]{2,1,0:T(8,128)(2,1)S(1)} async-done(((bf16[4,1024,256]{2,1,0:T(8,128)(2,1)}), bf16[4,1024,256]{2,1,0:T(8,128)(2,1)S(1)}, u32[]{:S(2)}, u32[]{:S(2)}) %all-to-all-start) | async-done | bytes 2097184 | tf_op jit(solution)/shard_map/all_to_all | solution.py:21
  47.9 0.3 broadcast_in_dim.53
  48.1 8.2 %all_to_all.10 = bf16[2,4096,256]{2,1,0:T(8,128)(2,1)} all-to-all(bf16[2,4096,256]{2,1,0:T(8,128)(2,1)S(1)} %broadcast_in_dim.53), channel_id=1, replica_groups=mesh['rh'=2,'core'=2,'ch'=4,'cl'=2] {'core'}, dimensions={0} | all-to-all | bytes 8388608 | tf_op jit(solution)/shard_map/all_to_all | solution.py:23
  56.3 2.9 %gather_fusion = bf16[20,256,256]{2,1,0:T(8,128)(2,1)S(1)} fusion(bf16[32,256,256]{2,1,0:T(8,128)(2,1)} %bitcast.26, s32[1024]{0:T(1024)S(1)} %pad_clamp_fusion), kind=kCustom, calls=%fused_computation | custom fusion | bytes 5242960 | tf_op jit(solution)/shard_map/jit(_take)/gather | solution.py:52
  59.2 0.0 copy-start.1
  59.2 1.1 %fusion = bf16[5,1024,256]{2,1,0:T(8,128)(2,1)S(1)} fusion(pred[5]{0:T(512)(128)(4,1)S(1)} %iota_compare_fusion, pred[5,1024]{1,0:T(8,128)(4,1)S(1)} %bitcast.29, bf16[5,1024,256]{2,1,0:T(8,128)(2,1)S(1)} %bitcast.27), kind=kLoop, calls=%fused_computation.2 | loop fusion | flops 2621440 | bytes 5248005 | tf_op jit(solution)/shard_map/jit(_where)/select_n | solution.py:54
  60.3 0.2 copy-done.1
  60.5 0.0 copy-start
  60.5 5.7 %fusion.1 = f32[256,1024]{1,0:T(8,128)S(1)} fusion(f32[256,1024]{1,0:T(8,128)S(1)} %copy-done.1, bf16[5,1024,256]{2,1,0:T(8,128)(2,1)S(1)} %fusion, bf16[5,1024,1024]{2,1,0:T(8,128)(2,1)} %param.5), kind=kOutput, calls=%fused_computation.4 | convolution fusion | flops 2684616704 | bytes 15204352 | tf_op jit(solution)/shard_map/dot_general | solution.py:55
  66.2 0.0 copy-done
  66.2 1.3 %convolution_bitcast_fusion.1 = f32[256,256]{1,0:T(8,128)S(1)} fusion(bf16[2,4096,256]{2,1,0:T(8,128)(2,1)S(1)} %copy-done), kind=kOutput, calls=%fused_computation.6 | convolution fusion | flops 1073741824 | bytes 4456448 | tf_op jit(solution)/shard_map/dot_general | solution.py:44
  67.5 2.0 %convolution_divide_fusion = f32[256,1024]{1,0:T(8,128)} fusion(f32[256,1024]{1,0:T(8,128)S(1)} %fusion.1, f32[256,256]{1,0:T(8,128)S(1)} %convolution_bitcast_fusion.1, f32[256,1024]{1,0:T(8,128)S(1)} %copy-done.1), kind=kOutput, calls=%fused_computation.5 | convolution fusion | flops 805568512 | bytes 3407872 | tf_op jit(solution)/shard_map/dot_general | solution.py:61
  (7 shorter events, 0.1 us)
Async XLA Ops:
  1.0 10.4 %collective-permute-start = (bf16[256,256]{1,0:T(8,128)(2,1)S(1)}, bf16[256,256]{1,0:T(8,128)(2,1)S(1)}, u32[]{:S(2)}, u32[]{:S(2)}) collective-permute-start(bf16[256,256]{1,0:T(8,128)(2,1)S(1)} %convert_element_type.3), channel_id=1, source_target_pairs={{0,4},{1,5},{2,6},{3,7},{4,0},{5,1},{6,2},{7,3},{8,12},{9,13},{10,... | collective-permute-start | bytes 393224 | tf_op jit(solution)/shard_map/ppermute | solution.py:12
  11.4 7.6 %collective-permute-start.1 = (bf16[512,256]{1,0:T(8,128)(2,1)S(1)}, bf16[512,256]{1,0:T(8,128)(2,1)S(1)}, u32[]{:S(2)}, u32[]{:S(2)}) collective-permute-start(bf16[512,256]{1,0:T(8,128)(2,1)S(1)} %pad_maximum_fusion.1), channel_id=1, source_target_pairs={{0,2},{1,3},{2,0},{3,1},{4,6},{5,7},{6,4},{7,5},{8,10},{9,11},{10,... | collective-permute-start | bytes 786440 | tf_op jit(solution)/shard_map/ppermute | solution.py:12
  20.5 4.4 %copy-start.2 = (s32[5]{0:T(128)S(1)}, s32[5]{0:T(128)}, u32[]{:S(2)}) copy-start(s32[5]{0:T(128)} %param.6) | copy-start | bytes 64
  20.5 27.4 %all-to-all-start = ((bf16[4,1024,256]{2,1,0:T(8,128)(2,1)}), bf16[4,1024,256]{2,1,0:T(8,128)(2,1)S(1)}, u32[]{:S(2)}, u32[]{:S(2)}) async-start(bf16[4,1024,256]{2,1,0:T(8,128)(2,1)} %broadcast_in_dim.51), calls=%async_computation | async-start | bytes 4194304 | tf_op jit(solution)/shard_map/all_to_all | solution.py:21
  59.2 1.2 %copy-start.1 = (f32[256,1024]{1,0:T(8,128)S(1)}, f32[256,1024]{1,0:T(8,128)}, u32[]{:S(2)}) copy-start(f32[256,1024]{1,0:T(8,128)} %param.9) | copy-start | bytes 3145732
  60.5 5.8 %copy-start = (bf16[2,4096,256]{2,1,0:T(8,128)(2,1)S(1)}, bf16[2,4096,256]{2,1,0:T(8,128)(2,1)}, u32[]{:S(2)}) copy-start(bf16[2,4096,256]{2,1,0:T(8,128)(2,1)} %all_to_all.10) | copy-start | bytes 12582916

commit v6 on v4

--- a/solution.py
+++ b/solution.py
@@ -19,7 +19,7 @@
     group = lax.psum(1, ("rh", "cl"))
     spread = jnp.broadcast_to(buf[None], (group,) + buf.shape)
     buf = lax.all_to_all(spread, ("rh", "cl"), 0, 0, tiled=False).reshape(-1, buf.shape[1])
-    return jnp.concatenate([buf, swap(buf, n_col, n)], axis=0)
+    return buf, swap(buf, n_col, n)
 
 
 def position_of(j, me, n_col, col_masks, group):
@@ -40,16 +40,20 @@
     share = w_rows.shape[0]
     col_masks = [2 << b for b in range(n_col.bit_length() - 2)][::-1]
     w_half = w_rows.astype(jnp.bfloat16)
-    buf = gather_rows(w_half, n, n_col, col_masks)
-    gram = lax.dot_general(buf, buf, contract_rows, preferred_element_type=jnp.float32)
+    mine, theirs = gather_rows(w_half, n, n_col, col_masks)
+    gram = lax.dot_general(mine, mine, contract_rows, preferred_element_type=jnp.float32)
+    gram = gram + lax.dot_general(theirs, theirs, contract_rows, preferred_element_type=jnp.float32)
     me = lax.axis_index(SUB)
     per_block = tile // share
     blocks_total = n // per_block
     rows_of = jnp.clip(tile_list, 0, blocks_total - 1)
     owners = rows_of[:, None] * per_block + jnp.arange(per_block, dtype=jnp.int32)[None, :]
     where = position_of(owners, me, n_col, col_masks, 2 * (n_row // 2))
-    pieces = buf.reshape(n, share, rank_size)
-    picked = jnp.take(pieces, where.reshape(-1), axis=0).reshape(slots, tile, rank_size)
+    half = n // 2
+    where = where.reshape(-1)
+    near = jnp.take(mine.reshape(half, share, rank_size), where % half, axis=0)
+    far = jnp.take(theirs.reshape(half, share, rank_size), where % half, axis=0)
+    picked = jnp.where((where >= half)[:, None, None], far, near).reshape(slots, tile, rank_size)
     live = jnp.arange(slots, dtype=jnp.int32) < tile_count[0]
     picked = jnp.where(live[:, None, None], picked, jnp.zeros_like(picked))
     numerator = lax.dot_general(

time: 69.3 us -> 66.5 us (0.960)
  local copies, waits for them, and re-layouts: 3.24 us -> 6.75 us
  waiting for transfers between devices: 16.3 us -> 13.3 us
  other arithmetic: 6.1 us -> 3.75 us
  matrix products: 9.79 us -> 8.77 us
    concatenate x1 -> x0, other arithmetic: 3.82 us -> none  [gather_rows(): return jnp.concatenate([buf, swap(buf, n_col, n)], axis=0)]
    gather x1 -> x2, local copies, waits for them, and re-layouts: 2.9 us -> 6.5 us  [the longest x1 4.12 us: shards(): far = jnp.take(theirs.reshape(half, share, rank_size), where % half, axis=0)]
    ppermute x3, waiting for transfers between devices: 16.3 us -> 13.3 us  [swap(): return lax.ppermute(value, SUB, [(i, i ^ mask) for i in range(n)])]
    select_n x1, other arithmetic: 0.03 us -> 2.36 us  [shards(): jnp.where((where >= half)[:, None, None], far, near)]
    dot_general x1 -> x2, matrix products: 4.89 us -> 3.85 us  [the longest x1 3.12 us: shards(): lax.dot_general(theirs, theirs, contract_rows, preferred_element_type=jnp...]
    select_n x1, other arithmetic: 1.05 us -> 0.24 us  [shards(): picked = jnp.where(live[:, None, None], picked, jnp.zeros_like(picked))]
  transfers between devices with their start and end apart: 3 -> 3, of which waited for: 3 -> 3; matrix products, arithmetic and copies ran while one was open for 1% -> 5% of each run, Pallas kernels for 0% -> 0%
where the time goes in v6:
time: 66.5 us; the launch traced here: 65.5 us
  blocking collectives  27.2 us (41%)
  waiting for transfers between devices  13.3 us (20%)
  matrix products  8.77 us (13%)
  local copies, waits for them, and re-layouts  6.75 us (10%)
  starting transfers between devices  4.89 us (7%)
  other arithmetic  3.75 us (6%)
  between operations  0.8 us (1%)
    all_to_all x1, blocking collectives, gather_rows(): lax.all_to_all(spread, ('rh', 'cl'), 0, 0, tiled=False)  27.2 us
    ppermute x3, waiting for transfers between devices, swap(): return lax.ppermute(value, SUB, [(i, i ^ mask) for i in range(n)])  13.3 us
    ppermute x3, starting transfers between devices, swap(): return lax.ppermute(value, SUB, [(i, i ^ mask) for i in range(n)])  4.89 us
    gather x1, local copies, waits for them, and re-layouts, shards(): far = jnp.take(theirs.reshape(half, share, rank_size), where % half, axis=0)  4.12 us
    dot_general x1, matrix products, shards(): lax.dot_general(picked.reshape(slots * tile, rank_size), tiles.reshape(sl...  3.88 us
    dot_general x1, matrix products, shards(): lax.dot_general(theirs, theirs, contract_rows, preferred_element_type=jnp...  3.12 us
    gather x1, local copies, waits for them, and re-layouts, shards(): near = jnp.take(mine.reshape(half, share, rank_size), where % half, axis=0)  2.38 us
    select_n x1, other arithmetic, shards(): jnp.where((where >= half)[:, None, None], far, near)  2.36 us
  transfers between devices with their start and end apart: 3, of which 3 were waited for; matrix products, arithmetic and copies ran while one was open for 5% of the time, Pallas kernels for 0%

profile of v6, /device:TPU:0, one launch (start us, length us, event | category | flops | bytes accessed | tf_op | source)
XLA Modules:
  0.0 65.5 jit_solution(1819586990080582898)
XLA Ops:
  0.0 1.0 %convert_element_type.3 = bf16[256,256]{1,0:T(8,128)(2,1)S(1)} convert(f32[256,256]{1,0:T(8,128)} %param.10) | non-fusion elementwise | flops 65536 | bytes 393216 | tf_op jit(solution)/shard_map/convert_element_type | solution.py:42
  1.0 4.1 %collective-permute-start = (bf16[256,256]{1,0:T(8,128)(2,1)S(1)}, bf16[256,256]{1,0:T(8,128)(2,1)S(1)}, u32[]{:S(2)}, u32[]{:S(2)}) collective-permute-start(bf16[256,256]{1,0:T(8,128)(2,1)S(1)} %convert_element_type.3), channel_id=1, source_target_pairs={{0,4},{1,5},{2,6},{3,7},{4,0},{5,1},{6,2},{7,3},{8,12},{9,13},{10,... | collective-permute-start | bytes 393224 | tf_op jit(solution)/shard_map/ppermute | solution.py:12
  5.1 6.3 %collective-permute-done = bf16[256,256]{1,0:T(8,128)(2,1)S(1)} collective-permute-done((bf16[256,256]{1,0:T(8,128)(2,1)S(1)}, bf16[256,256]{1,0:T(8,128)(2,1)S(1)}, u32[]{:S(2)}, u32[]{:S(2)}) %collective-permute-start) | collective-permute-done | bytes 131104 | tf_op jit(solution)/shard_map/ppermute | solution.py:12
  11.4 0.8 %collective-permute-start.1 = (bf16[512,256]{1,0:T(8,128)(2,1)S(1)}, bf16[512,256]{1,0:T(8,128)(2,1)S(1)}, u32[]{:S(2)}, u32[]{:S(2)}) collective-permute-start(bf16[512,256]{1,0:T(8,128)(2,1)S(1)} %pad_maximum_fusion.1), channel_id=1, source_target_pairs={{0,2},{1,3},{2,0},{3,1},{4,6},{5,7},{6,4},{7,5},{8,10},{9,11},{10,... | collective-permute-start | bytes 786440 | tf_op jit(solution)/shard_map/ppermute | solution.py:12
  12.2 6.8 %collective-permute-done.1 = bf16[512,256]{1,0:T(8,128)(2,1)S(1)} collective-permute-done((bf16[512,256]{1,0:T(8,128)(2,1)S(1)}, bf16[512,256]{1,0:T(8,128)(2,1)S(1)}, u32[]{:S(2)}, u32[]{:S(2)}) %collective-permute-start.1) | collective-permute-done | bytes 262176 | tf_op jit(solution)/shard_map/ppermute | solution.py:12
  19.0 0.1 broadcast_in_dim.51
  19.1 0.0 copy-start.2
  19.2 27.2 %all_to_all.5 = bf16[4,1024,256]{2,1,0:T(8,128)(2,1)S(1)} all-to-all(bf16[4,1024,256]{2,1,0:T(8,128)(2,1)S(1)} %broadcast_in_dim.51), channel_id=1, replica_groups=mesh['rh'=2,'core'=2,'ch'=4,'cl'=2] {'rh','cl'}, dimensions={0} | all-to-all | bytes 4194304 | tf_op jit(solution)/shard_map/all_to_all | solution.py:21
  46.4 0.0 collective-permute-start.2
  47.0 0.0 copy-done.2
  47.0 0.1 iota_add_fusion
  47.1 0.1 add.125
  47.3 2.4 %gather_fusion.1 = bf16[20,256,256]{2,1,0:T(8,128)(2,1)} fusion(bf16[16,256,256]{2,1,0:T(8,128)(2,1)S(1)} %bitcast.25, s32[1024]{0:T(1024)S(1)} %pad_clamp_fusion), kind=kCustom, calls=%fused_computation.1.clone | custom fusion | bytes 5242960 | tf_op jit(solution)/shard_map/jit(_take)/gather | solution.py:54
  49.6 0.7 %convolution_bitcast_fusion.1 = f32[256,256]{1,0:T(8,128)S(1)} fusion(bf16[4,1024,256]{2,1,0:T(8,128)(2,1)S(1)} %all_to_all.5), kind=kOutput, calls=%fused_computation.8 | convolution fusion | flops 536870912 | bytes 2359296 | tf_op jit(solution)/shard_map/dot_general | solution.py:44
  50.4 0.3 collective-permute-done.2
  50.6 0.0 copy-start
  50.6 4.1 %gather_fusion = bf16[20,256,256]{2,1,0:T(8,128)(2,1)} fusion(bf16[16,256,256]{2,1,0:T(8,128)(2,1)} %bitcast.2, s32[1024]{0:T(1024)S(1)} %pad_clamp_fusion), kind=kCustom, calls=%fused_computation.clone | custom fusion | bytes 5242960 | tf_op jit(solution)/shard_map/jit(_take)/gather | solution.py:55
  54.8 0.0 copy-done
  54.8 0.0 slice-start
  54.8 0.0 slice-start.1
  54.8 2.4 %select_select_fusion = bf16[20,256,256]{2,1,0:T(8,128)(2,1)S(1)} fusion(bf16[20,256,256]{2,1,0:T(8,128)(2,1)S(1)} %copy-done, bf16[20,256,256]{2,1,0:T(8,128)(2,1)} %gather_fusion, pred[20]{0:T(512)(128)(4,1)S(1)} %get-tuple-element.8, pred[20]{0:T(512)(128)(4,1)S(1)} %get-tuple-element.6), kind=kLoop, calls=%fused_computation.3 | loop fusion | flops 3932160 | bytes 7864360 | tf_op jit(solution)/shard_map/jit(_where)/select_n | solution.py:56
  57.1 0.2 bitcast_select_fusion
  57.4 0.0 copy-start.1
  57.4 0.0 slice-start.2
  57.4 3.1 %convolution_add_fusion = f32[256,256]{1,0:T(8,128)S(1)} fusion(f32[256,256]{1,0:T(8,128)S(1)} %convolution_bitcast_fusion.1, bf16[4096,256]{1,0:T(8,128)(2,1)} %collective-permute-done.2), kind=kOutput, calls=%fused_computation.7 | convolution fusion | flops 536936448 | bytes 2621440 | tf_op jit(solution)/shard_map/dot_general | solution.py:45
  60.5 0.0 copy-done.1
  60.5 1.0 %fusion.9 = f32[256,1024]{1,0:T(8,128)S(1)} fusion(f32[256,256]{1,0:T(8,128)S(1)} %convolution_add_fusion, f32[256,1024]{1,0:T(8,128)S(1)} %copy-done.1), kind=kOutput, calls=%fused_computation.43 | convolution fusion | flops 805306368 | bytes 2359296 | tf_op jit(solution)/shard_map/dot_general | solution.py:65
  61.6 0.0 slice-done
  61.6 0.0 slice-done.1
  61.6 0.0 slice-done.2
  61.6 3.9 %fusion.1 = f32[256,1024]{1,0:T(8,128)} fusion(f32[256,1024]{1,0:T(8,128)S(1)} %fusion.9, f32[256,1024]{1,0:T(8,128)S(1)} %copy-done.1, bf16[5,1024,256]{2,1,0:T(8,128)(2,1)S(1)} %bitcast_select_fusion, bf16[5,1024,1024]{2,1,0:T(8,128)(2,1)S(1)} %bitcast.28), kind=kOutput, calls=%fused_computation.6 | convolution fusion | flops 2684878848 | bytes 16252928 | tf_op jit(solution)/shard_map/dot_general | solution.py:59
  (8 shorter events, 0.1 us)
Async XLA Ops:
  1.0 10.4 %collective-permute-start = (bf16[256,256]{1,0:T(8,128)(2,1)S(1)}, bf16[256,256]{1,0:T(8,128)(2,1)S(1)}, u32[]{:S(2)}, u32[]{:S(2)}) collective-permute-start(bf16[256,256]{1,0:T(8,128)(2,1)S(1)} %convert_element_type.3), channel_id=1, source_target_pairs={{0,4},{1,5},{2,6},{3,7},{4,0},{5,1},{6,2},{7,3},{8,12},{9,13},{10,... | collective-permute-start | bytes 393224 | tf_op jit(solution)/shard_map/ppermute | solution.py:12
  11.4 7.6 %collective-permute-start.1 = (bf16[512,256]{1,0:T(8,128)(2,1)S(1)}, bf16[512,256]{1,0:T(8,128)(2,1)S(1)}, u32[]{:S(2)}, u32[]{:S(2)}) collective-permute-start(bf16[512,256]{1,0:T(8,128)(2,1)S(1)} %pad_maximum_fusion.1), channel_id=1, source_target_pairs={{0,2},{1,3},{2,0},{3,1},{4,6},{5,7},{6,4},{7,5},{8,10},{9,11},{10,... | collective-permute-start | bytes 786440 | tf_op jit(solution)/shard_map/ppermute | solution.py:12
  19.1 27.9 %copy-start.2 = (s32[5]{0:T(128)S(1)}, s32[5]{0:T(128)}, u32[]{:S(2)}) copy-start(s32[5]{0:T(128)} %param.8) | copy-start | bytes 64
  46.4 4.3 %collective-permute-start.2 = (bf16[4096,256]{1,0:T(8,128)(2,1)S(1)}, bf16[4096,256]{1,0:T(8,128)(2,1)}, u32[]{:S(2)}, u32[]{:S(2)}) collective-permute-start(bf16[4096,256]{1,0:T(8,128)(2,1)S(1)} %bitcast.24), channel_id=1, source_target_pairs={{0,8},{1,9},{2,10},{3,11},{4,12},{5,13},{6,14},{7,15},{8,0},{9,1},... | collective-permute-start | bytes 6291464 | tf_op jit(solution)/shard_map/ppermute | solution.py:12
  50.6 4.1 %copy-start = (bf16[20,256,256]{2,1,0:T(8,128)(2,1)S(1)}, bf16[20,256,256]{2,1,0:T(8,128)(2,1)}, u32[]{:S(2)}) copy-start(bf16[20,256,256]{2,1,0:T(8,128)(2,1)} %gather_fusion.1) | copy-start | bytes 7864324
  54.8 6.8 %slice-start = ((s8[10485760]{0:T(1024)(128)(4,1)}), s8[2097152]{0:T(1024)(128)(4,1)S(1)}, s32[]{:S(2)}) async-start(s8[10485760]{0:T(1024)(128)(4,1)} %bitcast.27), calls=%async_computation.1 | async-start | bytes 4194304
  54.8 6.8 %slice-start.1 = ((s8[10485760]{0:T(1024)(128)(4,1)}), s8[4194304]{0:T(1024)(128)(4,1)S(1)}, s32[]{:S(2)}) async-start(s8[10485760]{0:T(1024)(128)(4,1)} %bitcast.27), calls=%async_computation.2 | async-start | bytes 8388608
  57.4 3.2 %copy-start.1 = (f32[256,1024]{1,0:T(8,128)S(1)}, f32[256,1024]{1,0:T(8,128)}, u32[]{:S(2)}) copy-start(f32[256,1024]{1,0:T(8,128)} %param.11) | copy-start | bytes 3145732
  57.4 4.2 %slice-start.2 = ((s8[10485760]{0:T(1024)(128)(4,1)}), s8[4194304]{0:T(1024)(128)(4,1)S(1)}, s32[]{:S(2)}) async-start(s8[10485760]{0:T(1024)(128)(4,1)} %bitcast.27), calls=%async_computation.3 | async-start | bytes 8388608

commit v7 on v5

v7 whole, which is shorter than its diff:
```python
import jax
import jax.numpy as jnp
from jax import lax
from jax.sharding import Mesh
from jax.sharding import PartitionSpec as P

contract_rows = (((0,), (0,)), ((), ()))
SUB = ("rh", "core", "ch", "cl")


def swap(value, mask, n):
    return lax.ppermute(value, SUB, [(i, i ^ mask) for i in range(n)])


def gather_rows(w_half, me, n, n_col, col_masks):
    buf = w_half[None]
    for mask in col_masks:
        moved = swap(buf, mask, n)
        upper = (me & mask) != 0
        pair = jnp.where(upper, jnp.stack([moved, buf], axis=1), jnp.stack([buf, moved], axis=1))
        buf = pair.reshape((-1,) + w_half.shape)
    group = lax.psum(1, ("rh", "cl"))
    spread = jnp.broadcast_to(buf[None], (group,) + buf.shape)
    mine = lax.all_to_all(spread, ("rh", "cl"), 0, 1, tiled=False)
    mine = mine.reshape((buf.shape[0], group // 2, 2) + w_half.shape)
    return mine, swap(mine, n_col, n)


def shards(tiles, tile_list, tile_count, w_rows, h_cols, n_row, n_col):
    slots, tile = tiles.shape[0], tiles.shape[1]
    rank_size = h_cols.shape[0]
    n = n_row * n_col
    share = w_rows.shape[0]
    col_masks = [2 << b for b in range(n_col.bit_length() - 2)][::-1]
    me = lax.axis_index(SUB)
    w_half = w_rows.astype(jnp.bfloat16)
    mine, theirs = gather_rows(w_half, me, n, n_col, col_masks)
    flat_mine = mine.reshape(-1, rank_size)
    flat_theirs = theirs.reshape(-1, rank_size)
    gram = lax.dot_general(flat_mine, flat_mine, contract_rows, preferred_element_type=jnp.float32)
    gram = gram + lax.dot_general(flat_theirs, flat_theirs, contract_rows, preferred_element_type=jnp.float32)

    per_block = tile // share
    blocks_total = n // per_block
    first = jnp.clip(tile_list, 0, blocks_total - 1) * per_block
    row_idx, col_idx = first // n_col, first % n_col
    same_core = (row_idx % 2) == ((me // n_col) % 2)
    live = jnp.arange(slots, dtype=jnp.int32) < tile_count[0]
    picked = []
    for s in range(slots):
        start = (col_idx[s] // 2, row_idx[s] // 2, 0, 0, 0)
        size = (per_block // 2, 1, 2, share, rank_size)
        near = lax.dynamic_slice(mine, start, size)
        far = lax.dynamic_slice(theirs, start, size)
        block = jnp.where(same_core[s], near, far).reshape(tile, rank_size)
        picked.append(jnp.where(live[s], block, jnp.zeros_like(block)))
    picked = jnp.stack(picked)
    numerator = lax.dot_general(
        picked.reshape(slots * tile, rank_size),
        tiles.reshape(slots * tile, tiles.shape[2]),
        contract_rows,
        preferred_element_type=jnp.float32,
    )
    denominator = jnp.dot(
        gram, h_cols, precision=lax.Precision.HIGHEST, preferred_element_type=jnp.float32
    )
    return h_cols * numerator / denominator


def solution(mesh):
    n_row, n_col = mesh.shape["row"], mesh.shape["col"]
    sub = Mesh(mesh.devices.reshape(n_row // 2, 2, n_col // 2, 2), SUB)
    placed = (
        P(SUB, None, None),
        P(SUB),
        P(SUB),
        P(SUB, None),
        P(None, SUB),
    )

    def body(tiles, tile_list, tile_count, w_rows, h_cols):
        return shards(tiles, tile_list, tile_count, w_rows, h_cols, n_row, n_col)

    return jax.shard_map(
        body, mesh=sub, in_specs=placed, out_specs=P(None, SUB), check_vma=False
    )
```

time: 70.4 us -> 113 us (1.61); the launches traced: 69.5 us -> 111 us
  between operations: 0.76 us -> 25.7 us
  waiting for transfers between devices: 35.6 us -> 13 us
  blocking collectives: 8.18 us -> 27.2 us
  local copies, waits for them, and re-layouts: 5 us -> 16.5 us
  other arithmetic: 2.28 us -> 12 us
  starting transfers between devices: 8.63 us -> 4.89 us
  matrix products: 9.04 us -> 11.3 us
    all_to_all x1 -> x0, waiting for transfers between devices: 22.6 us -> none  [gather_rows(): lax.all_to_all(spread, ('rh', 'cl'), 0, 0, tiled=False)]
    all_to_all x1, blocking collectives: 8.18 us -> 27.2 us  [gather_rows(): mine = lax.all_to_all(spread, ('rh', 'cl'), 0, 1, tiled=False)]
    select_n x2 -> x6, other arithmetic: 1.08 us -> 11 us  [the longest x2 10.9 us: shards(): picked.append(jnp.where(live[s], block, jnp.zeros_like(block)))]
    select_n x0 -> x5, local copies, waits for them, and re-layouts: none -> 8.15 us  [shards(): picked.append(jnp.where(live[s], block, jnp.zeros_like(block)))]
    all_to_all x1 -> x0, starting transfers between devices: 3.74 us -> none  [gather_rows(): lax.all_to_all(spread, ('rh', 'cl'), 0, 0, tiled=False)]
    unnamed x8 -> x14, local copies, waits for them, and re-layouts: 0.26 us -> 3.7 us
    gather x1 -> x0, local copies, waits for them, and re-layouts: 2.9 us -> none  [shards(): jnp.take(pieces, where.reshape(-1), axis=0).reshape(slots, tile, rank_size)]
    slice x0 -> x4, local copies, waits for them, and re-layouts: none -> 2.71 us  [the longest x2 1.35 us: shards(): start = (col_idx[s] // 2, row_idx[s] // 2, 0, 0, 0)]
  transfers between devices with their start and end apart: 3 -> 3, of which waited for: 3 -> 2; matrix products, arithmetic and copies ran while one was open for 1% -> 5% of each run, Pallas kernels for 0% -> 0%
where the time goes in v7:
time: 113 us; the launch traced here: 111 us
  blocking collectives  27.2 us (24%)
  between operations  25.7 us (23%)
  local copies, waits for them, and re-layouts  16.5 us (15%)
  waiting for transfers between devices  13 us (12%)
  other arithmetic  12 us (11%)
  matrix products  11.3 us (10%)
  starting transfers between devices  4.89 us (4%)
    all_to_all x1, blocking collectives, gather_rows(): mine = lax.all_to_all(spread, ('rh', 'cl'), 0, 1, tiled=False)  27.2 us
    ppermute x3, waiting for transfers between devices, swap(): return lax.ppermute(value, SUB, [(i, i ^ mask) for i in range(n)])  13 us
    select_n x2, other arithmetic, shards(): picked.append(jnp.where(live[s], block, jnp.zeros_like(block)))  10.9 us
    select_n x5, local copies, waits for them, and re-layouts, shards(): picked.append(jnp.where(live[s], block, jnp.zeros_like(block)))  8.15 us
    dot_general x1, matrix products, shards(): lax.dot_general(picked.reshape(slots * tile, rank_size), tiles.reshape(sl...  5.61 us
    ppermute x3, starting transfers between devices, swap(): return lax.ppermute(value, SUB, [(i, i ^ mask) for i in range(n)])  4.89 us
    unnamed x14, local copies, waits for them, and re-layouts  3.7 us
    dot_general x1, matrix products, shards(): lax.dot_general(flat_mine, flat_mine, contract_rows, preferred_element_ty...  2.96 us
  transfers between devices with their start and end apart: 3, of which 2 were waited for; matrix products, arithmetic and copies ran while one was open for 5% of the time, Pallas kernels for 0%

profile of v7, /device:TPU:0, one launch (start us, length us, event | category | flops | bytes accessed | tf_op | source)
XLA Modules:
  0.0 110.6 jit_solution(8732077117037004692)
XLA Ops:
  0.0 1.0 convert_bitcast_fusion.1
  1.0 4.1 %collective-permute-start = (bf16[1,256,256]{2,1,0:T(8,128)(2,1)S(1)}, bf16[1,256,256]{2,1,0:T(8,128)(2,1)S(1)}, u32[]{:S(2)}, u32[]{:S(2)}) collective-permute-start(bf16[1,256,256]{2,1,0:T(8,128)(2,1)S(1)} %get-tuple-element.12), channel_id=1, source_target_pairs={{0,4},{1,5},{2,6},{3,7},{4,0},{5,1},{6,2},{7,3},{8,12},{9,13},{10,... | collective-permute-start | bytes 393224 | tf_op jit(solution)/shard_map/ppermute | solution.py:12
  5.1 6.3 %collective-permute-done = bf16[1,256,256]{2,1,0:T(8,128)(2,1)S(1)} collective-permute-done((bf16[1,256,256]{2,1,0:T(8,128)(2,1)S(1)}, bf16[1,256,256]{2,1,0:T(8,128)(2,1)S(1)}, u32[]{:S(2)}, u32[]{:S(2)}) %collective-permute-start) | collective-permute-done | bytes 131104 | tf_op jit(solution)/shard_map/ppermute | solution.py:12
  11.4 0.8 collective-permute-start.1
  12.2 6.7 %collective-permute-done.1 = bf16[2,256,256]{2,1,0:T(8,128)(2,1)S(1)} collective-permute-done((bf16[2,256,256]{2,1,0:T(8,128)(2,1)S(1)}, bf16[2,256,256]{2,1,0:T(8,128)(2,1)S(1)}, u32[]{:S(2)}, u32[]{:S(2)}) %collective-permute-start.1) | collective-permute-done | bytes 262176 | tf_op jit(solution)/shard_map/ppermute | solution.py:12
  19.0 0.2 broadcast_in_dim_broadcast_in_dim.2
  19.2 27.2 %all_to_all.15 = bf16[4,4,1,256,256]{4,3,1,2,0:T(8,128)(2,1)S(1)} all-to-all(bf16[4,4,1,256,256]{4,3,1,2,0:T(8,128)(2,1)S(1)} %broadcast_in_dim_broadcast_in_dim.2), channel_id=1, replica_groups=mesh['rh'=2,'core'=2,'ch'=4,'cl'=2] {'rh','cl'}, dimensions={0} | all-to-all | bytes 4194304 | tf_op jit(solution)/shard_map/all_to_all | solution.py:24
  46.4 0.0 copy-start
  46.4 0.0 copy-start.3
  46.4 1.7 %copy.11 = bf16[4,4,1,256,256]{4,3,0,1,2:T(8,128)(2,1)} copy(bf16[4,4,1,256,256]{4,3,1,2,0:T(8,128)(2,1)S(1)} %all_to_all.15) | data formatting | bytes 4194304 | tf_op jit(solution)/shard_map/all_to_all | solution.py:24
  48.1 0.3 copy-done
  48.4 0.0 collective-permute-start.2
  48.4 0.0 copy-done.3
  48.4 0.7 fusion.16
  61.5 0.7 fusion.15
  75.4 0.7 fusion.14
  76.0 0.7 fusion.13
  76.7 3.0 %fusion.4 = f32[256,256]{1,0:T(8,128)S(1)} fusion(bf16[4,4,1,256,256]{4,3,1,2,0:T(8,128)(2,1)} %copy-done), kind=kOutput, calls=%fused_computation.6 | convolution fusion | flops 536870912 | bytes 2359296 | tf_op jit(solution)/shard_map/dot_general | solution.py:40
  79.7 0.0 collective-permute-done.2
  79.7 7.8 %select_select_fusion = (bf16[2,1,2,256,256]{4,3,2,1,0:T(8,128)(2,1)}, bf16[2,1,2,256,256]{4,3,2,1,0:T(8,128)(2,1)}, bf16[2,1,2,256,256]{4,3,2,1,0:T(8,128)(2,1)S(1)}, bf16[2,1,2,256,256]{4,3,2,1,0:T(8,128)(2,1)S(1)}) fusion(bf16[4,2,2,256,256]{4,3,2,1,0:T(8,128)(2,1)S(1)} %collective-permute-done.2, s32[]{:T(128)S(6)} %select_n.297, s32[]{:T(128)S(6)} %select_n.299, ...), kind=kLoop, calls=%fused_computation.10 | loop fusion | flops 2097152 | bytes 6291496 | tf_op jit(solution)/shard_map/jit(_where)/select_n | solution.py:56
  87.5 2.0 %copy.27 = bf16[1,1024,256]{1,2,0:T(8,128)(2,1)} copy(bf16[1,1024,256]{2,1,0:T(8,128)(2,1)} %bitcast.72) | data formatting | bytes 1048576 | tf_op jit(solution)/shard_map/jit(_where)/select_n | solution.py:56
  89.6 2.1 %copy.26 = bf16[1,1024,256]{1,2,0:T(8,128)(2,1)} copy(bf16[1,1024,256]{2,1,0:T(8,128)(2,1)} %bitcast.71) | data formatting | bytes 1048576 | tf_op jit(solution)/shard_map/jit(_where)/select_n | solution.py:56
  91.6 3.0 %select_select_fusion.4 = bf16[2,1,2,256,256]{4,3,2,1,0:T(8,128)(2,1)} fusion(bf16[4,2,2,256,256]{4,3,2,1,0:T(8,128)(2,1)S(1)} %collective-permute-done.2, s32[]{:T(128)S(6)} %select_n.261, s32[]{:T(128)S(6)} %select_n.263, bf16[4,2,2,256,256]{4,3,2,1,0:T(8,128)(2,1)} %bitcast.10, pred[]{:T(512)} %bitcast.2, pred[]{:T(512)} %bitcast.1), kind=kLoop, calls=%fused_computation.14 | loop fusion | flops 524288 | bytes 1572874 | tf_op jit(solution)/shard_map/jit(_where)/select_n | solution.py:56
  94.7 2.0 %copy.23 = bf16[1,1024,256]{1,2,0:T(8,128)(2,1)} copy(bf16[1,1024,256]{2,1,0:T(8,128)(2,1)} %bitcast.74) | data formatting | bytes 1048576 | tf_op jit(solution)/shard_map/jit(_where)/select_n | solution.py:56
  96.7 1.0 copy.25
  97.7 0.0 copy-start.1
  97.7 1.0 copy.24
  98.7 0.0 copy-start.2
  98.7 0.0 copy-start.4
  98.7 1.2 %constant_dynamic-update-slice_fusion.4 = bf16[5,1024,256]{1,2,0:T(8,128)(2,1)S(1)} fusion(bf16[1,1024,256]{1,2,0:T(8,128)(2,1)} %copy.23), kind=kLoop, calls=%fused_computation.23 | loop fusion | bytes 1048576
  99.9 1.1 constant_dynamic-update-slice_fusion.3
  101.0 1.1 constant_dynamic-update-slice_fusion.2
  102.1 0.0 copy-done.2
  102.1 0.0 copy-done.1
  102.2 0.0 copy-done.4
  102.2 5.6 %fusion.3 = f32[256,1024]{1,0:T(8,128)S(1)} fusion(f32[256,1024]{1,0:T(8,128)S(1)} %copy-done.4, bf16[5,1024,256]{1,2,0:T(8,128)(2,1)S(1)} %constant_dynamic-update-slice_fusion, bf16[5,1024,1024]{2,1,0:T(8,128)(2,1)} %param.5), kind=kOutput, calls=%fused_computation.4 | convolution fusion | flops 2684616704 | bytes 15204352 | tf_op jit(solution)/shard_map/dot_general | solution.py:58
  107.8 0.7 fusion.9
  108.6 2.0 %convolution_divide_fusion = f32[256,1024]{1,0:T(8,128)} fusion(f32[256,1024]{1,0:T(8,128)S(1)} %fusion.3, f32[256,256]{1,0:T(8,128)S(1)} %fusion.9, f32[256,1024]{1,0:T(8,128)S(1)} %copy-done.4), kind=kOutput, calls=%fused_computation.5 | convolution fusion | flops 805568512 | bytes 3407872 | tf_op jit(solution)/shard_map/dot_general | solution.py:64
  (8 shorter events, 0.2 us)
Async XLA Ops:
  1.0 10.4 %collective-permute-start = (bf16[1,256,256]{2,1,0:T(8,128)(2,1)S(1)}, bf16[1,256,256]{2,1,0:T(8,128)(2,1)S(1)}, u32[]{:S(2)}, u32[]{:S(2)}) collective-permute-start(bf16[1,256,256]{2,1,0:T(8,128)(2,1)S(1)} %get-tuple-element.12), channel_id=1, source_target_pairs={{0,4},{1,5},{2,6},{3,7},{4,0},{5,1},{6,2},{7,3},{8,12},{9,13},{10,... | collective-permute-start | bytes 393224 | tf_op jit(solution)/shard_map/ppermute | solution.py:12
  11.4 7.6 %collective-permute-start.1 = (bf16[2,256,256]{2,1,0:T(8,128)(2,1)S(1)}, bf16[2,256,256]{2,1,0:T(8,128)(2,1)S(1)}, u32[]{:S(2)}, u32[]{:S(2)}) collective-permute-start(bf16[2,256,256]{2,1,0:T(8,128)(2,1)S(1)} %maximum_select_fusion.1), channel_id=1, source_target_pairs={{0,2},{1,3},{2,0},{3,1},{4,6},{5,7},{6,4},{7,5},{8,10},{9,11},{10,... | collective-permute-start | bytes 786440 | tf_op jit(solution)/shard_map/ppermute | solution.py:12
  46.4 2.0 %copy-start = (bf16[4,4,1,256,256]{4,3,1,2,0:T(8,128)(2,1)}, bf16[4,4,1,256,256]{4,3,1,2,0:T(8,128)(2,1)S(1)}, u32[]{:S(2)}) copy-start(bf16[4,4,1,256,256]{4,3,1,2,0:T(8,128)(2,1)S(1)} %all_to_all.15) | copy-start | bytes 6291460
  46.4 2.0 %copy-start.3 = (s32[5]{0:T(128)S(1)}, s32[5]{0:T(128)}, u32[]{:S(2)}) copy-start(s32[5]{0:T(128)} %param.6) | copy-start | bytes 64
  48.4 31.3 %collective-permute-start.2 = (bf16[4,2,2,256,256]{4,3,2,1,0:T(8,128)(2,1)}, bf16[4,2,2,256,256]{4,3,2,1,0:T(8,128)(2,1)S(1)}, u32[]{:S(2)}, u32[]{:S(2)}) collective-permute-start(bf16[4,2,2,256,256]{4,3,2,1,0:T(8,128)(2,1)} %bitcast.10), channel_id=1, source_target_pairs={{0,8},{1,9},{2,10},{3,11},{4,12},{5,13},{6,14},{7,15},{8,0},{9,1},... | collective-permute-start | bytes 6291464 | tf_op jit(solution)/shard_map/ppermute | solution.py:12
  97.7 4.4 %copy-start.1 = (bf16[1,1024,256]{1,2,0:T(8,128)(2,1)S(1)}, bf16[1,1024,256]{1,2,0:T(8,128)(2,1)}, u32[]{:S(2)}) copy-start(bf16[1,1024,256]{1,2,0:T(8,128)(2,1)} %copy.27) | copy-start | bytes 1572868
  98.7 3.4 %copy-start.2 = (bf16[1,1024,256]{1,2,0:T(8,128)(2,1)S(1)}, bf16[1,1024,256]{1,2,0:T(8,128)(2,1)}, u32[]{:S(2)}) copy-start(bf16[1,1024,256]{1,2,0:T(8,128)(2,1)} %copy.26) | copy-start | bytes 1572868
  98.7 3.5 %copy-start.4 = (f32[256,1024]{1,0:T(8,128)S(1)}, f32[256,1024]{1,0:T(8,128)}, u32[]{:S(2)}) copy-start(f32[256,1024]{1,0:T(8,128)} %param.9) | copy-start | bytes 3145732

commit v8 on v6

--- a/solution.py
+++ b/solution.py
@@ -5,7 +5,8 @@
 from jax.sharding import PartitionSpec as P
 
 contract_rows = (((0,), (0,)), ((), ()))
-SUB = ("rh", "core", "ch", "cl")
+SUB = ("rh", "core", "chh", "chl", "cl")
+GROUP = ("rh", "chl", "cl")
 
 
 def swap(value, mask, n):
@@ -16,9 +17,9 @@
     buf = w_half
     for mask in col_masks:
         buf = jnp.concatenate([buf, swap(buf, mask, n)], axis=0)
-    group = lax.psum(1, ("rh", "cl"))
+    group = lax.psum(1, GROUP)
     spread = jnp.broadcast_to(buf[None], (group,) + buf.shape)
-    buf = lax.all_to_all(spread, ("rh", "cl"), 0, 0, tiled=False).reshape(-1, buf.shape[1])
+    buf = lax.all_to_all(spread, GROUP, 0, 0, tiled=False).reshape(-1, buf.shape[1])
     return buf, swap(buf, n_col, n)
 
 
@@ -28,7 +29,7 @@
         near = near + jnp.where(((j ^ me) & mask) != 0, 1 << k, 0)
     first = 1 << len(col_masks)
     row_idx, col_idx = j // n_col, j % n_col
-    member = (row_idx // 2) * 2 + (col_idx % 2)
+    member = (row_idx // 2) * 4 + col_idx % 4
     other_core = (row_idx % 2) != ((me // n_col) % 2)
     return jnp.where(other_core, group * first, 0) + member * first + near
 
@@ -38,7 +39,7 @@
     rank_size = h_cols.shape[0]
     n = n_row * n_col
     share = w_rows.shape[0]
-    col_masks = [2 << b for b in range(n_col.bit_length() - 2)][::-1]
+    col_masks = [4 << b for b in range(n_col.bit_length() - 3)][::-1]
     w_half = w_rows.astype(jnp.bfloat16)
     mine, theirs = gather_rows(w_half, n, n_col, col_masks)
     gram = lax.dot_general(mine, mine, contract_rows, preferred_element_type=jnp.float32)
@@ -48,7 +49,7 @@
     blocks_total = n // per_block
     rows_of = jnp.clip(tile_list, 0, blocks_total - 1)
     owners = rows_of[:, None] * per_block + jnp.arange(per_block, dtype=jnp.int32)[None, :]
-    where = position_of(owners, me, n_col, col_masks, 2 * (n_row // 2))
+    where = position_of(owners, me, n_col, col_masks, 4 * (n_row // 2))
     half = n // 2
     where = where.reshape(-1)
     near = jnp.take(mine.reshape(half, share, rank_size), where % half, axis=0)
@@ -70,7 +71,7 @@
 
 def solution(mesh):
     n_row, n_col = mesh.shape["row"], mesh.shape["col"]
-    sub = Mesh(mesh.devices.reshape(n_row // 2, 2, n_col // 2, 2), SUB)
+    sub = Mesh(mesh.devices.reshape(n_row // 2, 2, n_col // 4, 2, 2), SUB)
     placed = (
         P(SUB, None, None),
         P(SUB),

time: 66.5 us -> 61.4 us (0.923); the launches traced: 65.5 us -> 61.2 us
  waiting for transfers between devices: 13.3 us -> 6.57 us
  blocking collectives: 27.2 us -> 30.5 us
  starting transfers between devices: 4.89 us -> 4.1 us
    ppermute x3 -> x2, waiting for transfers between devices: 13.3 us -> 6.57 us  [swap(): return lax.ppermute(value, SUB, [(i, i ^ mask) for i in range(n)])]
    all_to_all x1, blocking collectives: 27.2 us -> 30.5 us  [gather_rows(): lax.all_to_all(spread, GROUP, 0, 0, tiled=False).reshape(-1, buf.shape[1])]
    ppermute x3 -> x2, starting transfers between devices: 4.89 us -> 4.1 us  [swap(): return lax.ppermute(value, SUB, [(i, i ^ mask) for i in range(n)])]
  transfers between devices with their start and end apart: 3 -> 2, of which waited for: 3 -> 2; matrix products, arithmetic and copies ran while one was open for 5% -> 5% of each run, Pallas kernels for 0% -> 0%
where the time goes in v8:
time: 61.4 us; the launch traced here: 61.2 us
  blocking collectives  30.5 us (50%)
  matrix products  8.75 us (14%)
  local copies, waits for them, and re-layouts  6.76 us (11%)
  waiting for transfers between devices  6.57 us (11%)
  starting transfers between devices  4.1 us (7%)
  other arithmetic  3.71 us (6%)
  between operations  0.8 us (1%)
    all_to_all x1, blocking collectives, gather_rows(): lax.all_to_all(spread, GROUP, 0, 0, tiled=False).reshape(-1, buf.shape[1])  30.5 us
    ppermute x2, waiting for transfers between devices, swap(): return lax.ppermute(value, SUB, [(i, i ^ mask) for i in range(n)])  6.57 us
    gather x1, local copies, waits for them, and re-layouts, shards(): far = jnp.take(theirs.reshape(half, share, rank_size), where % half, axis=0)  4.13 us
    ppermute x2, starting transfers between devices, swap(): return lax.ppermute(value, SUB, [(i, i ^ mask) for i in range(n)])  4.1 us
    dot_general x1, matrix products, shards(): lax.dot_general(picked.reshape(slots * tile, rank_size), tiles.reshape(sl...  3.87 us
    dot_general x1, matrix products, shards(): lax.dot_general(theirs, theirs, contract_rows, preferred_element_type=jnp...  3.11 us
    gather x1, local copies, waits for them, and re-layouts, shards(): near = jnp.take(mine.reshape(half, share, rank_size), where % half, axis=0)  2.38 us
    select_n x1, other arithmetic, shards(): jnp.where((where >= half)[:, None, None], far, near)  2.36 us
  transfers between devices with their start and end apart: 2, of which 2 were waited for; matrix products, arithmetic and copies ran while one was open for 5% of the time, Pallas kernels for 0%

profile of v8, /device:TPU:0, one launch (start us, length us, event | category | flops | bytes accessed | tf_op | source)
XLA Modules:
  0.0 61.2 jit_solution(3893989579162154215)
XLA Ops:
  0.0 1.0 %convert_element_type.3 = bf16[256,256]{1,0:T(8,128)(2,1)S(1)} convert(f32[256,256]{1,0:T(8,128)} %param.10) | non-fusion elementwise | flops 65536 | bytes 393216 | tf_op jit(solution)/shard_map/convert_element_type | solution.py:43
  1.0 4.1 %collective-permute-start = (bf16[256,256]{1,0:T(8,128)(2,1)S(1)}, bf16[256,256]{1,0:T(8,128)(2,1)S(1)}, u32[]{:S(2)}, u32[]{:S(2)}) collective-permute-start(bf16[256,256]{1,0:T(8,128)(2,1)S(1)} %convert_element_type.3), channel_id=1, source_target_pairs={{0,4},{1,5},{2,6},{3,7},{4,0},{5,1},{6,2},{7,3},{8,12},{9,13},{10,... | collective-permute-start | bytes 393224 | tf_op jit(solution)/shard_map/ppermute | solution.py:13
  5.1 6.3 %collective-permute-done = bf16[256,256]{1,0:T(8,128)(2,1)S(1)} collective-permute-done((bf16[256,256]{1,0:T(8,128)(2,1)S(1)}, bf16[256,256]{1,0:T(8,128)(2,1)S(1)}, u32[]{:S(2)}, u32[]{:S(2)}) %collective-permute-start) | collective-permute-done | bytes 131104 | tf_op jit(solution)/shard_map/ppermute | solution.py:13
  11.4 0.1 broadcast_in_dim.49
  11.5 0.0 copy-start.2
  11.6 30.5 %all_to_all.5 = bf16[8,512,256]{2,1,0:T(8,128)(2,1)S(1)} all-to-all(bf16[8,512,256]{2,1,0:T(8,128)(2,1)S(1)} %broadcast_in_dim.49), channel_id=1, replica_groups=mesh['rh'=2,'core'=2,'chh'=2,'chl'=2,'cl'=2] {'rh','chl','cl'}, dimensions={0} | all-to-all | bytes 4194304 | tf_op jit(solution)/shard_map/all_to_all | solution.py:22
  42.0 0.0 collective-permute-start.1
  42.7 0.0 copy-done.2
  42.7 0.1 iota_add_fusion
  42.8 0.1 add.120
  42.9 2.4 %gather_fusion.1 = bf16[20,256,256]{2,1,0:T(8,128)(2,1)} fusion(bf16[16,256,256]{2,1,0:T(8,128)(2,1)S(1)} %bitcast.25, s32[1024]{0:T(1024)S(1)} %pad_clamp_fusion), kind=kCustom, calls=%fused_computation.1.clone | custom fusion | bytes 5242960 | tf_op jit(solution)/shard_map/jit(_take)/gather | solution.py:55
  45.3 0.7 %convolution_bitcast_fusion.1 = f32[256,256]{1,0:T(8,128)S(1)} fusion(bf16[8,512,256]{2,1,0:T(8,128)(2,1)S(1)} %all_to_all.5), kind=kOutput, calls=%fused_computation.8 | convolution fusion | flops 536870912 | bytes 2359296 | tf_op jit(solution)/shard_map/dot_general | solution.py:45
  46.1 0.3 collective-permute-done.1
  46.3 0.0 copy-start
  46.3 4.1 %gather_fusion = bf16[20,256,256]{2,1,0:T(8,128)(2,1)} fusion(bf16[16,256,256]{2,1,0:T(8,128)(2,1)} %bitcast.2, s32[1024]{0:T(1024)S(1)} %pad_clamp_fusion), kind=kCustom, calls=%fused_computation.clone | custom fusion | bytes 5242960 | tf_op jit(solution)/shard_map/jit(_take)/gather | solution.py:56
  50.5 0.0 copy-done
  50.5 0.0 slice-start
  50.5 0.0 slice-start.1
  50.5 2.4 %select_select_fusion = bf16[20,256,256]{2,1,0:T(8,128)(2,1)S(1)} fusion(bf16[20,256,256]{2,1,0:T(8,128)(2,1)S(1)} %copy-done, bf16[20,256,256]{2,1,0:T(8,128)(2,1)} %gather_fusion, pred[20]{0:T(512)(128)(4,1)S(1)} %get-tuple-element.8, pred[20]{0:T(512)(128)(4,1)S(1)} %get-tuple-element.6), kind=kLoop, calls=%fused_computation.3 | loop fusion | flops 3932160 | bytes 7864360 | tf_op jit(solution)/shard_map/jit(_where)/select_n | solution.py:57
  52.8 0.2 bitcast_select_fusion
  53.1 0.0 copy-start.1
  53.1 0.0 slice-start.2
  53.1 3.1 %convolution_add_fusion = f32[256,256]{1,0:T(8,128)S(1)} fusion(f32[256,256]{1,0:T(8,128)S(1)} %convolution_bitcast_fusion.1, bf16[4096,256]{1,0:T(8,128)(2,1)} %collective-permute-done.1), kind=kOutput, calls=%fused_computation.7 | convolution fusion | flops 536936448 | bytes 2621440 | tf_op jit(solution)/shard_map/dot_general | solution.py:46
  56.2 0.0 copy-done.1
  56.2 1.0 %fusion.8 = f32[256,1024]{1,0:T(8,128)S(1)} fusion(f32[256,256]{1,0:T(8,128)S(1)} %convolution_add_fusion, f32[256,1024]{1,0:T(8,128)S(1)} %copy-done.1), kind=kOutput, calls=%fused_computation.40 | convolution fusion | flops 805306368 | bytes 2359296 | tf_op jit(solution)/shard_map/dot_general | solution.py:66
  57.3 0.0 slice-done
  57.3 0.0 slice-done.1
  57.3 0.0 slice-done.2
  57.3 3.9 %fusion.1 = f32[256,1024]{1,0:T(8,128)} fusion(f32[256,1024]{1,0:T(8,128)S(1)} %fusion.8, f32[256,1024]{1,0:T(8,128)S(1)} %copy-done.1, bf16[5,1024,256]{2,1,0:T(8,128)(2,1)S(1)} %bitcast_select_fusion, bf16[5,1024,1024]{2,1,0:T(8,128)(2,1)S(1)} %bitcast.28), kind=kOutput, calls=%fused_computation.6 | convolution fusion | flops 2684878848 | bytes 16252928 | tf_op jit(solution)/shard_map/dot_general | solution.py:60
  (7 shorter events, 0.1 us)
Async XLA Ops:
  1.0 10.4 %collective-permute-start = (bf16[256,256]{1,0:T(8,128)(2,1)S(1)}, bf16[256,256]{1,0:T(8,128)(2,1)S(1)}, u32[]{:S(2)}, u32[]{:S(2)}) collective-permute-start(bf16[256,256]{1,0:T(8,128)(2,1)S(1)} %convert_element_type.3), channel_id=1, source_target_pairs={{0,4},{1,5},{2,6},{3,7},{4,0},{5,1},{6,2},{7,3},{8,12},{9,13},{10,... | collective-permute-start | bytes 393224 | tf_op jit(solution)/shard_map/ppermute | solution.py:13
  11.5 31.2 %copy-start.2 = (s32[5]{0:T(128)S(1)}, s32[5]{0:T(128)}, u32[]{:S(2)}) copy-start(s32[5]{0:T(128)} %param.8) | copy-start | bytes 64
  42.0 4.3 %collective-permute-start.1 = (bf16[4096,256]{1,0:T(8,128)(2,1)S(1)}, bf16[4096,256]{1,0:T(8,128)(2,1)}, u32[]{:S(2)}, u32[]{:S(2)}) collective-permute-start(bf16[4096,256]{1,0:T(8,128)(2,1)S(1)} %bitcast.24), channel_id=1, source_target_pairs={{0,8},{1,9},{2,10},{3,11},{4,12},{5,13},{6,14},{7,15},{8,0},{9,1},... | collective-permute-start | bytes 6291464 | tf_op jit(solution)/shard_map/ppermute | solution.py:13
  46.3 4.1 %copy-start = (bf16[20,256,256]{2,1,0:T(8,128)(2,1)S(1)}, bf16[20,256,256]{2,1,0:T(8,128)(2,1)}, u32[]{:S(2)}) copy-start(bf16[20,256,256]{2,1,0:T(8,128)(2,1)} %gather_fusion.1) | copy-start | bytes 7864324
  50.5 6.8 %slice-start = ((s8[10485760]{0:T(1024)(128)(4,1)}), s8[2097152]{0:T(1024)(128)(4,1)S(1)}, s32[]{:S(2)}) async-start(s8[10485760]{0:T(1024)(128)(4,1)} %bitcast.27), calls=%async_computation.1 | async-start | bytes 4194304
  50.5 6.8 %slice-start.1 = ((s8[10485760]{0:T(1024)(128)(4,1)}), s8[4194304]{0:T(1024)(128)(4,1)S(1)}, s32[]{:S(2)}) async-start(s8[10485760]{0:T(1024)(128)(4,1)} %bitcast.27), calls=%async_computation.2 | async-start | bytes 8388608
  53.1 3.1 %copy-start.1 = (f32[256,1024]{1,0:T(8,128)S(1)}, f32[256,1024]{1,0:T(8,128)}, u32[]{:S(2)}) copy-start(f32[256,1024]{1,0:T(8,128)} %param.11) | copy-start | bytes 3145732
  53.1 4.2 %slice-start.2 = ((s8[10485760]{0:T(1024)(128)(4,1)}), s8[4194304]{0:T(1024)(128)(4,1)S(1)}, s32[]{:S(2)}) async-start(s8[10485760]{0:T(1024)(128)(4,1)} %bitcast.27), calls=%async_computation.3 | async-start | bytes 8388608

commit v9 on v8

--- a/solution.py
+++ b/solution.py
@@ -43,7 +43,7 @@
     w_half = w_rows.astype(jnp.bfloat16)
     mine, theirs = gather_rows(w_half, n, n_col, col_masks)
     gram = lax.dot_general(mine, mine, contract_rows, preferred_element_type=jnp.float32)
-    gram = gram + lax.dot_general(theirs, theirs, contract_rows, preferred_element_type=jnp.float32)
+    gram = gram + swap(gram, n_col, n)
     me = lax.axis_index(SUB)
     per_block = tile // share
     blocks_total = n // per_block

time: 61.4 us -> 65.7 us (1.070)
  matrix products: 8.75 us -> 11.6 us
  local copies, waits for them, and re-layouts: 6.76 us -> 8 us
    dot_general x1, matrix products: 3.87 us -> 7.87 us  [shards(): lax.dot_general(picked.reshape(slots * tile, rank_size), tiles.reshape(sl...]
    dot_general x1 -> x0, matrix products: 3.11 us -> none  [shards(): lax.dot_general(theirs, theirs, contract_rows, preferred_element_type=jnp...]
    dot_general x1, matrix products: 1.03 us -> 2.95 us  [shards(): jnp.dot(gram, h_cols, precision=lax.Precision.HIGHEST, preferred_element_...]
    unnamed x12 -> x10, local copies, waits for them, and re-layouts: 0.03 us -> 1.3 us
    ppermute x2 -> x3, starting transfers between devices: 4.1 us -> 4.68 us  [swap(): return lax.ppermute(value, SUB, [(i, i ^ mask) for i in range(n)])]
    ppermute x2 -> x3, waiting for transfers between devices: 6.57 us -> 6.38 us  [swap(): return lax.ppermute(value, SUB, [(i, i ^ mask) for i in range(n)])]
  transfers between devices with their start and end apart: 2 -> 3, of which waited for: 2 -> 2; matrix products, arithmetic and copies ran while one was open for 5% -> 10% of each run, Pallas kernels for 0% -> 0%
where the time goes in v9:
time: 65.7 us; the launch traced here: 65.4 us
  blocking collectives  30.5 us (46%)
  matrix products  11.6 us (18%)
  local copies, waits for them, and re-layouts  8 us (12%)
  waiting for transfers between devices  6.38 us (10%)
  starting transfers between devices  4.68 us (7%)
  other arithmetic  3.56 us (5%)
  between operations  0.75 us (1%)
    all_to_all x1, blocking collectives, gather_rows(): lax.all_to_all(spread, GROUP, 0, 0, tiled=False).reshape(-1, buf.shape[1])  30.5 us
    dot_general x1, matrix products, shards(): lax.dot_general(picked.reshape(slots * tile, rank_size), tiles.reshape(sl...  7.87 us
    ppermute x3, waiting for transfers between devices, swap(): return lax.ppermute(value, SUB, [(i, i ^ mask) for i in range(n)])  6.38 us
    ppermute x3, starting transfers between devices, swap(): return lax.ppermute(value, SUB, [(i, i ^ mask) for i in range(n)])  4.68 us
    gather x1, local copies, waits for them, and re-layouts, shards(): far = jnp.take(theirs.reshape(half, share, rank_size), where % half, axis=0)  4.11 us
    dot_general x1, matrix products, shards(): jnp.dot(gram, h_cols, precision=lax.Precision.HIGHEST, preferred_element_...  2.95 us
    gather x1, local copies, waits for them, and re-layouts, shards(): near = jnp.take(mine.reshape(half, share, rank_size), where % half, axis=0)  2.38 us
    select_n x1, other arithmetic, shards(): jnp.where((where >= half)[:, None, None], far, near)  2.21 us
  transfers between devices with their start and end apart: 3, of which 2 were waited for; matrix products, arithmetic and copies ran while one was open for 10% of the time, Pallas kernels for 0%

profile of v9, /device:TPU:0, one launch (start us, length us, event | category | flops | bytes accessed | tf_op | source)
XLA Modules:
  0.0 65.4 jit_solution(15578911696499125731)
XLA Ops:
  0.0 1.0 %convert_element_type.3 = bf16[256,256]{1,0:T(8,128)(2,1)S(1)} convert(f32[256,256]{1,0:T(8,128)} %param.10) | non-fusion elementwise | flops 65536 | bytes 393216 | tf_op jit(solution)/shard_map/convert_element_type | solution.py:43
  1.0 4.1 %collective-permute-start = (bf16[256,256]{1,0:T(8,128)(2,1)S(1)}, bf16[256,256]{1,0:T(8,128)(2,1)S(1)}, u32[]{:S(2)}, u32[]{:S(2)}) collective-permute-start(bf16[256,256]{1,0:T(8,128)(2,1)S(1)} %convert_element_type.3), channel_id=1, source_target_pairs={{0,4},{1,5},{2,6},{3,7},{4,0},{5,1},{6,2},{7,3},{8,12},{9,13},{10,... | collective-permute-start | bytes 393224 | tf_op jit(solution)/shard_map/ppermute | solution.py:13
  5.1 6.3 %collective-permute-done = bf16[256,256]{1,0:T(8,128)(2,1)S(1)} collective-permute-done((bf16[256,256]{1,0:T(8,128)(2,1)S(1)}, bf16[256,256]{1,0:T(8,128)(2,1)S(1)}, u32[]{:S(2)}, u32[]{:S(2)}) %collective-permute-start) | collective-permute-done | bytes 131104 | tf_op jit(solution)/shard_map/ppermute | solution.py:13
  11.4 0.1 broadcast_in_dim.49
  11.5 0.0 copy-start.4
  11.6 30.5 %all_to_all.5 = bf16[8,512,256]{2,1,0:T(8,128)(2,1)S(1)} all-to-all(bf16[8,512,256]{2,1,0:T(8,128)(2,1)S(1)} %broadcast_in_dim.49), channel_id=1, replica_groups=mesh['rh'=2,'core'=2,'chh'=2,'chl'=2,'cl'=2] {'rh','chl','cl'}, dimensions={0} | all-to-all | bytes 4194304 | tf_op jit(solution)/shard_map/all_to_all | solution.py:22
  42.0 0.0 collective-permute-start.1
  42.0 0.0 copy-done.4
  42.1 0.1 iota_add_fusion
  42.1 0.1 add.120
  42.2 0.7 %convolution_bitcast_fusion.1 = f32[256,256]{1,0:T(8,128)S(1)} fusion(bf16[8,512,256]{2,1,0:T(8,128)(2,1)S(1)} %all_to_all.5), kind=kOutput, calls=%fused_computation.7 | convolution fusion | flops 536870912 | bytes 2359296 | tf_op jit(solution)/shard_map/dot_general | solution.py:45
  43.0 0.6 collective-permute-start.2
  44.2 0.0 copy-start.1
  44.3 2.4 %gather_fusion.1 = bf16[20,256,256]{2,1,0:T(8,128)(2,1)} fusion(bf16[16,256,256]{2,1,0:T(8,128)(2,1)S(1)} %bitcast.22, s32[1024]{0:T(1024)S(1)} %pad_clamp_fusion), kind=kCustom, calls=%fused_computation.1.clone | custom fusion | bytes 5242960 | tf_op jit(solution)/shard_map/jit(_take)/gather | solution.py:55
  46.6 0.1 collective-permute-done.2
  46.7 0.0 copy-done.1
  46.7 3.0 %fusion.2 = f32[256,1024]{1,0:T(8,128)} fusion(f32[256,1024]{1,0:T(8,128)S(1)} %copy-done.1, f32[256,256]{1,0:T(8,128)S(1)} %convolution_bitcast_fusion.1, f32[256,256]{1,0:T(8,128)} %collective-permute-done.2), kind=kOutput, calls=%fused_computation.9 | convolution fusion | flops 805371904 | bytes 2621440 | tf_op jit(solution)/shard_map/dot_general | solution.py:66
  49.7 0.0 collective-permute-done.1
  49.7 0.0 copy-start
  49.7 4.1 %gather_fusion = bf16[20,256,256]{2,1,0:T(8,128)(2,1)} fusion(bf16[16,256,256]{2,1,0:T(8,128)(2,1)} %bitcast.2, s32[1024]{0:T(1024)S(1)} %pad_clamp_fusion), kind=kCustom, calls=%fused_computation.clone | custom fusion | bytes 5242960 | tf_op jit(solution)/shard_map/jit(_take)/gather | solution.py:56
  53.8 0.0 copy-done
  53.8 2.2 %select_select_fusion = bf16[20,256,256]{2,1,0:T(8,128)(2,1)S(1)} fusion(bf16[20,256,256]{2,1,0:T(8,128)(2,1)S(1)} %copy-done, bf16[20,256,256]{2,1,0:T(8,128)(2,1)} %gather_fusion, pred[20]{0:T(512)(128)(4,1)S(1)} %get-tuple-element.8, pred[20]{0:T(512)(128)(4,1)S(1)} %get-tuple-element.6), kind=kLoop, calls=%fused_computation.3 | loop fusion | flops 3932160 | bytes 7864360 | tf_op jit(solution)/shard_map/jit(_where)/select_n | solution.py:57
  56.0 0.0 copy-start.2
  56.0 0.0 copy-start.3
  56.0 0.2 bitcast_select_fusion
  56.3 1.0 %copy-done.2 = f32[256,1024]{1,0:T(8,128)S(1)} copy-done((f32[256,1024]{1,0:T(8,128)S(1)}, f32[256,1024]{1,0:T(8,128)}, u32[]{:S(2)}) %copy-start.2) | copy-done | bytes 1048600
  57.2 0.3 copy-done.3
  57.5 7.9 %fusion.1 = f32[256,1024]{1,0:T(8,128)} fusion(f32[256,1024]{1,0:T(8,128)S(1)} %copy-done.3, f32[256,1024]{1,0:T(8,128)S(1)} %copy-done.2, bf16[5,1024,256]{2,1,0:T(8,128)(2,1)S(1)} %bitcast_select_fusion, bf16[5,1024,1024]{2,1,0:T(8,128)(2,1)} %param.7), kind=kOutput, calls=%fused_computation.6 | convolution fusion | flops 2684878848 | bytes 16252928 | tf_op jit(solution)/shard_map/dot_general | solution.py:60
  (6 shorter events, 0.1 us)
Async XLA Ops:
  1.0 10.4 %collective-permute-start = (bf16[256,256]{1,0:T(8,128)(2,1)S(1)}, bf16[256,256]{1,0:T(8,128)(2,1)S(1)}, u32[]{:S(2)}, u32[]{:S(2)}) collective-permute-start(bf16[256,256]{1,0:T(8,128)(2,1)S(1)} %convert_element_type.3), channel_id=1, source_target_pairs={{0,4},{1,5},{2,6},{3,7},{4,0},{5,1},{6,2},{7,3},{8,12},{9,13},{10,... | collective-permute-start | bytes 393224 | tf_op jit(solution)/shard_map/ppermute | solution.py:13
  11.5 30.5 %copy-start.4 = (s32[5]{0:T(128)S(1)}, s32[5]{0:T(128)}, u32[]{:S(2)}) copy-start(s32[5]{0:T(128)} %param.8) | copy-start | bytes 64
  42.0 7.6 %collective-permute-start.1 = (bf16[4096,256]{1,0:T(8,128)(2,1)S(1)}, bf16[4096,256]{1,0:T(8,128)(2,1)}, u32[]{:S(2)}, u32[]{:S(2)}) collective-permute-start(bf16[4096,256]{1,0:T(8,128)(2,1)S(1)} %bitcast.21), channel_id=1, source_target_pairs={{0,8},{1,9},{2,10},{3,11},{4,12},{5,13},{6,14},{7,15},{8,0},{9,1},... | collective-permute-start | bytes 6291464 | tf_op jit(solution)/shard_map/ppermute | solution.py:13
  43.0 3.7 %collective-permute-start.2 = (f32[256,256]{1,0:T(8,128)S(1)}, f32[256,256]{1,0:T(8,128)}, u32[]{:S(2)}, u32[]{:S(2)}) collective-permute-start(f32[256,256]{1,0:T(8,128)S(1)} %convolution_bitcast_fusion.1), channel_id=1, source_target_pairs={{0,8},{1,9},{2,10},{3,11},{4,12},{5,13},{6,14},{7,15},{8,0},{9,1},... | collective-permute-start | bytes 786440 | tf_op jit(solution)/shard_map/ppermute | solution.py:13
  44.2 2.5 %copy-start.1 = (f32[256,1024]{1,0:T(8,128)S(1)}, f32[256,1024]{1,0:T(8,128)}, u32[]{:S(2)}) copy-start(f32[256,1024]{1,0:T(8,128)} %param.11) | copy-start | bytes 3145732
  49.7 4.1 %copy-start = (bf16[20,256,256]{2,1,0:T(8,128)(2,1)S(1)}, bf16[20,256,256]{2,1,0:T(8,128)(2,1)}, u32[]{:S(2)}) copy-start(bf16[20,256,256]{2,1,0:T(8,128)(2,1)} %gather_fusion.1) | copy-start | bytes 7864324
  56.0 1.2 %copy-start.2 = (f32[256,1024]{1,0:T(8,128)S(1)}, f32[256,1024]{1,0:T(8,128)}, u32[]{:S(2)}) copy-start(f32[256,1024]{1,0:T(8,128)} %param.11) | copy-start | bytes 3145732
  56.0 1.5 %copy-start.3 = (f32[256,1024]{1,0:T(8,128)S(1)}, f32[256,1024]{1,0:T(8,128)}, u32[]{:S(2)}) copy-start(f32[256,1024]{1,0:T(8,128)} %fusion.2) | copy-start | bytes 3145732

commit v10 on v8

--- a/solution.py
+++ b/solution.py
@@ -1,6 +1,8 @@
 import jax
 import jax.numpy as jnp
 from jax import lax
+from jax.experimental import pallas as pl
+from jax.experimental.pallas import tpu as pltpu
 from jax.sharding import Mesh
 from jax.sharding import PartitionSpec as P
 
@@ -34,6 +36,45 @@
     return jnp.where(other_core, group * first, 0) + member * first + near
 
 
+def pick_kernel(src_ref, far_ref, live_ref, mine_hbm, theirs_hbm, out_ref, sems):
+    for p in range(out_ref.shape[0]):
+        @pl.when((live_ref[p] != 0) & (far_ref[p] != 0))
+        def _():
+            pltpu.make_async_copy(theirs_hbm.at[src_ref[p]], out_ref.at[p], sems.at[p]).start()
+
+        @pl.when((live_ref[p] != 0) & (far_ref[p] == 0))
+        def _():
+            pltpu.make_async_copy(mine_hbm.at[src_ref[p]], out_ref.at[p], sems.at[p]).start()
+
+        @pl.when(live_ref[p] == 0)
+        def _():
+            out_ref[p] = jnp.zeros(out_ref.shape[1:], out_ref.dtype)
+
+    for p in range(out_ref.shape[0]):
+        @pl.when(live_ref[p] != 0)
+        def _():
+            pltpu.make_async_copy(mine_hbm.at[0], out_ref.at[p], sems.at[p]).wait()
+
+
+def pick_pieces(mine, theirs, src, far, live):
+    count = src.shape[0]
+    piece = mine.shape[1:]
+    return pl.pallas_call(
+        pick_kernel,
+        out_shape=jax.ShapeDtypeStruct((count,) + piece, mine.dtype),
+        grid_spec=pltpu.PrefetchScalarGridSpec(
+            num_scalar_prefetch=3,
+            grid=(),
+            in_specs=[pl.BlockSpec(memory_space=pl.ANY), pl.BlockSpec(memory_space=pl.ANY)],
+            out_specs=pl.BlockSpec((count,) + piece, lambda *_: (0, 0, 0)),
+            scratch_shapes=[pltpu.SemaphoreType.DMA((count,))],
+        ),
+        cost_estimate=pl.CostEstimate(
+            flops=0, transcendentals=0, bytes_accessed=2 * count * piece[0] * piece[1] * 2
+        ),
+    )(src, far, live, mine, theirs)
+
+
 def shards(tiles, tile_list, tile_count, w_rows, h_cols, n_row, n_col):
     slots, tile = tiles.shape[0], tiles.shape[1]
     rank_size = h_cols.shape[0]
@@ -52,11 +93,15 @@
     where = position_of(owners, me, n_col, col_masks, 4 * (n_row // 2))
     half = n // 2
     where = where.reshape(-1)
-    near = jnp.take(mine.reshape(half, share, rank_size), where % half, axis=0)
-    far = jnp.take(theirs.reshape(half, share, rank_size), where % half, axis=0)
-    picked = jnp.where((where >= half)[:, None, None], far, near).reshape(slots, tile, rank_size)
     live = jnp.arange(slots, dtype=jnp.int32) < tile_count[0]
-    picked = jnp.where(live[:, None, None], picked, jnp.zeros_like(picked))
+    live_piece = jnp.repeat(live, per_block).astype(jnp.int32)
+    picked = pick_pieces(
+        mine.reshape(half, share, rank_size),
+        theirs.reshape(half, share, rank_size),
+        jnp.clip(where % half, 0, half - 1),
+        (where >= half).astype(jnp.int32),
+        live_piece,
+    ).reshape(slots, tile, rank_size)
     numerator = lax.dot_general(
         picked.reshape(slots * tile, rank_size),
         tiles.reshape(slots * tile, tiles.shape[2]),

time: 61.4 us -> 63.2 us (1.029)
  local copies, waits for them, and re-layouts: 6.76 us -> 0.92 us
  matrix products: 8.75 us -> 13.4 us
  Pallas kernels: 0 us -> 4.15 us
  other arithmetic: 3.71 us -> 2.18 us
    gather x2 -> x0, local copies, waits for them, and re-layouts: 6.51 us -> none  [the longest x1 4.13 us: shards(): far = jnp.take(theirs.reshape(half, share, rank_size), where % half, axis=0)]
    dot_general x1, matrix products: 3.87 us -> 8.65 us  [shards(): lax.dot_general(picked.reshape(slots * tile, rank_size), tiles.reshape(sl...]
    pallas_call x0 -> x1, Pallas kernels: none -> 4.15 us  [pick_pieces(): pl.pallas_call(pick_kernel, out_shape=jax.ShapeDtypeStruct((count,) + pie...]
    select_n x2 -> x0, other arithmetic: 2.6 us -> none  [the longest x1 2.36 us: shards(): jnp.where((where >= half)[:, None, None], far, near)]
  transfers between devices with their start and end apart: 2 -> 2, of which waited for: 2 -> 2; matrix products, arithmetic and copies ran while one was open for 5% -> 4% of each run, Pallas kernels for 0% -> 0%
where the time goes in v10:
time: 63.2 us
  blocking collectives  30.5 us (48%)
  matrix products  13.4 us (21%)
  waiting for transfers between devices  7.14 us (11%)
  Pallas kernels  4.15 us (7%)
  starting transfers between devices  4.1 us (6%)
  other arithmetic  2.18 us (3%)
  local copies, waits for them, and re-layouts  0.92 us (1%)
  between operations  0.8 us (1%)
    all_to_all x1, blocking collectives, gather_rows(): lax.all_to_all(spread, GROUP, 0, 0, tiled=False).reshape(-1, buf.shape[1])  30.5 us
    dot_general x1, matrix products, shards(): lax.dot_general(picked.reshape(slots * tile, rank_size), tiles.reshape(sl...  8.65 us
    ppermute x2, waiting for transfers between devices, swap(): return lax.ppermute(value, SUB, [(i, i ^ mask) for i in range(n)])  7.14 us
    pallas_call x1, Pallas kernels, pick_pieces(): pl.pallas_call(pick_kernel, out_shape=jax.ShapeDtypeStruct((count,) + pie...  4.15 us
    ppermute x2, starting transfers between devices, swap(): return lax.ppermute(value, SUB, [(i, i ^ mask) for i in range(n)])  4.1 us
    dot_general x1, matrix products, shards(): lax.dot_general(theirs, theirs, contract_rows, preferred_element_type=jnp...  2.96 us
  transfers between devices with their start and end apart: 2, of which 2 were waited for; matrix products, arithmetic and copies ran while one was open for 4% of the time, Pallas kernels for 0%

profile of v10, /device:TPU:0, one launch (start us, length us, event | category | flops | bytes accessed | tf_op | source)
XLA Modules:
  0.0 63.2 jit_solution(13020442519888080054)
XLA Ops:
  0.0 1.0 %convert_element_type.14 = bf16[256,256]{1,0:T(8,128)(2,1)S(1)} convert(f32[256,256]{1,0:T(8,128)} %param.8) | non-fusion elementwise | flops 65536 | bytes 393216 | tf_op jit(solution)/shard_map/convert_element_type | solution.py:84
  1.0 4.1 %collective-permute-start = (bf16[256,256]{1,0:T(8,128)(2,1)S(1)}, bf16[256,256]{1,0:T(8,128)(2,1)S(1)}, u32[]{:S(2)}, u32[]{:S(2)}) collective-permute-start(bf16[256,256]{1,0:T(8,128)(2,1)S(1)} %convert_element_type.14), channel_id=1, source_target_pairs={{0,4},{1,5},{2,6},{3,7},{4,0},{5,1},{6,2},{7,3},{8,12},{9,13},{10,... | collective-permute-start | bytes 393224 | tf_op jit(solution)/shard_map/ppermute | solution.py:15
  5.1 6.3 %collective-permute-done = bf16[256,256]{1,0:T(8,128)(2,1)S(1)} collective-permute-done((bf16[256,256]{1,0:T(8,128)(2,1)S(1)}, bf16[256,256]{1,0:T(8,128)(2,1)S(1)}, u32[]{:S(2)}, u32[]{:S(2)}) %collective-permute-start) | collective-permute-done | bytes 131104 | tf_op jit(solution)/shard_map/ppermute | solution.py:15
  11.4 0.1 broadcast_in_dim.21
  11.5 0.0 copy-start.2
  11.6 30.5 %all_to_all.5 = bf16[8,512,256]{2,1,0:T(8,128)(2,1)S(1)} all-to-all(bf16[8,512,256]{2,1,0:T(8,128)(2,1)S(1)} %broadcast_in_dim.21), channel_id=1, replica_groups=mesh['rh'=2,'core'=2,'chh'=2,'chl'=2,'cl'=2] {'rh','chl','cl'}, dimensions={0} | all-to-all | bytes 4194304 | tf_op jit(solution)/shard_map/all_to_all | solution.py:24
  42.0 0.0 copy-start
  42.0 0.0 collective-permute-start.1
  42.0 0.0 copy-done.2
  42.1 0.1 iota_add_fusion
  42.1 0.1 add.79
  42.9 0.1 broadcast_in_dim.20
  43.0 0.6 convert_element_type.13.live_ref
  43.6 0.5 compare_convert_fusion.1
  44.1 0.6 fusion.4.src_ref
  44.7 0.7 %convolution_bitcast_fusion = f32[256,256]{1,0:T(8,128)S(1)} fusion(bf16[8,512,256]{2,1,0:T(8,128)(2,1)S(1)} %all_to_all.5), kind=kOutput, calls=%fused_computation.3 | convolution fusion | flops 536870912 | bytes 2359296 | tf_op jit(solution)/shard_map/dot_general | solution.py:86
  45.5 0.0 copy-done
  45.5 0.0 copy-start.1
  45.5 0.8 %collective-permute-done.1 = bf16[4096,256]{1,0:T(8,128)(2,1)} collective-permute-done((bf16[4096,256]{1,0:T(8,128)(2,1)S(1)}, bf16[4096,256]{1,0:T(8,128)(2,1)}, u32[]{:S(2)}, u32[]{:S(2)}) %collective-permute-start.1) | collective-permute-done | bytes 2097184 | tf_op jit(solution)/shard_map/ppermute | solution.py:15
  46.3 3.0 %convolution_add_fusion = f32[256,256]{1,0:T(8,128)S(1)} fusion(f32[256,256]{1,0:T(8,128)S(1)} %convolution_bitcast_fusion, bf16[4096,256]{1,0:T(8,128)(2,1)} %collective-permute-done.1), kind=kOutput, calls=%fused_computation.2 | convolution fusion | flops 536936448 | bytes 2621440 | tf_op jit(solution)/shard_map/dot_general | solution.py:87
  49.3 0.0 copy-done.1
  49.3 1.0 %fusion.8 = f32[256,1024]{1,0:T(8,128)S(1)} fusion(f32[256,256]{1,0:T(8,128)S(1)} %convolution_add_fusion, f32[256,1024]{1,0:T(8,128)S(1)} %copy-done.1), kind=kOutput, calls=%fused_computation.33 | convolution fusion | flops 805306368 | bytes 2359296 | tf_op jit(solution)/shard_map/dot_general | solution.py:111
  50.3 4.2 %shard_map.55 = bf16[20,256,256]{2,1,0:T(8,128)(2,1)} custom-call(s32[20]{0:T(128)} %fusion.4.src_ref, s32[20]{0:T(128)} %get-tuple-element.5.far_ref, s32[20]{0:T(128)} %convert_element_type.13.live_ref, bf16[16,256,256]{2,1,0:T(8,128)(2,1)} %bitcast.20, bf16[16,256,256]{2,1,0:T(8,128)(2,1)} %bitcast.3.theirs_hbm), custom_call_target="tpu_custom_call" | custom-call | bytes 5242880 | tf_op jit(solution)/shard_map/pallas_call | solution.py:62
  54.5 8.7 %fusion = f32[256,1024]{1,0:T(8,128)} fusion(f32[256,1024]{1,0:T(8,128)S(1)} %fusion.8, f32[256,1024]{1,0:T(8,128)S(1)} %copy-done.1, bf16[5120,256]{1,0:T(8,128)(2,1)} %bitcast.18, bf16[5120,1024]{1,0:T(8,128)(2,1)} %bitcast.17), kind=kOutput, calls=%fused_computation.1 | convolution fusion | flops 2684878848 | bytes 16252928 | tf_op jit(solution)/shard_map/dot_general | solution.py:105
  (3 shorter events, 0.0 us)
Async XLA Ops:
  1.0 10.4 %collective-permute-start = (bf16[256,256]{1,0:T(8,128)(2,1)S(1)}, bf16[256,256]{1,0:T(8,128)(2,1)S(1)}, u32[]{:S(2)}, u32[]{:S(2)}) collective-permute-start(bf16[256,256]{1,0:T(8,128)(2,1)S(1)} %convert_element_type.14), channel_id=1, source_target_pairs={{0,4},{1,5},{2,6},{3,7},{4,0},{5,1},{6,2},{7,3},{8,12},{9,13},{10,... | collective-permute-start | bytes 393224 | tf_op jit(solution)/shard_map/ppermute | solution.py:15
  11.5 30.5 %copy-start.2 = (s32[5]{0:T(128)S(1)}, s32[5]{0:T(128)}, u32[]{:S(2)}) copy-start(s32[5]{0:T(128)} %param.6) | copy-start | bytes 64
  42.0 3.4 %copy-start = (bf16[8,512,256]{2,1,0:T(8,128)(2,1)}, bf16[8,512,256]{2,1,0:T(8,128)(2,1)S(1)}, u32[]{:S(2)}) copy-start(bf16[8,512,256]{2,1,0:T(8,128)(2,1)S(1)} %all_to_all.5) | copy-start | bytes 6291460
  42.0 4.3 %collective-permute-start.1 = (bf16[4096,256]{1,0:T(8,128)(2,1)S(1)}, bf16[4096,256]{1,0:T(8,128)(2,1)}, u32[]{:S(2)}, u32[]{:S(2)}) collective-permute-start(bf16[4096,256]{1,0:T(8,128)(2,1)S(1)} %bitcast.19), channel_id=1, source_target_pairs={{0,8},{1,9},{2,10},{3,11},{4,12},{5,13},{6,14},{7,15},{8,0},{9,1},... | collective-permute-start | bytes 6291464 | tf_op jit(solution)/shard_map/ppermute | solution.py:15
  45.5 3.8 %copy-start.1 = (f32[256,1024]{1,0:T(8,128)S(1)}, f32[256,1024]{1,0:T(8,128)}, u32[]{:S(2)}) copy-start(f32[256,1024]{1,0:T(8,128)} %param.9) | copy-start | bytes 3145732

commit v11 on v9

--- a/solution.py
+++ b/solution.py
@@ -19,8 +19,7 @@
         buf = jnp.concatenate([buf, swap(buf, mask, n)], axis=0)
     group = lax.psum(1, GROUP)
     spread = jnp.broadcast_to(buf[None], (group,) + buf.shape)
-    buf = lax.all_to_all(spread, GROUP, 0, 0, tiled=False).reshape(-1, buf.shape[1])
-    return buf, swap(buf, n_col, n)
+    return lax.all_to_all(spread, GROUP, 0, 0, tiled=False).reshape(-1, buf.shape[1])
 
 
 def position_of(j, me, n_col, col_masks, group):
@@ -41,19 +40,26 @@
     share = w_rows.shape[0]
     col_masks = [4 << b for b in range(n_col.bit_length() - 3)][::-1]
     w_half = w_rows.astype(jnp.bfloat16)
-    mine, theirs = gather_rows(w_half, n, n_col, col_masks)
-    gram = lax.dot_general(mine, mine, contract_rows, preferred_element_type=jnp.float32)
-    gram = gram + swap(gram, n_col, n)
     me = lax.axis_index(SUB)
+    partner = me ^ n_col
+    request = swap(jnp.concatenate([tile_list, tile_count]), n_col, n)
+    mine = gather_rows(w_half, n, n_col, col_masks)
+    half = n // 2
+    pieces = mine.reshape(half, share, rank_size)
     per_block = tile // share
     blocks_total = n // per_block
-    rows_of = jnp.clip(tile_list, 0, blocks_total - 1)
-    owners = rows_of[:, None] * per_block + jnp.arange(per_block, dtype=jnp.int32)[None, :]
-    where = position_of(owners, me, n_col, col_masks, 4 * (n_row // 2))
-    half = n // 2
-    where = where.reshape(-1)
-    near = jnp.take(mine.reshape(half, share, rank_size), where % half, axis=0)
-    far = jnp.take(theirs.reshape(half, share, rank_size), where % half, axis=0)
+    lanes = jnp.arange(per_block, dtype=jnp.int32)[None, :]
+
+    def positions(blocks, device):
+        owners = jnp.clip(blocks, 0, blocks_total - 1)[:, None] * per_block + lanes
+        return position_of(owners, device, n_col, col_masks, 4 * (n_row // 2)).reshape(-1)
+
+    where = positions(tile_list, me)
+    for_partner = jnp.take(pieces, positions(request[:slots], partner) % half, axis=0)
+    own_gram = lax.dot_general(mine, mine, contract_rows, preferred_element_type=jnp.float32)
+    far = swap(for_partner, n_col, n)
+    gram = own_gram + swap(own_gram, n_col, n)
+    near = jnp.take(pieces, where % half, axis=0)
     picked = jnp.where((where >= half)[:, None, None], far, near).reshape(slots, tile, rank_size)
     live = jnp.arange(slots, dtype=jnp.int32) < tile_count[0]
     picked = jnp.where(live[:, None, None], picked, jnp.zeros_like(picked))

time: 65.7 us -> 71 us (1.081)
  waiting for transfers between devices: 6.38 us -> 36.9 us
  blocking collectives: 30.5 us -> 0 us
  starting transfers between devices: 4.68 us -> 8.7 us
  other arithmetic: 3.56 us -> 7.27 us
  local copies, waits for them, and re-layouts: 8 us -> 6.37 us
  matrix products: 11.6 us -> 10.6 us
    all_to_all x1 -> x0, blocking collectives: 30.5 us -> none  [gather_rows(): lax.all_to_all(spread, GROUP, 0, 0, tiled=False).reshape(-1, buf.shape[1])]
    all_to_all x0 -> x1, waiting for transfers between devices: none -> 28.1 us  [gather_rows(): lax.all_to_all(spread, GROUP, 0, 0, tiled=False).reshape(-1, buf.shape[1])]
    all_to_all x0 -> x1, starting transfers between devices: none -> 4.01 us  [gather_rows(): lax.all_to_all(spread, GROUP, 0, 0, tiled=False).reshape(-1, buf.shape[1])]
    select_n x0 -> x1, other arithmetic: none -> 3.54 us  [shards(): jnp.take(pieces, positions(request[:slots], partner) % half, axis=0)]
    ppermute x3 -> x4, waiting for transfers between devices: 6.38 us -> 8.84 us  [swap(): return lax.ppermute(value, SUB, [(i, i ^ mask) for i in range(n)])]
    gather x2, local copies, waits for them, and re-layouts: 6.48 us -> 4.73 us  [the longest x1 2.37 us: shards(): near = jnp.take(pieces, where % half, axis=0)]
    broadcast_in_dim x1, local copies, waits for them, and re-layouts: 0.14 us -> 1.47 us  [gather_rows(): spread = jnp.broadcast_to(buf[None], (group,) + buf.shape)]
    unnamed x10 -> x6, local copies, waits for them, and re-layouts: 1.3 us -> 0.01 us
  transfers between devices with their start and end apart: 3 -> 5, of which waited for: 2 -> 4; matrix products, arithmetic and copies ran while one was open for 10% -> 8% of each run, Pallas kernels for 0% -> 0%
where the time goes in v11:
time: 71 us; the launch traced here: 70.7 us
  waiting for transfers between devices  36.9 us (52%)
  matrix products  10.6 us (15%)
  starting transfers between devices  8.7 us (12%)
  other arithmetic  7.27 us (10%)
  local copies, waits for them, and re-layouts  6.37 us (9%)
  between operations  0.81 us (1%)
    all_to_all x1, waiting for transfers between devices, gather_rows(): lax.all_to_all(spread, GROUP, 0, 0, tiled=False).reshape(-1, buf.shape[1])  28.1 us
    ppermute x4, waiting for transfers between devices, swap(): return lax.ppermute(value, SUB, [(i, i ^ mask) for i in range(n)])  8.84 us
    dot_general x1, matrix products, shards(): lax.dot_general(picked.reshape(slots * tile, rank_size), tiles.reshape(sl...  7.86 us
    ppermute x4, starting transfers between devices, swap(): return lax.ppermute(value, SUB, [(i, i ^ mask) for i in range(n)])  4.69 us
    all_to_all x1, starting transfers between devices, gather_rows(): lax.all_to_all(spread, GROUP, 0, 0, tiled=False).reshape(-1, buf.shape[1])  4.01 us
    select_n x1, other arithmetic, shards(): jnp.take(pieces, positions(request[:slots], partner) % half, axis=0)  3.54 us
    gather x1, local copies, waits for them, and re-layouts, shards(): near = jnp.take(pieces, where % half, axis=0)  2.37 us
    gather x1, local copies, waits for them, and re-layouts, shards(): jnp.take(pieces, positions(request[:slots], partner) % half, axis=0)  2.35 us
  transfers between devices with their start and end apart: 5, of which 4 were waited for; matrix products, arithmetic and copies ran while one was open for 8% of the time, Pallas kernels for 0%

profile of v11, /device:TPU:0, one launch (start us, length us, event | category | flops | bytes accessed | tf_op | source)
XLA Modules:
  0.0 70.7 jit_solution(2296505030820979609)
XLA Ops:
  0.0 1.0 %convert_element_type.3 = bf16[256,256]{1,0:T(8,128)(2,1)S(1)} convert(f32[256,256]{1,0:T(8,128)} %param.10) | non-fusion elementwise | flops 65536 | bytes 393216 | tf_op jit(solution)/shard_map/convert_element_type | solution.py:42
  1.0 4.1 %collective-permute-start = (bf16[256,256]{1,0:T(8,128)(2,1)S(1)}, bf16[256,256]{1,0:T(8,128)(2,1)S(1)}, u32[]{:S(2)}, u32[]{:S(2)}) collective-permute-start(bf16[256,256]{1,0:T(8,128)(2,1)S(1)} %convert_element_type.3), channel_id=1, source_target_pairs={{0,4},{1,5},{2,6},{3,7},{4,0},{5,1},{6,2},{7,3},{8,12},{9,13},{10,... | collective-permute-start | bytes 393224 | tf_op jit(solution)/shard_map/ppermute | solution.py:13
  5.1 6.3 %collective-permute-done = bf16[256,256]{1,0:T(8,128)(2,1)S(1)} collective-permute-done((bf16[256,256]{1,0:T(8,128)(2,1)S(1)}, bf16[256,256]{1,0:T(8,128)(2,1)S(1)}, u32[]{:S(2)}, u32[]{:S(2)}) %collective-permute-start) | collective-permute-done | bytes 131104 | tf_op jit(solution)/shard_map/ppermute | solution.py:13
  11.4 1.5 %broadcast_in_dim.54 = bf16[8,512,256]{2,1,0:T(8,128)(2,1)} broadcast(bf16[512,256]{1,0:T(8,128)(2,1)S(1)} %pad_maximum_fusion), dimensions={1,2} | broadcast | bytes 2359296 | tf_op jit(solution)/shard_map/broadcast_in_dim | solution.py:21
  12.9 0.0 copy-start.2
  12.9 4.0 %all-to-all-start = ((bf16[8,512,256]{2,1,0:T(8,128)(2,1)}), bf16[8,512,256]{2,1,0:T(8,128)(2,1)S(1)}, u32[]{:S(2)}, u32[]{:S(2)}) async-start(bf16[8,512,256]{2,1,0:T(8,128)(2,1)} %broadcast_in_dim.54), calls=%async_computation | async-start | bytes 4194304 | tf_op jit(solution)/shard_map/all_to_all | solution.py:22
  17.5 0.0 copy-done.2
  17.5 0.1 pad_add_fusion
  17.6 0.0 collective-permute-start.1
  17.7 1.1 %collective-permute-done.1 = s32[6]{0:T(128)S(1)} collective-permute-done((s32[6]{0:T(128)S(1)}, s32[6]{0:T(128)S(1)}, u32[]{:S(2)}, u32[]{:S(2)}) %collective-permute-start.1) | collective-permute-done | bytes 56 | tf_op jit(solution)/shard_map/ppermute | solution.py:13
  18.7 0.1 iota_add_fusion
  18.8 0.1 add.189
  19.0 28.1 %all-to-all-done = bf16[8,512,256]{2,1,0:T(8,128)(2,1)S(1)} async-done(((bf16[8,512,256]{2,1,0:T(8,128)(2,1)}), bf16[8,512,256]{2,1,0:T(8,128)(2,1)S(1)}, u32[]{:S(2)}, u32[]{:S(2)}) %all-to-all-start) | async-done | bytes 2097184 | tf_op jit(solution)/shard_map/all_to_all | solution.py:22
  47.1 2.4 %gather_fusion = bf16[20,256,256]{2,1,0:T(8,128)(2,1)} fusion(bf16[16,256,256]{2,1,0:T(8,128)(2,1)S(1)} %bitcast.19, s32[1024]{0:T(1024)S(1)} %pad_clamp_fusion.1), kind=kCustom, calls=%fused_computation.clone | custom fusion | bytes 5242960 | tf_op jit(solution)/shard_map/jit(_take)/gather | solution.py:58
  49.4 3.5 %broadcast_select_fusion = bf16[20,256,256]{2,1,0:T(8,128)(2,1)} fusion(bf16[20,256,256]{2,1,0:T(8,128)(2,1)} %gather_fusion, pred[20]{0:T(512)(128)(4,1)S(1)} %get-tuple-element.10), kind=kLoop, calls=%fused_computation.4 | loop fusion | flops 1310720 | bytes 5242900 | tf_op jit(solution)/shard_map/jit(_take)/select_n | solution.py:58
  53.0 0.0 collective-permute-start.2
  53.0 0.1 iota_add_fusion.1
  53.0 0.1 add.174
  53.1 0.7 %convolution_bitcast_fusion.1 = f32[256,256]{1,0:T(8,128)S(1)} fusion(bf16[8,512,256]{2,1,0:T(8,128)(2,1)S(1)} %all-to-all-done), kind=kOutput, calls=%fused_computation.8 | convolution fusion | flops 536870912 | bytes 2359296 | tf_op jit(solution)/shard_map/dot_general | solution.py:59
  53.9 0.6 collective-permute-start.3
  54.5 0.0 copy-start.1
  54.5 2.4 %gather_fusion.1 = bf16[20,256,256]{2,1,0:T(8,128)(2,1)} fusion(bf16[16,256,256]{2,1,0:T(8,128)(2,1)S(1)} %bitcast.20, s32[1024]{0:T(1024)S(1)} %pad_clamp_fusion), kind=kCustom, calls=%fused_computation.1.clone | custom fusion | bytes 5242960 | tf_op jit(solution)/shard_map/jit(_take)/gather | solution.py:62
  56.9 0.0 copy-start
  56.9 1.5 %collective-permute-done.3 = f32[256,256]{1,0:T(8,128)} collective-permute-done((f32[256,256]{1,0:T(8,128)S(1)}, f32[256,256]{1,0:T(8,128)}, u32[]{:S(2)}, u32[]{:S(2)}) %collective-permute-start.3) | collective-permute-done | bytes 262176 | tf_op jit(solution)/shard_map/ppermute | solution.py:13
  58.4 0.0 copy-done.1
  58.4 2.0 %fusion.2 = f32[256,1024]{1,0:T(8,128)S(1)} fusion(f32[256,1024]{1,0:T(8,128)S(1)} %copy-done.1, f32[256,256]{1,0:T(8,128)S(1)} %convolution_bitcast_fusion.1, f32[256,256]{1,0:T(8,128)} %collective-permute-done.3), kind=kOutput, calls=%fused_computation.10 | convolution fusion | flops 805371904 | bytes 2621440 | tf_op jit(solution)/shard_map/dot_general | solution.py:72
  60.4 0.0 collective-permute-done.2
  60.4 0.0 copy-done
  60.4 2.2 %select_select_fusion = bf16[20,256,256]{2,1,0:T(8,128)(2,1)S(1)} fusion(bf16[20,256,256]{2,1,0:T(8,128)(2,1)} %collective-permute-done.2, bf16[20,256,256]{2,1,0:T(8,128)(2,1)S(1)} %copy-done, pred[20]{0:T(512)(128)(4,1)S(1)} %get-tuple-element.8, pred[20]{0:T(512)(128)(4,1)S(1)} %get-tuple-element.6), kind=kLoop, calls=%fused_computation.3 | loop fusion | flops 2621440 | bytes 7864360 | tf_op jit(solution)/shard_map/jit(_where)/select_n | solution.py:63
  62.6 0.2 bitcast_select_fusion
  62.8 7.9 %fusion.1 = f32[256,1024]{1,0:T(8,128)} fusion(f32[256,1024]{1,0:T(8,128)S(1)} %fusion.2, f32[256,1024]{1,0:T(8,128)S(1)} %copy-done.1, bf16[5,1024,256]{2,1,0:T(8,128)(2,1)S(1)} %bitcast_select_fusion, bf16[5,1024,1024]{2,1,0:T(8,128)(2,1)} %param.7), kind=kOutput, calls=%fused_computation.7 | convolution fusion | flops 2684878848 | bytes 16252928 | tf_op jit(solution)/shard_map/dot_general | solution.py:66
  (9 shorter events, 0.1 us)
Async XLA Ops:
  1.0 10.4 %collective-permute-start = (bf16[256,256]{1,0:T(8,128)(2,1)S(1)}, bf16[256,256]{1,0:T(8,128)(2,1)S(1)}, u32[]{:S(2)}, u32[]{:S(2)}) collective-permute-start(bf16[256,256]{1,0:T(8,128)(2,1)S(1)} %convert_element_type.3), channel_id=1, source_target_pairs={{0,4},{1,5},{2,6},{3,7},{4,0},{5,1},{6,2},{7,3},{8,12},{9,13},{10,... | collective-permute-start | bytes 393224 | tf_op jit(solution)/shard_map/ppermute | solution.py:13
  12.9 4.7 %copy-start.2 = (s32[5]{0:T(128)S(1)}, s32[5]{0:T(128)}, u32[]{:S(2)}) copy-start(s32[5]{0:T(128)} %param.8) | copy-start | bytes 64
  12.9 34.2 %all-to-all-start = ((bf16[8,512,256]{2,1,0:T(8,128)(2,1)}), bf16[8,512,256]{2,1,0:T(8,128)(2,1)S(1)}, u32[]{:S(2)}, u32[]{:S(2)}) async-start(bf16[8,512,256]{2,1,0:T(8,128)(2,1)} %broadcast_in_dim.54), calls=%async_computation | async-start | bytes 4194304 | tf_op jit(solution)/shard_map/all_to_all | solution.py:22
  17.6 1.1 %collective-permute-start.1 = (s32[6]{0:T(128)S(1)}, s32[6]{0:T(128)S(1)}, u32[]{:S(2)}, u32[]{:S(2)}) collective-permute-start(s32[6]{0:T(128)S(1)} %pad_add_fusion), channel_id=1, source_target_pairs={{0,8},{1,9},{2,10},{3,11},{4,12},{5,13},{6,14},{7,15},{8,0},{9,1},... | collective-permute-start | bytes 80 | tf_op jit(solution)/shard_map/ppermute | solution.py:13
  53.0 7.4 %collective-permute-start.2 = (bf16[20,256,256]{2,1,0:T(8,128)(2,1)}, bf16[20,256,256]{2,1,0:T(8,128)(2,1)}, u32[]{:S(2)}, u32[]{:S(2)}) collective-permute-start(bf16[20,256,256]{2,1,0:T(8,128)(2,1)} %broadcast_select_fusion), channel_id=1, source_target_pairs={{0,8},{1,9},{2,10},{3,11},{4,12},{5,13},{6,14},{7,15},{8,0},{9,1},... | collective-permute-start | bytes 7864328 | tf_op jit(solution)/shard_map/ppermute | solution.py:13
  53.9 4.5 %collective-permute-start.3 = (f32[256,256]{1,0:T(8,128)S(1)}, f32[256,256]{1,0:T(8,128)}, u32[]{:S(2)}, u32[]{:S(2)}) collective-permute-start(f32[256,256]{1,0:T(8,128)S(1)} %convolution_bitcast_fusion.1), channel_id=1, source_target_pairs={{0,8},{1,9},{2,10},{3,11},{4,12},{5,13},{6,14},{7,15},{8,0},{9,1},... | collective-permute-start | bytes 786440 | tf_op jit(solution)/shard_map/ppermute | solution.py:13
  54.5 3.9 %copy-start.1 = (f32[256,1024]{1,0:T(8,128)S(1)}, f32[256,1024]{1,0:T(8,128)}, u32[]{:S(2)}) copy-start(f32[256,1024]{1,0:T(8,128)} %param.11) | copy-start | bytes 3145732
  56.9 3.5 %copy-start = (bf16[20,256,256]{2,1,0:T(8,128)(2,1)S(1)}, bf16[20,256,256]{2,1,0:T(8,128)(2,1)}, u32[]{:S(2)}) copy-start(bf16[20,256,256]{2,1,0:T(8,128)(2,1)} %gather_fusion.1) | copy-start | bytes 7864324

commit v12 on v8

--- a/solution.py
+++ b/solution.py
@@ -52,8 +52,11 @@
     where = position_of(owners, me, n_col, col_masks, 4 * (n_row // 2))
     half = n // 2
     where = where.reshape(-1)
-    near = jnp.take(mine.reshape(half, share, rank_size), where % half, axis=0)
-    far = jnp.take(theirs.reshape(half, share, rank_size), where % half, axis=0)
+    index = where % half
+    near_src = mine.reshape(half, share, rank_size)
+    far_src = theirs.reshape(half, share, rank_size)
+    near = jnp.stack([lax.dynamic_index_in_dim(near_src, index[p], keepdims=False) for p in range(index.shape[0])])
+    far = jnp.stack([lax.dynamic_index_in_dim(far_src, index[p], keepdims=False) for p in range(index.shape[0])])
     picked = jnp.where((where >= half)[:, None, None], far, near).reshape(slots, tile, rank_size)
     live = jnp.arange(slots, dtype=jnp.int32) < tile_count[0]
     picked = jnp.where(live[:, None, None], picked, jnp.zeros_like(picked))

time: 61.4 us -> 67.9 us (1.11); the launches traced: 61.2 us -> 67 us
  between operations: 0.8 us -> 36.5 us
  blocking collectives: 30.5 us -> 0 us
  starting transfers between devices: 4.1 us -> 8.18 us
  waiting for transfers between devices: 6.57 us -> 9.19 us
  matrix products: 8.75 us -> 6.37 us
  local copies, waits for them, and re-layouts: 6.76 us -> 4.43 us
  other arithmetic: 3.71 us -> 2.25 us
    all_to_all x1 -> x0, blocking collectives: 30.5 us -> none  [gather_rows(): lax.all_to_all(spread, GROUP, 0, 0, tiled=False).reshape(-1, buf.shape[1])]
    gather x2 -> x0, local copies, waits for them, and re-layouts: 6.51 us -> none  [the longest x1 4.13 us: shards(): far = jnp.take(theirs.reshape(half, share, rank_size), where % half, axis=0)]
    all_to_all x0 -> x1, starting transfers between devices: none -> 4.01 us  [gather_rows(): lax.all_to_all(spread, GROUP, 0, 0, tiled=False).reshape(-1, buf.shape[1])]
    ppermute x2, waiting for transfers between devices: 6.57 us -> 9.19 us  [swap(): return lax.ppermute(value, SUB, [(i, i ^ mask) for i in range(n)])]
    dot_general x1, matrix products: 3.11 us -> 0.75 us  [shards(): lax.dot_general(theirs, theirs, contract_rows, preferred_element_type=jnp...]
    select_n x1, other arithmetic: 2.36 us -> 0.03 us  [shards(): index = where % half]
    unnamed x12 -> x50, local copies, waits for them, and re-layouts: 0.03 us -> 2.11 us
    broadcast_in_dim x1, local copies, waits for them, and re-layouts: 0.14 us -> 1.47 us  [gather_rows(): spread = jnp.broadcast_to(buf[None], (group,) + buf.shape)]
  transfers between devices with their start and end apart: 2 -> 3, of which waited for: 2 -> 2; matrix products, arithmetic and copies ran while one was open for 5% -> 3% of each run, Pallas kernels for 0% -> 0%
where the time goes in v12:
time: 67.9 us; the launch traced here: 67 us
  between operations  36.5 us (54%)
  waiting for transfers between devices  9.19 us (14%)
  starting transfers between devices  8.18 us (12%)
  matrix products  6.37 us (9%)
  local copies, waits for them, and re-layouts  4.43 us (7%)
  other arithmetic  2.25 us (3%)
    ppermute x2, waiting for transfers between devices, swap(): return lax.ppermute(value, SUB, [(i, i ^ mask) for i in range(n)])  9.19 us
    ppermute x2, starting transfers between devices, swap(): return lax.ppermute(value, SUB, [(i, i ^ mask) for i in range(n)])  4.17 us
    all_to_all x1, starting transfers between devices, gather_rows(): lax.all_to_all(spread, GROUP, 0, 0, tiled=False).reshape(-1, buf.shape[1])  4.01 us
    dot_general x1, matrix products, shards(): lax.dot_general(picked.reshape(slots * tile, rank_size), tiles.reshape(sl...  3.86 us
    unnamed x50, local copies, waits for them, and re-layouts  2.11 us
    broadcast_in_dim x1, local copies, waits for them, and re-layouts, gather_rows(): spread = jnp.broadcast_to(buf[None], (group,) + buf.shape)  1.47 us
  transfers between devices with their start and end apart: 3, of which 2 were waited for; matrix products, arithmetic and copies ran while one was open for 3% of the time, Pallas kernels for 0%

profile of v12, /device:TPU:0, one launch (start us, length us, event | category | flops | bytes accessed | tf_op | source)
XLA Modules:
  0.0 67.0 jit_solution(16012674322154996584)
XLA Ops:
  0.0 1.0 %convert_element_type.3 = bf16[256,256]{1,0:T(8,128)(2,1)S(1)} convert(f32[256,256]{1,0:T(8,128)} %param.8) | non-fusion elementwise | flops 65536 | bytes 393216 | tf_op jit(solution)/shard_map/convert_element_type | solution.py:43
  1.0 4.1 %collective-permute-start = (bf16[256,256]{1,0:T(8,128)(2,1)S(1)}, bf16[256,256]{1,0:T(8,128)(2,1)S(1)}, u32[]{:S(2)}, u32[]{:S(2)}) collective-permute-start(bf16[256,256]{1,0:T(8,128)(2,1)S(1)} %convert_element_type.3), channel_id=1, source_target_pairs={{0,4},{1,5},{2,6},{3,7},{4,0},{5,1},{6,2},{7,3},{8,12},{9,13},{10,... | collective-permute-start | bytes 393224 | tf_op jit(solution)/shard_map/ppermute | solution.py:13
  5.1 6.3 %collective-permute-done = bf16[256,256]{1,0:T(8,128)(2,1)S(1)} collective-permute-done((bf16[256,256]{1,0:T(8,128)(2,1)S(1)}, bf16[256,256]{1,0:T(8,128)(2,1)S(1)}, u32[]{:S(2)}, u32[]{:S(2)}) %collective-permute-start) | collective-permute-done | bytes 131104 | tf_op jit(solution)/shard_map/ppermute | solution.py:13
  11.4 1.5 %broadcast_in_dim.48 = bf16[8,512,256]{2,1,0:T(8,128)(2,1)} broadcast(bf16[512,256]{1,0:T(8,128)(2,1)S(1)} %pad_maximum_fusion), dimensions={1,2} | broadcast | bytes 2359296 | tf_op jit(solution)/shard_map/broadcast_in_dim | solution.py:21
  12.9 0.0 copy-start.1
  12.9 4.0 %all-to-all-start = ((bf16[8,512,256]{2,1,0:T(8,128)(2,1)}), bf16[8,512,256]{2,1,0:T(8,128)(2,1)S(1)}, u32[]{:S(2)}, u32[]{:S(2)}) async-start(bf16[8,512,256]{2,1,0:T(8,128)(2,1)} %broadcast_in_dim.48), calls=%async_computation | async-start | bytes 4194304 | tf_op jit(solution)/shard_map/all_to_all | solution.py:22
  16.9 0.0 copy-done.1
  16.9 0.1 iota_add_fusion
  17.0 0.1 add.219
  17.2 0.7 %fusion.23 = (s32[1]{0:T(128)}, s32[1]{0:T(128)}, s32[1]{0:T(128)}, s32[1]{0:T(128)}, s32[1]{0:T(128)}, /*index=5*/s32[1]{0:T(128)}, s32[1]{0:T(128)}, s32[1]{0:...) fusion(s32[20]{0:T(128)S(1)} %and_select_fusion), kind=kLoop, calls=%fused_computation.106 | loop fusion | bytes 152 | tf_op jit(solution)/shard_map/slice | solution.py:59
  42.1 0.1 fusion.9
  42.2 0.1 broadcast_bitcast_fusion
  54.1 0.0 all-to-all-done
  54.1 0.1 collective-permute-start.1
  54.7 0.7 %convolution_bitcast_fusion.1 = f32[256,256]{1,0:T(8,128)S(1)} fusion(bf16[8,512,256]{2,1,0:T(8,128)(2,1)S(1)} %all-to-all-done), kind=kOutput, calls=%fused_computation.6 | convolution fusion | flops 536870912 | bytes 2359296 | tf_op jit(solution)/shard_map/dot_general | solution.py:45
  55.5 2.9 %collective-permute-done.1 = bf16[4096,256]{1,0:T(8,128)(2,1)S(1)} collective-permute-done((bf16[4096,256]{1,0:T(8,128)(2,1)S(1)}, bf16[4096,256]{1,0:T(8,128)(2,1)S(1)}, u32[]{:S(2)}, u32[]{:S(2)}) %collective-permute-start.1) | collective-permute-done | bytes 2097184 | tf_op jit(solution)/shard_map/ppermute | solution.py:13
  58.5 0.0 slice-start
  58.8 0.0 copy-start
  58.9 0.0 slice-start.1
  58.9 0.7 %convolution_add_fusion = f32[256,256]{1,0:T(8,128)S(1)} fusion(f32[256,256]{1,0:T(8,128)S(1)} %convolution_bitcast_fusion.1, bf16[4096,256]{1,0:T(8,128)(2,1)S(1)} %collective-permute-done.1), kind=kOutput, calls=%fused_computation.5 | convolution fusion | flops 536936448 | bytes 2621440 | tf_op jit(solution)/shard_map/dot_general | solution.py:46
  59.6 0.6 copy-done
  60.2 1.0 %fusion.24 = f32[256,1024]{1,0:T(8,128)S(1)} fusion(f32[256,256]{1,0:T(8,128)S(1)} %convolution_add_fusion, f32[256,1024]{1,0:T(8,128)S(1)} %copy-done), kind=kOutput, calls=%fused_computation.107 | convolution fusion | flops 805306368 | bytes 2359296 | tf_op jit(solution)/shard_map/dot_general | solution.py:69
  61.2 0.0 slice-start.2
  61.2 1.1 %fusion = bf16[5,1024,256]{2,1,0:T(8,128)(2,1)S(1)} fusion(pred[5]{0:T(512)(128)(4,1)S(1)} %iota_compare_fusion, pred[5,1024]{1,0:T(8,128)(4,1)S(1)} %bitcast.101, bf16[5,1024,256]{2,1,0:T(8,128)(2,1)S(1)} %bitcast.97, bf16[5,1024,256]{2,1,0:T(8,128)(2,1)S(1)} %bitcast.96), kind=kLoop, calls=%fused_computation.1 | loop fusion | flops 2621440 | bytes 7869445 | tf_op jit(solution)/shard_map/jit(_where)/select_n | solution.py:62
  62.3 0.0 slice-done
  62.3 0.0 slice-done.1
  62.3 0.8 %slice-done.2 = s8[2097152]{0:T(1024)(128)(4,1)S(1)} async-done(((s8[10485760]{0:T(1024)(128)(4,1)}), s8[2097152]{0:T(1024)(128)(4,1)S(1)}, s32[]{:S(2)}) %slice-start.2) | async-done | bytes 2097176
  63.1 3.9 %fusion.2 = f32[256,1024]{1,0:T(8,128)} fusion(f32[256,1024]{1,0:T(8,128)S(1)} %fusion.24, f32[256,1024]{1,0:T(8,128)S(1)} %copy-done, bf16[5,1024,256]{2,1,0:T(8,128)(2,1)S(1)} %fusion, bf16[5,1024,1024]{2,1,0:T(8,128)(2,1)S(1)} %bitcast.75), kind=kOutput, calls=%fused_computation.4 | convolution fusion | flops 2684878848 | bytes 16252928 | tf_op jit(solution)/shard_map/dot_general | solution.py:63
  (46 shorter events, 0.8 us)
Async XLA Ops:
  1.0 10.4 %collective-permute-start = (bf16[256,256]{1,0:T(8,128)(2,1)S(1)}, bf16[256,256]{1,0:T(8,128)(2,1)S(1)}, u32[]{:S(2)}, u32[]{:S(2)}) collective-permute-start(bf16[256,256]{1,0:T(8,128)(2,1)S(1)} %convert_element_type.3), channel_id=1, source_target_pairs={{0,4},{1,5},{2,6},{3,7},{4,0},{5,1},{6,2},{7,3},{8,12},{9,13},{10,... | collective-permute-start | bytes 393224 | tf_op jit(solution)/shard_map/ppermute | solution.py:13
  12.9 4.0 %copy-start.1 = (s32[5]{0:T(128)S(1)}, s32[5]{0:T(128)}, u32[]{:S(2)}) copy-start(s32[5]{0:T(128)} %param.6) | copy-start | bytes 64
  12.9 41.2 %all-to-all-start = ((bf16[8,512,256]{2,1,0:T(8,128)(2,1)}), bf16[8,512,256]{2,1,0:T(8,128)(2,1)S(1)}, u32[]{:S(2)}, u32[]{:S(2)}) async-start(bf16[8,512,256]{2,1,0:T(8,128)(2,1)} %broadcast_in_dim.48), calls=%async_computation | async-start | bytes 4194304 | tf_op jit(solution)/shard_map/all_to_all | solution.py:22
  54.1 4.2 %collective-permute-start.1 = (bf16[4096,256]{1,0:T(8,128)(2,1)S(1)}, bf16[4096,256]{1,0:T(8,128)(2,1)S(1)}, u32[]{:S(2)}, u32[]{:S(2)}) collective-permute-start(bf16[4096,256]{1,0:T(8,128)(2,1)S(1)} %bitcast.53), channel_id=1, source_target_pairs={{0,8},{1,9},{2,10},{3,11},{4,12},{5,13},{6,14},{7,15},{8,0},{9,1},... | collective-permute-start | bytes 6291464 | tf_op jit(solution)/shard_map/ppermute | solution.py:13
  58.5 3.8 %slice-start = ((s8[10485760]{0:T(1024)(128)(4,1)}), s8[4194304]{0:T(1024)(128)(4,1)S(1)}, s32[]{:S(2)}) async-start(s8[10485760]{0:T(1024)(128)(4,1)} %bitcast.74), calls=%async_computation.1 | async-start | bytes 8388608
  58.8 1.4 %copy-start = (f32[256,1024]{1,0:T(8,128)S(1)}, f32[256,1024]{1,0:T(8,128)}, u32[]{:S(2)}) copy-start(f32[256,1024]{1,0:T(8,128)} %param.9) | copy-start | bytes 3145732
  58.9 3.5 %slice-start.1 = ((s8[10485760]{0:T(1024)(128)(4,1)}), s8[4194304]{0:T(1024)(128)(4,1)S(1)}, s32[]{:S(2)}) async-start(s8[10485760]{0:T(1024)(128)(4,1)} %bitcast.74), calls=%async_computation.2 | async-start | bytes 8388608
  61.2 1.9 %slice-start.2 = ((s8[10485760]{0:T(1024)(128)(4,1)}), s8[2097152]{0:T(1024)(128)(4,1)S(1)}, s32[]{:S(2)}) async-start(s8[10485760]{0:T(1024)(128)(4,1)} %bitcast.74), calls=%async_computation.3 | async-start | bytes 4194304

commit v13 on v8

--- a/solution.py
+++ b/solution.py
@@ -52,8 +52,9 @@
     where = position_of(owners, me, n_col, col_masks, 4 * (n_row // 2))
     half = n // 2
     where = where.reshape(-1)
-    near = jnp.take(mine.reshape(half, share, rank_size), where % half, axis=0)
-    far = jnp.take(theirs.reshape(half, share, rank_size), where % half, axis=0)
+    index = where % half
+    near = mine.reshape(half, share, rank_size).at[index].get(mode="promise_in_bounds")
+    far = theirs.reshape(half, share, rank_size).at[index].get(mode="promise_in_bounds")
     picked = jnp.where((where >= half)[:, None, None], far, near).reshape(slots, tile, rank_size)
     live = jnp.arange(slots, dtype=jnp.int32) < tile_count[0]
     picked = jnp.where(live[:, None, None], picked, jnp.zeros_like(picked))

time: 61.4 us -> 62 us (level)
  matrix products: 8.75 us -> 12.8 us
  local copies, waits for them, and re-layouts: 6.76 us -> 4.99 us
  other arithmetic: 3.71 us -> 2.26 us
    dot_general x1, matrix products: 3.87 us -> 7.87 us  [shards(): lax.dot_general(picked.reshape(slots * tile, rank_size), tiles.reshape(sl...]
    select_n x1, other arithmetic: 2.36 us -> 0.03 us  [shards(): theirs.reshape(half, share, rank_size).at[index]]
    gather x2, local copies, waits for them, and re-layouts: 6.51 us -> 4.67 us  [the longest x1 2.37 us: shards(): mine.reshape(half, share, rank_size).at[index].get(mode='promise_in_bounds')]
    select_n x1, other arithmetic: 0.24 us -> 1.06 us  [shards(): picked = jnp.where(live[:, None, None], picked, jnp.zeros_like(picked))]
  transfers between devices with their start and end apart: 2 -> 2, of which waited for: 2 -> 2; matrix products, arithmetic and copies ran while one was open for 5% -> 6% of each run, Pallas kernels for 0% -> 0%
where the time goes in v13:
time: 62 us; the launch traced here: 61.8 us
  blocking collectives  30.5 us (49%)
  matrix products  12.8 us (21%)
  waiting for transfers between devices  6.41 us (10%)
  local copies, waits for them, and re-layouts  4.99 us (8%)
  starting transfers between devices  4.1 us (7%)
  other arithmetic  2.26 us (4%)
  between operations  0.78 us (1%)
    all_to_all x1, blocking collectives, gather_rows(): lax.all_to_all(spread, GROUP, 0, 0, tiled=False).reshape(-1, buf.shape[1])  30.5 us
    dot_general x1, matrix products, shards(): lax.dot_general(picked.reshape(slots * tile, rank_size), tiles.reshape(sl...  7.87 us
    ppermute x2, waiting for transfers between devices, swap(): return lax.ppermute(value, SUB, [(i, i ^ mask) for i in range(n)])  6.41 us
    ppermute x2, starting transfers between devices, swap(): return lax.ppermute(value, SUB, [(i, i ^ mask) for i in range(n)])  4.1 us
    dot_general x1, matrix products, shards(): lax.dot_general(theirs, theirs, contract_rows, preferred_element_type=jnp...  3.11 us
    gather x1, local copies, waits for them, and re-layouts, shards(): mine.reshape(half, share, rank_size).at[index].get(mode='promise_in_bounds')  2.37 us
    gather x1, local copies, waits for them, and re-layouts, shards(): theirs.reshape(half, share, rank_size).at[index]  2.3 us
  transfers between devices with their start and end apart: 2, of which 2 were waited for; matrix products, arithmetic and copies ran while one was open for 6% of the time, Pallas kernels for 0%

profile of v13, /device:TPU:0, one launch (start us, length us, event | category | flops | bytes accessed | tf_op | source)
XLA Modules:
  0.0 61.8 jit_solution(10836511001785766218)
XLA Ops:
  0.0 1.0 %convert_element_type.3 = bf16[256,256]{1,0:T(8,128)(2,1)S(1)} convert(f32[256,256]{1,0:T(8,128)} %param.8) | non-fusion elementwise | flops 65536 | bytes 393216 | tf_op jit(solution)/shard_map/convert_element_type | solution.py:43
  1.0 4.1 %collective-permute-start = (bf16[256,256]{1,0:T(8,128)(2,1)S(1)}, bf16[256,256]{1,0:T(8,128)(2,1)S(1)}, u32[]{:S(2)}, u32[]{:S(2)}) collective-permute-start(bf16[256,256]{1,0:T(8,128)(2,1)S(1)} %convert_element_type.3), channel_id=1, source_target_pairs={{0,4},{1,5},{2,6},{3,7},{4,0},{5,1},{6,2},{7,3},{8,12},{9,13},{10,... | collective-permute-start | bytes 393224 | tf_op jit(solution)/shard_map/ppermute | solution.py:13
  5.1 6.3 %collective-permute-done = bf16[256,256]{1,0:T(8,128)(2,1)S(1)} collective-permute-done((bf16[256,256]{1,0:T(8,128)(2,1)S(1)}, bf16[256,256]{1,0:T(8,128)(2,1)S(1)}, u32[]{:S(2)}, u32[]{:S(2)}) %collective-permute-start) | collective-permute-done | bytes 131104 | tf_op jit(solution)/shard_map/ppermute | solution.py:13
  11.4 0.1 broadcast_in_dim.50
  11.5 0.0 copy-start.2
  11.6 30.5 %all_to_all.5 = bf16[8,512,256]{2,1,0:T(8,128)(2,1)S(1)} all-to-all(bf16[8,512,256]{2,1,0:T(8,128)(2,1)S(1)} %broadcast_in_dim.50), channel_id=1, replica_groups=mesh['rh'=2,'core'=2,'chh'=2,'chl'=2,'cl'=2] {'rh','chl','cl'}, dimensions={0} | all-to-all | bytes 4194304 | tf_op jit(solution)/shard_map/all_to_all | solution.py:22
  42.0 0.0 collective-permute-start.1
  42.7 0.0 copy-done.2
  42.7 0.1 iota_add_fusion
  42.8 0.1 add.219
  42.9 0.1 fusion.9
  43.0 0.1 broadcast_bitcast_fusion
  43.1 2.4 %gather_fusion.1 = bf16[20,256,256]{2,1,0:T(8,128)(2,1)} fusion(bf16[16,256,256]{2,1,0:T(8,128)(2,1)S(1)} %bitcast.35, s32[1024]{0:T(1024)S(1)} %pad_clamp_fusion), kind=kCustom, calls=%fused_computation.1 | custom fusion | bytes 5242960 | tf_op jit(solution)/shard_map/gather | solution.py:56
  45.5 0.7 %convolution_bitcast_fusion.1 = f32[256,256]{1,0:T(8,128)S(1)} fusion(bf16[8,512,256]{2,1,0:T(8,128)(2,1)S(1)} %all_to_all.5), kind=kOutput, calls=%fused_computation.8 | convolution fusion | flops 536870912 | bytes 2359296 | tf_op jit(solution)/shard_map/dot_general | solution.py:45
  46.2 0.1 collective-permute-done.1
  46.3 2.3 %gather_fusion = bf16[20,256,256]{2,1,0:T(8,128)(2,1)S(1)} fusion(bf16[16,256,256]{2,1,0:T(8,128)(2,1)} %bitcast.2, s32[1024]{0:T(1024)S(1)} %pad_clamp_fusion), kind=kCustom, calls=%fused_computation | custom fusion | bytes 5242960 | tf_op jit(solution)/shard_map/gather | solution.py:57
  48.6 0.0 copy-start.1
  48.7 0.0 copy-start
  48.7 3.1 %convolution_add_fusion = f32[256,256]{1,0:T(8,128)S(1)} fusion(f32[256,256]{1,0:T(8,128)S(1)} %convolution_bitcast_fusion.1, bf16[4096,256]{1,0:T(8,128)(2,1)} %collective-permute-done.1), kind=kOutput, calls=%fused_computation.7 | convolution fusion | flops 536936448 | bytes 2621440 | tf_op jit(solution)/shard_map/dot_general | solution.py:46
  51.8 0.0 copy-done.1
  51.8 1.0 %fusion.24 = f32[256,1024]{1,0:T(8,128)S(1)} fusion(f32[256,256]{1,0:T(8,128)S(1)} %convolution_add_fusion, f32[256,1024]{1,0:T(8,128)S(1)} %copy-done.1), kind=kOutput, calls=%fused_computation.71 | convolution fusion | flops 805306368 | bytes 2359296 | tf_op jit(solution)/shard_map/dot_general | solution.py:67
  52.8 0.0 copy-done
  52.8 1.1 %fusion = bf16[5,1024,256]{2,1,0:T(8,128)(2,1)S(1)} fusion(pred[5]{0:T(512)(128)(4,1)S(1)} %iota_compare_fusion, pred[5,1024]{1,0:T(8,128)(4,1)S(1)} %bitcast.38, bf16[5,1024,256]{2,1,0:T(8,128)(2,1)S(1)} %bitcast.36, bf16[5,1024,256]{2,1,0:T(8,128)(2,1)S(1)} %bitcast.37), kind=kLoop, calls=%fused_computation.3 | loop fusion | flops 2621440 | bytes 7869445 | tf_op jit(solution)/shard_map/jit(_where)/select_n | solution.py:60
  53.9 7.9 %fusion.2 = f32[256,1024]{1,0:T(8,128)} fusion(f32[256,1024]{1,0:T(8,128)S(1)} %fusion.24, f32[256,1024]{1,0:T(8,128)S(1)} %copy-done.1, bf16[5,1024,256]{2,1,0:T(8,128)(2,1)S(1)} %fusion, bf16[5,1024,1024]{2,1,0:T(8,128)(2,1)} %param.5), kind=kOutput, calls=%fused_computation.6 | convolution fusion | flops 2684878848 | bytes 16252928 | tf_op jit(solution)/shard_map/dot_general | solution.py:61
  (6 shorter events, 0.1 us)
Async XLA Ops:
  1.0 10.4 %collective-permute-start = (bf16[256,256]{1,0:T(8,128)(2,1)S(1)}, bf16[256,256]{1,0:T(8,128)(2,1)S(1)}, u32[]{:S(2)}, u32[]{:S(2)}) collective-permute-start(bf16[256,256]{1,0:T(8,128)(2,1)S(1)} %convert_element_type.3), channel_id=1, source_target_pairs={{0,4},{1,5},{2,6},{3,7},{4,0},{5,1},{6,2},{7,3},{8,12},{9,13},{10,... | collective-permute-start | bytes 393224 | tf_op jit(solution)/shard_map/ppermute | solution.py:13
  11.5 31.2 %copy-start.2 = (s32[5]{0:T(128)S(1)}, s32[5]{0:T(128)}, u32[]{:S(2)}) copy-start(s32[5]{0:T(128)} %param.6) | copy-start | bytes 64
  42.0 4.3 %collective-permute-start.1 = (bf16[4096,256]{1,0:T(8,128)(2,1)S(1)}, bf16[4096,256]{1,0:T(8,128)(2,1)}, u32[]{:S(2)}, u32[]{:S(2)}) collective-permute-start(bf16[4096,256]{1,0:T(8,128)(2,1)S(1)} %bitcast.34), channel_id=1, source_target_pairs={{0,8},{1,9},{2,10},{3,11},{4,12},{5,13},{6,14},{7,15},{8,0},{9,1},... | collective-permute-start | bytes 6291464 | tf_op jit(solution)/shard_map/ppermute | solution.py:13
  48.6 3.1 %copy-start.1 = (f32[256,1024]{1,0:T(8,128)S(1)}, f32[256,1024]{1,0:T(8,128)}, u32[]{:S(2)}) copy-start(f32[256,1024]{1,0:T(8,128)} %param.9) | copy-start | bytes 3145732
  48.7 4.2 %copy-start = (bf16[20,256,256]{2,1,0:T(8,128)(2,1)S(1)}, bf16[20,256,256]{2,1,0:T(8,128)(2,1)}, u32[]{:S(2)}) copy-start(bf16[20,256,256]{2,1,0:T(8,128)(2,1)} %gather_fusion.1) | copy-start | bytes 7864324

commit v14 on v9

--- a/solution.py
+++ b/solution.py
@@ -42,8 +42,7 @@
     col_masks = [4 << b for b in range(n_col.bit_length() - 3)][::-1]
     w_half = w_rows.astype(jnp.bfloat16)
     mine, theirs = gather_rows(w_half, n, n_col, col_masks)
-    gram = lax.dot_general(mine, mine, contract_rows, preferred_element_type=jnp.float32)
-    gram = gram + swap(gram, n_col, n)
+    own_gram = lax.dot_general(mine, mine, contract_rows, preferred_element_type=jnp.float32)
     me = lax.axis_index(SUB)
     per_block = tile // share
     blocks_total = n // per_block
@@ -57,6 +56,8 @@
     picked = jnp.where((where >= half)[:, None, None], far, near).reshape(slots, tile, rank_size)
     live = jnp.arange(slots, dtype=jnp.int32) < tile_count[0]
     picked = jnp.where(live[:, None, None], picked, jnp.zeros_like(picked))
+    own_gram, picked = lax.optimization_barrier((own_gram, picked))
+    gram = own_gram + swap(own_gram, n_col, n)
     numerator = lax.dot_general(
         picked.reshape(slots * tile, rank_size),
         tiles.reshape(slots * tile, tiles.shape[2]),

time: 65.7 us -> 61.8 us (0.941)
  matrix products: 11.6 us -> 8.38 us
    dot_general x1, matrix products: 7.87 us -> 5.61 us  [shards(): lax.dot_general(picked.reshape(slots * tile, rank_size), tiles.reshape(sl...]
    dot_general x1, matrix products: 2.95 us -> 2.03 us  [shards(): jnp.dot(gram, h_cols, precision=lax.Precision.HIGHEST, preferred_element_...]
  transfers between devices with their start and end apart: 3 -> 3, of which waited for: 2 -> 2; matrix products, arithmetic and copies ran while one was open for 10% -> 15% of each run, Pallas kernels for 0% -> 0%
where the time goes in v14:
time: 61.8 us; the launch traced here: 61.6 us
  blocking collectives  30.5 us (49%)
  matrix products  8.38 us (14%)
  local copies, waits for them, and re-layouts  7.36 us (12%)
  waiting for transfers between devices  6.56 us (11%)
  starting transfers between devices  4.44 us (7%)
  other arithmetic  3.56 us (6%)
  between operations  0.76 us (1%)
    all_to_all x1, blocking collectives, gather_rows(): lax.all_to_all(spread, GROUP, 0, 0, tiled=False).reshape(-1, buf.shape[1])  30.5 us
    ppermute x3, waiting for transfers between devices, swap(): return lax.ppermute(value, SUB, [(i, i ^ mask) for i in range(n)])  6.56 us
    dot_general x1, matrix products, shards(): lax.dot_general(picked.reshape(slots * tile, rank_size), tiles.reshape(sl...  5.61 us
    ppermute x3, starting transfers between devices, swap(): return lax.ppermute(value, SUB, [(i, i ^ mask) for i in range(n)])  4.44 us
    gather x1, local copies, waits for them, and re-layouts, shards(): far = jnp.take(theirs.reshape(half, share, rank_size), where % half, axis=0)  4.12 us
    gather x1, local copies, waits for them, and re-layouts, shards(): near = jnp.take(mine.reshape(half, share, rank_size), where % half, axis=0)  2.39 us
    select_n x1, other arithmetic, shards(): jnp.where((where >= half)[:, None, None], far, near)  2.21 us
    dot_general x1, matrix products, shards(): jnp.dot(gram, h_cols, precision=lax.Precision.HIGHEST, preferred_element_...  2.03 us
  transfers between devices with their start and end apart: 3, of which 2 were waited for; matrix products, arithmetic and copies ran while one was open for 15% of the time, Pallas kernels for 0%

profile of v14, /device:TPU:0, one launch (start us, length us, event | category | flops | bytes accessed | tf_op | source)
XLA Modules:
  0.0 61.6 jit_solution(14236742694769263331)
XLA Ops:
  0.0 1.0 %convert_element_type.3 = bf16[256,256]{1,0:T(8,128)(2,1)S(1)} convert(f32[256,256]{1,0:T(8,128)} %param.10) | non-fusion elementwise | flops 65536 | bytes 393216 | tf_op jit(solution)/shard_map/convert_element_type | solution.py:43
  1.0 4.1 %collective-permute-start = (bf16[256,256]{1,0:T(8,128)(2,1)S(1)}, bf16[256,256]{1,0:T(8,128)(2,1)S(1)}, u32[]{:S(2)}, u32[]{:S(2)}) collective-permute-start(bf16[256,256]{1,0:T(8,128)(2,1)S(1)} %convert_element_type.3), channel_id=1, source_target_pairs={{0,4},{1,5},{2,6},{3,7},{4,0},{5,1},{6,2},{7,3},{8,12},{9,13},{10,... | collective-permute-start | bytes 393224 | tf_op jit(solution)/shard_map/ppermute | solution.py:13
  5.1 6.3 %collective-permute-done = bf16[256,256]{1,0:T(8,128)(2,1)S(1)} collective-permute-done((bf16[256,256]{1,0:T(8,128)(2,1)S(1)}, bf16[256,256]{1,0:T(8,128)(2,1)S(1)}, u32[]{:S(2)}, u32[]{:S(2)}) %collective-permute-start) | collective-permute-done | bytes 131104 | tf_op jit(solution)/shard_map/ppermute | solution.py:13
  11.4 0.1 broadcast_in_dim.46
  11.5 0.0 copy-start.2
  11.6 30.5 %all_to_all.5 = bf16[8,512,256]{2,1,0:T(8,128)(2,1)S(1)} all-to-all(bf16[8,512,256]{2,1,0:T(8,128)(2,1)S(1)} %broadcast_in_dim.46), channel_id=1, replica_groups=mesh['rh'=2,'core'=2,'chh'=2,'chl'=2,'cl'=2] {'rh','chl','cl'}, dimensions={0} | all-to-all | bytes 4194304 | tf_op jit(solution)/shard_map/all_to_all | solution.py:22
  42.0 0.0 collective-permute-start.1
  42.0 0.0 copy-done.2
  42.1 0.1 iota_add_fusion
  42.1 0.1 add.120
  42.9 2.4 %gather_fusion.1 = bf16[20,256,256]{2,1,0:T(8,128)(2,1)} fusion(bf16[16,256,256]{2,1,0:T(8,128)(2,1)S(1)} %bitcast.20, s32[1024]{0:T(1024)S(1)} %pad_clamp_fusion), kind=kCustom, calls=%fused_computation.1.clone | custom fusion | bytes 5242960 | tf_op jit(solution)/shard_map/jit(_take)/gather | solution.py:54
  45.3 0.7 %convolution_bitcast_fusion.1 = f32[256,256]{1,0:T(8,128)S(1)} fusion(bf16[8,512,256]{2,1,0:T(8,128)(2,1)S(1)} %all_to_all.5), kind=kOutput, calls=%fused_computation.7 | convolution fusion | flops 536870912 | bytes 2359296 | tf_op jit(solution)/shard_map/dot_general | solution.py:45
  46.1 0.3 collective-permute-done.1
  46.3 0.0 copy-start
  46.3 4.1 %gather_fusion = bf16[20,256,256]{2,1,0:T(8,128)(2,1)} fusion(bf16[16,256,256]{2,1,0:T(8,128)(2,1)} %bitcast.3, s32[1024]{0:T(1024)S(1)} %pad_clamp_fusion), kind=kCustom, calls=%fused_computation.clone | custom fusion | bytes 5242960 | tf_op jit(solution)/shard_map/jit(_take)/gather | solution.py:55
  50.4 0.0 copy-done
  50.5 2.2 %select_select_fusion = bf16[20,256,256]{2,1,0:T(8,128)(2,1)S(1)} fusion(bf16[20,256,256]{2,1,0:T(8,128)(2,1)S(1)} %copy-done, bf16[20,256,256]{2,1,0:T(8,128)(2,1)} %gather_fusion, pred[20]{0:T(512)(128)(4,1)S(1)} %get-tuple-element.12, pred[20]{0:T(512)(128)(4,1)S(1)} %get-tuple-element.10), kind=kLoop, calls=%fused_computation.3 | loop fusion | flops 3932160 | bytes 7864360 | tf_op jit(solution)/shard_map/jit(_where)/select_n | solution.py:56
  52.7 0.0 copy-start.1
  52.7 0.2 bitcast_select_fusion
  52.9 0.3 collective-permute-start.2
  53.3 0.6 %copy-done.1 = f32[256,1024]{1,0:T(8,128)S(1)} copy-done((f32[256,1024]{1,0:T(8,128)S(1)}, f32[256,1024]{1,0:T(8,128)}, u32[]{:S(2)}) %copy-start.1) | copy-done | bytes 1048600
  53.9 5.6 %fusion = f32[256,1024]{1,0:T(8,128)S(1)} fusion(f32[256,1024]{1,0:T(8,128)S(1)} %copy-done.1, bf16[5,1024,256]{2,1,0:T(8,128)(2,1)S(1)} %bitcast_select_fusion, bf16[5,1024,1024]{2,1,0:T(8,128)(2,1)} %param.7), kind=kOutput, calls=%fused_computation.5 | convolution fusion | flops 2684616704 | bytes 15204352 | tf_op jit(solution)/shard_map/dot_general | solution.py:61
  59.5 0.0 collective-permute-done.2
  59.5 2.0 %convolution_divide_fusion = f32[256,1024]{1,0:T(8,128)} fusion(f32[256,1024]{1,0:T(8,128)S(1)} %fusion, f32[256,1024]{1,0:T(8,128)S(1)} %copy-done.1, f32[256,256]{1,0:T(8,128)S(1)} %convolution_bitcast_fusion.1, f32[256,256]{1,0:T(8,128)S(1)} %collective-permute-done.2), kind=kOutput, calls=%fused_computation.6 | convolution fusion | flops 805634048 | bytes 3670016 | tf_op jit(solution)/shard_map/dot_general | solution.py:67
  (6 shorter events, 0.1 us)
Async XLA Ops:
  1.0 10.4 %collective-permute-start = (bf16[256,256]{1,0:T(8,128)(2,1)S(1)}, bf16[256,256]{1,0:T(8,128)(2,1)S(1)}, u32[]{:S(2)}, u32[]{:S(2)}) collective-permute-start(bf16[256,256]{1,0:T(8,128)(2,1)S(1)} %convert_element_type.3), channel_id=1, source_target_pairs={{0,4},{1,5},{2,6},{3,7},{4,0},{5,1},{6,2},{7,3},{8,12},{9,13},{10,... | collective-permute-start | bytes 393224 | tf_op jit(solution)/shard_map/ppermute | solution.py:13
  11.5 30.5 %copy-start.2 = (s32[5]{0:T(128)S(1)}, s32[5]{0:T(128)}, u32[]{:S(2)}) copy-start(s32[5]{0:T(128)} %param.8) | copy-start | bytes 64
  42.0 4.3 %collective-permute-start.1 = (bf16[4096,256]{1,0:T(8,128)(2,1)S(1)}, bf16[4096,256]{1,0:T(8,128)(2,1)}, u32[]{:S(2)}, u32[]{:S(2)}) collective-permute-start(bf16[4096,256]{1,0:T(8,128)(2,1)S(1)} %bitcast.19), channel_id=1, source_target_pairs={{0,8},{1,9},{2,10},{3,11},{4,12},{5,13},{6,14},{7,15},{8,0},{9,1},... | collective-permute-start | bytes 6291464 | tf_op jit(solution)/shard_map/ppermute | solution.py:13
  46.3 4.1 %copy-start = (bf16[20,256,256]{2,1,0:T(8,128)(2,1)S(1)}, bf16[20,256,256]{2,1,0:T(8,128)(2,1)}, u32[]{:S(2)}) copy-start(bf16[20,256,256]{2,1,0:T(8,128)(2,1)} %gather_fusion.1) | copy-start | bytes 7864324
  52.7 1.2 %copy-start.1 = (f32[256,1024]{1,0:T(8,128)S(1)}, f32[256,1024]{1,0:T(8,128)}, u32[]{:S(2)}) copy-start(f32[256,1024]{1,0:T(8,128)} %param.11) | copy-start | bytes 3145732
  52.9 6.6 %collective-permute-start.2 = (f32[256,256]{1,0:T(8,128)S(1)}, f32[256,256]{1,0:T(8,128)S(1)}, u32[]{:S(2)}, u32[]{:S(2)}) collective-permute-start(f32[256,256]{1,0:T(8,128)S(1)} %convolution_bitcast_fusion.1), channel_id=1, source_target_pairs={{0,8},{1,9},{2,10},{3,11},{4,12},{5,13},{6,14},{7,15},{8,0},{9,1},... | collective-permute-start | bytes 786440 | tf_op jit(solution)/shard_map/ppermute | solution.py:13

commit v15 on v14

--- a/solution.py
+++ b/solution.py
@@ -53,11 +53,12 @@
     where = where.reshape(-1)
     near = jnp.take(mine.reshape(half, share, rank_size), where % half, axis=0)
     far = jnp.take(theirs.reshape(half, share, rank_size), where % half, axis=0)
+    own_gram, far = lax.optimization_barrier((own_gram, far))
+    gram = own_gram + swap(own_gram, n_col, n)
     picked = jnp.where((where >= half)[:, None, None], far, near).reshape(slots, tile, rank_size)
     live = jnp.arange(slots, dtype=jnp.int32) < tile_count[0]
     picked = jnp.where(live[:, None, None], picked, jnp.zeros_like(picked))
-    own_gram, picked = lax.optimization_barrier((own_gram, picked))
-    gram = own_gram + swap(own_gram, n_col, n)
+    gram, picked = lax.optimization_barrier((gram, picked))
     numerator = lax.dot_general(
         picked.reshape(slots * tile, rank_size),
         tiles.reshape(slots * tile, tiles.shape[2]),

time: 61.8 us -> 58 us (0.939)
  matrix products: 8.38 us -> 5.63 us
  other arithmetic: 3.56 us -> 2.06 us
    unnamed x6 -> x12, local copies, waits for them, and re-layouts: 0.64 us -> 2.92 us
    select_n x1, other arithmetic: 2.21 us -> 0.36 us  [shards(): jnp.where((where >= half)[:, None, None], far, near)]
    gather x1, local copies, waits for them, and re-layouts: 4.12 us -> 2.3 us  [shards(): far = jnp.take(theirs.reshape(half, share, rank_size), where % half, axis=0)]
    dot_general x1, matrix products: 5.61 us -> 3.86 us  [shards(): lax.dot_general(picked.reshape(slots * tile, rank_size), tiles.reshape(sl...]
    dot_general x1, matrix products: 2.03 us -> 1.03 us  [shards(): jnp.dot(gram, h_cols, precision=lax.Precision.HIGHEST, preferred_element_...]
  transfers between devices with their start and end apart: 3 -> 3, of which waited for: 2 -> 2; matrix products, arithmetic and copies ran while one was open for 15% -> 7% of each run, Pallas kernels for 0% -> 0%
where the time goes in v15:
time: 58 us; the launch traced here: 57.8 us
  blocking collectives  30.5 us (53%)
  local copies, waits for them, and re-layouts  7.82 us (13%)
  waiting for transfers between devices  6.58 us (11%)
  matrix products  5.63 us (10%)
  starting transfers between devices  4.42 us (8%)
  other arithmetic  2.06 us (4%)
  between operations  0.81 us (1%)
    all_to_all x1, blocking collectives, gather_rows(): lax.all_to_all(spread, GROUP, 0, 0, tiled=False).reshape(-1, buf.shape[1])  30.5 us
    ppermute x3, waiting for transfers between devices, swap(): return lax.ppermute(value, SUB, [(i, i ^ mask) for i in range(n)])  6.58 us
    ppermute x3, starting transfers between devices, swap(): return lax.ppermute(value, SUB, [(i, i ^ mask) for i in range(n)])  4.42 us
    dot_general x1, matrix products, shards(): lax.dot_general(picked.reshape(slots * tile, rank_size), tiles.reshape(sl...  3.86 us
    unnamed x12, local copies, waits for them, and re-layouts  2.92 us
    gather x1, local copies, waits for them, and re-layouts, shards(): near = jnp.take(mine.reshape(half, share, rank_size), where % half, axis=0)  2.38 us
    gather x1, local copies, waits for them, and re-layouts, shards(): far = jnp.take(theirs.reshape(half, share, rank_size), where % half, axis=0)  2.3 us
  transfers between devices with their start and end apart: 3, of which 2 were waited for; matrix products, arithmetic and copies ran while one was open for 7% of the time, Pallas kernels for 0%

profile of v15, /device:TPU:0, one launch (start us, length us, event | category | flops | bytes accessed | tf_op | source)
XLA Modules:
  0.0 57.8 jit_solution(17008637374645857778)
XLA Ops:
  0.0 1.0 %convert_element_type.3 = bf16[256,256]{1,0:T(8,128)(2,1)S(1)} convert(f32[256,256]{1,0:T(8,128)} %param.10) | non-fusion elementwise | flops 65536 | bytes 393216 | tf_op jit(solution)/shard_map/convert_element_type | solution.py:43
  1.0 4.1 %collective-permute-start = (bf16[256,256]{1,0:T(8,128)(2,1)S(1)}, bf16[256,256]{1,0:T(8,128)(2,1)S(1)}, u32[]{:S(2)}, u32[]{:S(2)}) collective-permute-start(bf16[256,256]{1,0:T(8,128)(2,1)S(1)} %convert_element_type.3), channel_id=1, source_target_pairs={{0,4},{1,5},{2,6},{3,7},{4,0},{5,1},{6,2},{7,3},{8,12},{9,13},{10,... | collective-permute-start | bytes 393224 | tf_op jit(solution)/shard_map/ppermute | solution.py:13
  5.1 6.3 %collective-permute-done = bf16[256,256]{1,0:T(8,128)(2,1)S(1)} collective-permute-done((bf16[256,256]{1,0:T(8,128)(2,1)S(1)}, bf16[256,256]{1,0:T(8,128)(2,1)S(1)}, u32[]{:S(2)}, u32[]{:S(2)}) %collective-permute-start) | collective-permute-done | bytes 131104 | tf_op jit(solution)/shard_map/ppermute | solution.py:13
  11.4 0.1 broadcast_in_dim.46
  11.5 0.0 copy-start.2
  11.6 30.5 %all_to_all.5 = bf16[8,512,256]{2,1,0:T(8,128)(2,1)S(1)} all-to-all(bf16[8,512,256]{2,1,0:T(8,128)(2,1)S(1)} %broadcast_in_dim.46), channel_id=1, replica_groups=mesh['rh'=2,'core'=2,'chh'=2,'chl'=2,'cl'=2] {'rh','chl','cl'}, dimensions={0} | all-to-all | bytes 4194304 | tf_op jit(solution)/shard_map/all_to_all | solution.py:22
  42.0 0.0 collective-permute-start.1
  42.7 0.0 copy-done.2
  42.7 0.1 iota_add_fusion
  42.8 0.1 add.120
  42.9 2.4 %gather_fusion.1 = bf16[20,256,256]{2,1,0:T(8,128)(2,1)} fusion(bf16[16,256,256]{2,1,0:T(8,128)(2,1)S(1)} %bitcast.23, s32[1024]{0:T(1024)S(1)} %pad_clamp_fusion), kind=kCustom, calls=%fused_computation.1.clone | custom fusion | bytes 5242960 | tf_op jit(solution)/shard_map/jit(_take)/gather | solution.py:54
  45.3 0.7 %convolution_bitcast_fusion.1 = f32[256,256]{1,0:T(8,128)S(1)} fusion(bf16[8,512,256]{2,1,0:T(8,128)(2,1)S(1)} %all_to_all.5), kind=kOutput, calls=%fused_computation.8 | convolution fusion | flops 536870912 | bytes 2359296 | tf_op jit(solution)/shard_map/dot_general | solution.py:45
  46.1 0.3 collective-permute-done.1
  46.3 2.3 %gather_fusion = bf16[20,256,256]{2,1,0:T(8,128)(2,1)S(1)} fusion(bf16[16,256,256]{2,1,0:T(8,128)(2,1)} %bitcast.2, s32[1024]{0:T(1024)S(1)} %pad_clamp_fusion), kind=kCustom, calls=%fused_computation.clone | custom fusion | bytes 5242960 | tf_op jit(solution)/shard_map/jit(_take)/gather | solution.py:55
  48.6 0.0 copy-start
  48.7 0.0 slice-start
  48.7 0.3 broadcast_select_fusion
  49.0 0.3 collective-permute-start.2
  49.3 1.1 %copy-done = bf16[20,256,256]{2,1,0:T(8,128)(2,1)S(1)} copy-done((bf16[20,256,256]{2,1,0:T(8,128)(2,1)S(1)}, bf16[20,256,256]{2,1,0:T(8,128)(2,1)}, u32[]{:S(2)}) %copy-start) | copy-done | bytes 2621464
  50.4 0.0 slice-start.1
  50.4 0.4 select_select_fusion
  50.7 0.0 copy-start.1
  50.8 0.0 slice-start.2
  50.8 0.2 bitcast_select_fusion
  51.0 0.0 collective-permute-done.2
  51.1 1.3 %copy-done.1 = f32[256,1024]{1,0:T(8,128)S(1)} copy-done((f32[256,1024]{1,0:T(8,128)S(1)}, f32[256,1024]{1,0:T(8,128)}, u32[]{:S(2)}) %copy-start.1) | copy-done | bytes 1048600
  52.4 1.0 %fusion.8 = f32[256,1024]{1,0:T(8,128)S(1)} fusion(f32[256,256]{1,0:T(8,128)S(1)} %add.133, f32[256,1024]{1,0:T(8,128)S(1)} %copy-done.1), kind=kOutput, calls=%fused_computation.40 | convolution fusion | flops 805306368 | bytes 2359296 | tf_op jit(solution)/shard_map/dot_general | solution.py:68
  53.4 0.0 slice-done
  53.4 0.0 slice-done.1
  53.4 0.5 slice-done.2
  53.9 3.9 %fusion.1 = f32[256,1024]{1,0:T(8,128)} fusion(f32[256,1024]{1,0:T(8,128)S(1)} %fusion.8, f32[256,1024]{1,0:T(8,128)S(1)} %copy-done.1, bf16[5,1024,256]{2,1,0:T(8,128)(2,1)S(1)} %bitcast_select_fusion, bf16[5,1024,1024]{2,1,0:T(8,128)(2,1)S(1)} %bitcast.26), kind=kOutput, calls=%fused_computation.7 | convolution fusion | flops 2684878848 | bytes 16252928 | tf_op jit(solution)/shard_map/dot_general | solution.py:62
  (8 shorter events, 0.1 us)
Async XLA Ops:
  1.0 10.4 %collective-permute-start = (bf16[256,256]{1,0:T(8,128)(2,1)S(1)}, bf16[256,256]{1,0:T(8,128)(2,1)S(1)}, u32[]{:S(2)}, u32[]{:S(2)}) collective-permute-start(bf16[256,256]{1,0:T(8,128)(2,1)S(1)} %convert_element_type.3), channel_id=1, source_target_pairs={{0,4},{1,5},{2,6},{3,7},{4,0},{5,1},{6,2},{7,3},{8,12},{9,13},{10,... | collective-permute-start | bytes 393224 | tf_op jit(solution)/shard_map/ppermute | solution.py:13
  11.5 31.2 %copy-start.2 = (s32[5]{0:T(128)S(1)}, s32[5]{0:T(128)}, u32[]{:S(2)}) copy-start(s32[5]{0:T(128)} %param.8) | copy-start | bytes 64
  42.0 4.3 %collective-permute-start.1 = (bf16[4096,256]{1,0:T(8,128)(2,1)S(1)}, bf16[4096,256]{1,0:T(8,128)(2,1)}, u32[]{:S(2)}, u32[]{:S(2)}) collective-permute-start(bf16[4096,256]{1,0:T(8,128)(2,1)S(1)} %bitcast.22), channel_id=1, source_target_pairs={{0,8},{1,9},{2,10},{3,11},{4,12},{5,13},{6,14},{7,15},{8,0},{9,1},... | collective-permute-start | bytes 6291464 | tf_op jit(solution)/shard_map/ppermute | solution.py:13
  48.6 1.7 %copy-start = (bf16[20,256,256]{2,1,0:T(8,128)(2,1)S(1)}, bf16[20,256,256]{2,1,0:T(8,128)(2,1)}, u32[]{:S(2)}) copy-start(bf16[20,256,256]{2,1,0:T(8,128)(2,1)} %gather_fusion.1) | copy-start | bytes 7864324
  48.7 4.8 %slice-start = ((s8[10485760]{0:T(1024)(128)(4,1)}), s8[4194304]{0:T(1024)(128)(4,1)S(1)}, s32[]{:S(2)}) async-start(s8[10485760]{0:T(1024)(128)(4,1)} %bitcast.25), calls=%async_computation.1 | async-start | bytes 8388608
  49.0 2.0 %collective-permute-start.2 = (f32[256,256]{1,0:T(8,128)S(1)}, f32[256,256]{1,0:T(8,128)S(1)}, u32[]{:S(2)}, u32[]{:S(2)}) collective-permute-start(f32[256,256]{1,0:T(8,128)S(1)} %convolution_bitcast_fusion.1), channel_id=1, source_target_pairs={{0,8},{1,9},{2,10},{3,11},{4,12},{5,13},{6,14},{7,15},{8,0},{9,1},... | collective-permute-start | bytes 786440 | tf_op jit(solution)/shard_map/ppermute | solution.py:13
  50.4 3.0 %slice-start.1 = ((s8[10485760]{0:T(1024)(128)(4,1)}), s8[4194304]{0:T(1024)(128)(4,1)S(1)}, s32[]{:S(2)}) async-start(s8[10485760]{0:T(1024)(128)(4,1)} %bitcast.25), calls=%async_computation.2 | async-start | bytes 8388608
  50.7 1.6 %copy-start.1 = (f32[256,1024]{1,0:T(8,128)S(1)}, f32[256,1024]{1,0:T(8,128)}, u32[]{:S(2)}) copy-start(f32[256,1024]{1,0:T(8,128)} %param.11) | copy-start | bytes 3145732
  50.8 3.2 %slice-start.2 = ((s8[10485760]{0:T(1024)(128)(4,1)}), s8[2097152]{0:T(1024)(128)(4,1)S(1)}, s32[]{:S(2)}) async-start(s8[10485760]{0:T(1024)(128)(4,1)} %bitcast.25), calls=%async_computation.3 | async-start | bytes 4194304
